TPU v7x, 512 devices: a whole 4x4x16 slice. The times are simulated.
512 devices in a mesh: space: 64 (over z_lo, x, core), ky: 8 (over z_hi, y).
Axes of the slice: x: 4, y: 4, z: 16 (z_hi: 2, z_lo: 8; z = z_hi * 8 + z_lo), core: 2. Of those that a mesh axis runs over, the one named last changes fastest.
Arguments:
- distribution: float32 [64, 128, 256, 128], P('space', 'ky'), may hold values from 0 to 2
- region: int32 [64, 256], P('space'), may hold values from 0 to 5, as said below
- region_doping: float32 [6], replicated, may hold values from -1 to 2
- region_relax: float32 [6], replicated, may hold values from 0.2 to 1
- equilibrium: float32 [128, 128], P('ky'), may hold values from 0.3 to 3
- kx_speed: float32 [128], replicated, may hold values from 0.1 to 1
- upwind_sign: int32 [128], replicated, may hold values from -1 to 1, as said below
Outputs:
- advanced: float32 [64, 128, 256, 128], P('space', 'ky')
Inputs may be any that keep to these rules, and one draw needn't show every extreme that they name: region[x, y] = 2 band(y) + m[x, y], with m[x, y] 0 or 1 and band(y) = 0, 1, 2 on three runs of columns, each run at least 32 columns long. `upwind_sign`: exactly 64 entries are 1 and the others -1.
All inputs are finite; a program needn't handle non-finite values.
Results may differ from a plain program's by a relative error of at most 0.0003.
Values sent between devices are 32-bit elements; how exact they have to be, the bound alone decides.
No kernel may reach another device: no remote copies, remote signals or barrier semaphores. Data moves between devices by JAX's collectives and lax.ppermute only.
A program may use at most 64 MiB of HBM per device.

v0:
```python
import math

import jax
import jax.numpy as jnp
from jax import lax
from jax.sharding import PartitionSpec as P

COUPLING = 0.04
POISSON = 0.1
STEP = 0.4
DRIFT_Y = 0.8


def with_halo(block, sides, width):
    for axis, dim in sides:
        count = lax.axis_size(axis)
        forward = [(i, i + 1) for i in range(count - 1)]
        backward = [(target, source) for source, target in forward]
        low = lax.ppermute(
            lax.slice_in_dim(block, block.shape[dim] - width, None, axis=dim), axis, forward
        )
        high = lax.ppermute(lax.slice_in_dim(block, 0, width, axis=dim), axis, backward)
        block = jnp.concatenate([low, block, high], axis=dim)
    return block


def sine_table(length):
    positions = jnp.arange(1, length + 1, dtype=jnp.int32)
    phase_index = positions[:, None] * positions[None, :] % (2 * length + 2)
    return jnp.sqrt(2.0 / (length + 1.0)) * jnp.sin(
        math.pi * phase_index.astype(jnp.float32) / (length + 1.0)
    )


def eigen_values(length):
    positions = jnp.arange(1, length + 1, dtype=jnp.int32).astype(jnp.float32)
    return 4.0 * jnp.sin(0.5 * math.pi * positions / (length + 1.0)) ** 2


def wigner_tables(modes):
    half_count = modes // 2
    shifts = jnp.arange(1, half_count + 1, dtype=jnp.int32)
    wave_index = jnp.arange(modes, dtype=jnp.int32)
    phase_index = shifts[:, None] * wave_index[None, :] % modes
    angles = 2.0 * math.pi / modes * phase_index.astype(jnp.float32)
    forward = jnp.concatenate([jnp.cos(angles), jnp.sin(angles)], axis=0)
    backward = jnp.concatenate([jnp.sin(angles).T, -jnp.cos(angles).T], axis=1)
    return (forward, backward)


def own_differences(potential, modes, first_col, local_cols):
    half_count = modes // 2
    padded = jnp.pad(potential, ((0, 0), (half_count, half_count)))
    window = lax.dynamic_slice_in_dim(padded, first_col, local_cols + 2 * half_count, 1)
    pieces = []
    for offset in range(1, half_count + 1):
        ahead_vals = window[:, half_count + offset : half_count + offset + local_cols]
        behind = window[:, half_count - offset : half_count - offset + local_cols]
        pieces.append(ahead_vals - behind)
    return COUPLING * jnp.stack(pieces, axis=1)


def lookup(region, values_table):
    classes = jnp.arange(values_table.shape[0], dtype=jnp.int32)
    return jnp.sum(jnp.where(region[..., None] == classes, values_table, 0.0), axis=-1)


def shards(distribution, region, region_doping, region_relax, equilibrium, kx_speed, upwind_sign):
    precise = lax.Precision.HIGHEST
    triple = lax.Precision.HIGH
    row_count, ky_local, col_count, kx_count = distribution.shape
    ky_count = ky_local * lax.axis_size("ky")
    grid_rows = row_count * lax.axis_size("space")
    row_start = lax.axis_index("space") * row_count
    partial_value = jnp.sum(distribution, axis=(1, 3)) / (ky_count * kx_count)
    density = lax.psum(partial_value, "ky")
    doping = lookup(region, region_doping)
    relax_rate = lookup(region, region_relax)
    charge = density - doping
    sine_rows = sine_table(grid_rows)
    sine_cols = sine_table(col_count)
    eigen_cols = eigen_values(col_count)
    every_row = lax.all_gather(charge, "space", axis=0, tiled=True)
    along_x = jnp.dot(sine_rows, every_row, precision=precise)
    spectral = jnp.dot(along_x, sine_cols, precision=precise)
    spectral = spectral / (eigen_values(grid_rows)[:, None] + eigen_cols[None, :])
    back_cols = jnp.dot(spectral, sine_cols, precision=precise)
    own_rows = lax.dynamic_slice_in_dim(sine_rows, row_start, row_count, 0)
    potential = POISSON * jnp.dot(own_rows, back_cols, precision=precise)
    spread = lax.all_to_all(distribution, "ky", split_axis=2, concat_axis=1, tiled=True)
    local_cols = spread.shape[2]
    forward, backward = wigner_tables(ky_count)
    weights = own_differences(potential, ky_count, lax.axis_index("ky") * local_cols, local_cols)
    flattened = spread.reshape(row_count, ky_count, local_cols * kx_count)
    coeffs = jnp.einsum("ab,rbm->ram", forward, flattened, precision=triple)
    coeffs = coeffs.reshape(row_count, ky_count, local_cols, kx_count)
    scaled = coeffs * jnp.concatenate([weights, weights], axis=1)[..., None]
    mixed = jnp.einsum(
        "ab,rbm->ram",
        backward,
        scaled.reshape(row_count, ky_count, local_cols * kx_count),
        precision=triple,
    )
    mixed = mixed.reshape(row_count, ky_count, local_cols, kx_count)
    wigner = lax.all_to_all(mixed, "ky", split_axis=1, concat_axis=2, tiled=True)
    positive_kx = upwind_sign > 0
    padded = with_halo(distribution, (("space", 0),), 1)
    from_left = padded[:-2]
    from_right = padded[2:]
    upstream_x = jnp.where(positive_kx[None, None, None, :], from_left, from_right)
    drift_x = -kx_speed[None, None, None, :] * (distribution - upstream_x)
    ky_global = lax.axis_index("ky") * ky_local + jnp.arange(ky_local, dtype=jnp.int32)
    upward = ky_global >= ky_count // 2
    vertical = DRIFT_Y * (ky_global.astype(jnp.float32) + 0.5 - 0.5 * ky_count) / (0.5 * ky_count)
    zero_col = jnp.zeros_like(distribution[:, :, :1])
    from_low = jnp.concatenate([zero_col, distribution[:, :, :-1]], axis=2)
    from_high = jnp.concatenate([distribution[:, :, 1:], zero_col], axis=2)
    upstream_y = jnp.where(upward[None, :, None, None], from_low, from_high)
    drift_y = -jnp.abs(vertical)[None, :, None, None] * (distribution - upstream_y)
    relaxation = relax_rate[:, None, :, None] * (
        density[:, None, :, None] * equilibrium[None, :, None, :] - distribution
    )
    return distribution + STEP * (drift_x + drift_y + wigner + relaxation)


def solution(mesh):
    return jax.shard_map(
        shards,
        mesh=mesh,
        in_specs=(
            P("space", "ky", None, None),
            P("space", None),
            P(),
            P(),
            P("ky", None),
            P(),
            P(),
        ),
        out_specs=P("space", "ky", None, None),
        check_vma=False,
    )
```

profile of v0, /device:TPU:40, one launch (start us, length us, event | category | flops | bytes accessed | tf_op | source)
XLA Modules:
  0.0 378.3 jit_solution(6376607305004779924)
XLA Ops:
  0.0 4.1 %copy.28 = f32[1,16,256,128]{3,1,0,2:T(8,128)} copy(f32[1,16,256,128]{3,2,1,0:T(8,128)} %param.7) | data formatting | bytes 4194304 | tf_op args[0]
  4.1 17.4 %all-to-all-start = ((f32[1,16,256,128]{3,1,0,2:T(8,128)}), f32[1,16,256,128]{3,1,0,2:T(8,128)}, u32[]{:S(2)}, u32[]{:S(2)}) async-start(f32[1,16,256,128]{3,1,0,2:T(8,128)} %copy.28), calls=%async_computation | async-start | bytes 4194304 | tf_op jit(solution)/shard_map/all_to_all | solution.py:90
  21.6 0.2 reduce_sum.29
  21.8 118.1 %psum.7 = f32[1,256]{1,0:T(1,128)S(1)} all-reduce(f32[1,256]{1,0:T(1,128)S(1)} %bitcast.205), channel_id=1, replica_groups=mesh['space'=64,'ky'=8] {'ky'}, use_global_device_ids=true, to_apply=%region_1.0 | all-reduce | flops 256 | bytes 2048 | tf_op jit(solution)/shard_map/psum | solution.py:76
  139.9 0.1 fusion.65
  140.0 105.4 %all-gather = f32[64,1,256]{2,1,0:T(1,128)S(1)} all-gather(f32[1,1,256]{2,1,0:T(1,128)S(1)} %subtract_bitcast_fusion), channel_id=1, replica_groups=mesh['space'=64,'ky'=8] {'space'}, dimensions={0}, use_global_device_ids=true | all-gather | bytes 66560 | tf_op jit(solution)/shard_map/all_gather | solution.py:83
  245.4 0.2 fusion.53
  245.7 0.4 fusion.39
  246.1 1.3 convolution_divide_fusion
  247.4 1.3 fusion.14
  248.7 0.1 fusion.67
  248.9 0.1 fusion.180
  249.1 0.1 fusion.174
  249.3 0.1 fusion.184
  249.5 0.1 fusion.194
  249.7 0.1 fusion.196
  249.9 0.1 fusion.172
  250.1 0.1 fusion.178
  250.4 0.1 fusion.186
  250.6 0.1 fusion.182
  250.8 0.1 fusion.170
  251.0 0.1 fusion.192
  251.1 0.1 copy.90
  251.2 0.1 fusion.176
  251.4 0.1 fusion.188
  251.6 0.1 fusion.168
  251.7 0.1 copy.78
  251.8 0.1 fusion.190
  252.0 0.1 fusion.70
  256.4 0.3 stack.259
  256.9 0.1 copy.94
  257.0 1.9 mul.263
  258.9 2.7 mul.264
  261.6 0.2 fusion.62
  261.9 0.3 fusion.54
  262.2 2.4 copy.29
  264.5 2.2 fusion.1
  266.7 3.2 fusion.35
  269.9 3.1 copy.95
  273.1 6.8 %all-to-all-start.1 = ((f32[1,128,32,128]{3,2,0,1:T(8,128)}), f32[1,128,32,128]{3,2,0,1:T(8,128)}, u32[]{:S(2)}, u32[]{:S(2)}) async-start(f32[1,128,32,128]{3,2,0,1:T(8,128)} %copy.95), calls=%async_computation.1 | async-start | bytes 4194304 | tf_op jit(solution)/shard_map/all_to_all | solution.py:105
  279.9 2.1 collective-permute-start.1
  282.0 2.2 collective-permute-start
  284.3 2.5 fusion.209
  286.8 45.5 %all-to-all-done.1 = f32[1,128,32,128]{3,2,0,1:T(8,128)} async-done(((f32[1,128,32,128]{3,2,0,1:T(8,128)}), f32[1,128,32,128]{3,2,0,1:T(8,128)}, u32[]{:S(2)}, u32[]{:S(2)}) %all-to-all-start.1) | async-done | bytes 2097184 | tf_op jit(solution)/shard_map/all_to_all | solution.py:105
  332.3 2.0 copy.96
  334.3 30.2 %collective-permute-done.1 = f32[1,16,256,128]{3,2,1,0:T(8,128)} collective-permute-done((f32[1,16,256,128]{3,2,1,0:T(8,128)S(1)}, f32[1,16,256,128]{3,2,1,0:T(8,128)}, u32[]{:S(2)}, u32[]{:S(2)}) %collective-permute-start.1) | collective-permute-done | bytes 2097184 | tf_op jit(solution)/shard_map/ppermute | solution.py:22
  364.5 8.3 %collective-permute-done = f32[1,16,256,128]{3,2,1,0:T(8,128)} collective-permute-done((f32[1,16,256,128]{3,2,1,0:T(8,128)S(1)}, f32[1,16,256,128]{3,2,1,0:T(8,128)}, u32[]{:S(2)}, u32[]{:S(2)}) %collective-permute-start) | collective-permute-done | bytes 2097184 | tf_op jit(solution)/shard_map/ppermute | solution.py:19
  372.8 5.5 %fusion.6 = f32[1,16,256,128]{3,2,1,0:T(8,128)} fusion(f32[1,16,256,128]{3,2,1,0:T(8,128)S(1)} %copy-done, f32[1,16,8,32,128]{4,3,2,1,0:T(8,128)S(1)} %copy.96, f32[1,16,255,128]{3,2,1,0:T(8,128)S(1)} %copy-done.3, f32[1,16,255,128]{3,2,1,0:T(8,128)S(1)} %copy-done.2, f32[1,16,256,128]{3,2,1,0:T(8,128)} %collective-permute-done, ...), kind=kLoop, calls=%fused_computation.8 | loop fusion | flops 7340032 | bytes 14674640 | tf_op jit(solution)/shard_map/add | solution.py:123
  (96 shorter events, 5.7 us)
Async XLA Ops:
  4.1 17.4 %copy-start = (f32[1,16,256,128]{3,2,1,0:T(8,128)S(1)}, f32[1,16,256,128]{3,2,1,0:T(8,128)}, u32[]{:S(2)}) copy-start(f32[1,16,256,128]{3,2,1,0:T(8,128)} %param.7) | copy-start | bytes 6291460
  4.1 258.0 %all-to-all-start = ((f32[1,16,256,128]{3,1,0,2:T(8,128)}), f32[1,16,256,128]{3,1,0,2:T(8,128)}, u32[]{:S(2)}, u32[]{:S(2)}) async-start(f32[1,16,256,128]{3,1,0,2:T(8,128)} %copy.28), calls=%async_computation | async-start | bytes 4194304 | tf_op jit(solution)/shard_map/all_to_all | solution.py:90
  21.5 118.3 %copy-start.5 = (s32[1,256]{1,0:T(1,128)S(1)}, s32[1,256]{1,0:T(1,128)}, u32[]{:S(2)}) copy-start(s32[1,256]{1,0:T(1,128)} %param.8) | copy-start | bytes 3076
  21.5 118.3 %copy-start.6 = (f32[6]{0:T(128)S(1)}, f32[6]{0:T(128)}, u32[]{:S(2)}) copy-start(f32[6]{0:T(128)} %param.10) | copy-start | bytes 76
  21.5 118.3 %copy-start.7 = (f32[6]{0:T(128)S(1)}, f32[6]{0:T(128)}, u32[]{:S(2)}) copy-start(f32[6]{0:T(128)} %param.9) | copy-start | bytes 76
  262.1 2.4 copy-start.1
  273.0 11.2 %copy-start.8 = (f32[128]{0:T(128)S(1)}, f32[128]{0:T(128)}, u32[]{:S(2)}) copy-start(f32[128]{0:T(128)} %param.12) | copy-start | bytes 1540
  273.0 11.2 %copy-start.9 = (s32[128]{0:T(128)S(1)}, s32[128]{0:T(128)}, u32[]{:S(2)}) copy-start(s32[128]{0:T(128)} %param.13) | copy-start | bytes 1540
  273.1 59.2 %all-to-all-start.1 = ((f32[1,128,32,128]{3,2,0,1:T(8,128)}), f32[1,128,32,128]{3,2,0,1:T(8,128)}, u32[]{:S(2)}, u32[]{:S(2)}) async-start(f32[1,128,32,128]{3,2,0,1:T(8,128)} %copy.95), calls=%async_computation.1 | async-start | bytes 4194304 | tf_op jit(solution)/shard_map/all_to_all | solution.py:105
  279.9 84.6 %collective-permute-start.1 = (f32[1,16,256,128]{3,2,1,0:T(8,128)S(1)}, f32[1,16,256,128]{3,2,1,0:T(8,128)}, u32[]{:S(2)}, u32[]{:S(2)}) collective-permute-start(f32[1,16,256,128]{3,2,1,0:T(8,128)S(1)} %copy-done), channel_id=1, source_target_pairs={{8,0},{16,8},{24,16},{32,24},{40,32},{48,40},{56,48},{64,56},{72,6... | collective-permute-start | bytes 6291464 | tf_op jit(solution)/shard_map/ppermute | solution.py:22
  282.0 90.8 %collective-permute-start = (f32[1,16,256,128]{3,2,1,0:T(8,128)S(1)}, f32[1,16,256,128]{3,2,1,0:T(8,128)}, u32[]{:S(2)}, u32[]{:S(2)}) collective-permute-start(f32[1,16,256,128]{3,2,1,0:T(8,128)S(1)} %copy-done), channel_id=1, source_target_pairs={{0,8},{8,16},{16,24},{24,32},{32,40},{40,48},{48,56},{56,64},{64,7... | collective-permute-start | bytes 6291464 | tf_op jit(solution)/shard_map/ppermute | solution.py:19
  284.3 88.5 %copy-start.4 = (f32[16,128]{1,0:T(8,128)S(1)}, f32[16,128]{1,0:T(8,128)}, u32[]{:S(2)}) copy-start(f32[16,128]{1,0:T(8,128)} %param.11) | copy-start | bytes 24580
  332.3 40.5 %copy-start.2 = (f32[1,16,255,128]{3,2,1,0:T(8,128)S(1)}, f32[1,16,255,128]{3,2,1,0:T(8,128)}, u32[]{:S(2)}) copy-start(f32[1,16,255,128]{3,2,1,0:T(8,128)} %get-tuple-element.7) | copy-start | bytes 6266884
  332.3 40.5 %copy-start.3 = (f32[1,16,255,128]{3,2,1,0:T(8,128)S(1)}, f32[1,16,255,128]{3,2,1,0:T(8,128)}, u32[]{:S(2)}) copy-start(f32[1,16,255,128]{3,2,1,0:T(8,128)} %get-tuple-element.8) | copy-start | bytes 6266884
where the time goes:
time: 379 us; the launch traced here: 378 us
  blocking collectives  223 us (59%)
  waiting for transfers between devices  84 us (22%)
  starting transfers between devices  28.5 us (8%)
  local copies, waits for them, and re-layouts  24.8 us (7%)
  other arithmetic  8.64 us (2%)
  matrix products  8.58 us (2%)
    psum x1, blocking collectives, shards(): density = lax.psum(partial_value, 'ky')  118 us
    all_gather x1, blocking collectives, shards(): every_row = lax.all_gather(charge, 'space', axis=0, tiled=True)  105 us
    all_to_all x1, waiting for transfers between devices, shards(): lax.all_to_all(mixed, 'ky', split_axis=1, concat_axis=2, tiled=True)  45.5 us
    ppermute x1, waiting for transfers between devices, with_halo(): lax.ppermute(lax.slice_in_dim(block, 0, width, axis=dim), axis, backward)  30.2 us
    all_to_all x1, starting transfers between devices, shards(): lax.all_to_all(distribution, 'ky', split_axis=2, concat_axis=1, tiled=True)  17.4 us
    ppermute x1, waiting for transfers between devices, with_halo(): lax.ppermute(lax.slice_in_dim(block, block.shape[dim] - width, None, axis...  8.26 us
  transfers between devices with their start and end apart: 4, of which 3 were waited for; matrix products, arithmetic and copies ran while one was open for 6% of the time, Pallas kernels for 0%

commit v1 on v0

--- a/solution.py
+++ b/solution.py
@@ -9,19 +9,6 @@
 POISSON = 0.1
 STEP = 0.4
 DRIFT_Y = 0.8
-
-
-def with_halo(block, sides, width):
-    for axis, dim in sides:
-        count = lax.axis_size(axis)
-        forward = [(i, i + 1) for i in range(count - 1)]
-        backward = [(target, source) for source, target in forward]
-        low = lax.ppermute(
-            lax.slice_in_dim(block, block.shape[dim] - width, None, axis=dim), axis, forward
-        )
-        high = lax.ppermute(lax.slice_in_dim(block, 0, width, axis=dim), axis, backward)
-        block = jnp.concatenate([low, block, high], axis=dim)
-    return block
 
 
 def sine_table(length):
@@ -65,28 +52,61 @@
     return jnp.sum(jnp.where(region[..., None] == classes, values_table, 0.0), axis=-1)
 
 
+def xor_pairs(count, bit):
+    return [(i, i ^ bit) for i in range(count)]
+
+
+def sum_over(value, axis):
+    count = lax.axis_size(axis)
+    bit = 1
+    while bit < count:
+        value = value + lax.ppermute(value, axis, xor_pairs(count, bit))
+        bit *= 2
+    return value
+
+
+def gather_rows(value, axis):
+    count = lax.axis_size(axis)
+    index = lax.axis_index(axis)
+    bit, level = 1, 0
+    while bit < count:
+        other = lax.ppermute(value, axis, xor_pairs(count, bit))
+        low = ((index >> level) & 1) == 0
+        value = jnp.where(
+            low, jnp.concatenate([value, other], 0), jnp.concatenate([other, value], 0)
+        )
+        bit *= 2
+        level += 1
+    return value
+
+
 def shards(distribution, region, region_doping, region_relax, equilibrium, kx_speed, upwind_sign):
     precise = lax.Precision.HIGHEST
     triple = lax.Precision.HIGH
     row_count, ky_local, col_count, kx_count = distribution.shape
     ky_count = ky_local * lax.axis_size("ky")
-    grid_rows = row_count * lax.axis_size("space")
-    row_start = lax.axis_index("space") * row_count
+    space_count = lax.axis_size("space")
+    grid_rows = row_count * space_count
+    space_index = lax.axis_index("space")
+    row_start = space_index * row_count
+
     partial_value = jnp.sum(distribution, axis=(1, 3)) / (ky_count * kx_count)
-    density = lax.psum(partial_value, "ky")
+    density = sum_over(partial_value, "ky")
     doping = lookup(region, region_doping)
     relax_rate = lookup(region, region_relax)
     charge = density - doping
+    every_row = gather_rows(charge, "space")
+
     sine_rows = sine_table(grid_rows)
     sine_cols = sine_table(col_count)
     eigen_cols = eigen_values(col_count)
-    every_row = lax.all_gather(charge, "space", axis=0, tiled=True)
     along_x = jnp.dot(sine_rows, every_row, precision=precise)
     spectral = jnp.dot(along_x, sine_cols, precision=precise)
     spectral = spectral / (eigen_values(grid_rows)[:, None] + eigen_cols[None, :])
     back_cols = jnp.dot(spectral, sine_cols, precision=precise)
     own_rows = lax.dynamic_slice_in_dim(sine_rows, row_start, row_count, 0)
     potential = POISSON * jnp.dot(own_rows, back_cols, precision=precise)
+
     spread = lax.all_to_all(distribution, "ky", split_axis=2, concat_axis=1, tiled=True)
     local_cols = spread.shape[2]
     forward, backward = wigner_tables(ky_count)
@@ -103,12 +123,27 @@
     )
     mixed = mixed.reshape(row_count, ky_count, local_cols, kx_count)
     wigner = lax.all_to_all(mixed, "ky", split_axis=1, concat_axis=2, tiled=True)
+
     positive_kx = upwind_sign > 0
-    padded = with_halo(distribution, (("space", 0),), 1)
-    from_left = padded[:-2]
-    from_right = padded[2:]
-    upstream_x = jnp.where(positive_kx[None, None, None, :], from_left, from_right)
+    half_kx = kx_count // 2
+    rank_pos = jnp.cumsum(positive_kx.astype(jnp.int32)) - 1
+    rank_neg = jnp.cumsum((~positive_kx).astype(jnp.int32)) - 1
+    slots = jnp.arange(half_kx, dtype=jnp.int32)
+    pick_pos = (positive_kx[:, None] & (rank_pos[:, None] == slots[None, :])).astype(jnp.float32)
+    pick_neg = ((~positive_kx)[:, None] & (rank_neg[:, None] == slots[None, :])).astype(jnp.float32)
+    flat = distribution.reshape(-1, kx_count)
+    send_right = jnp.dot(flat, pick_pos, precision=precise)
+    send_left = jnp.dot(flat, pick_neg, precision=precise)
+    forward_pairs = [(i, i + 1) for i in range(space_count - 1)]
+    backward_pairs = [(i + 1, i) for i in range(space_count - 1)]
+    got_left = lax.ppermute(send_right, "space", forward_pairs)
+    got_right = lax.ppermute(send_left, "space", backward_pairs)
+    upstream_x = jnp.dot(got_left, pick_pos.T, precision=precise) + jnp.dot(
+        got_right, pick_neg.T, precision=precise
+    )
+    upstream_x = upstream_x.reshape(distribution.shape)
     drift_x = -kx_speed[None, None, None, :] * (distribution - upstream_x)
+
     ky_global = lax.axis_index("ky") * ky_local + jnp.arange(ky_local, dtype=jnp.int32)
     upward = ky_global >= ky_count // 2
     vertical = DRIFT_Y * (ky_global.astype(jnp.float32) + 0.5 - 0.5 * ky_count) / (0.5 * ky_count)

time: 379 us -> 310 us (0.82)
  the two profiles are of different devices: /device:TPU:40 before, /device:TPU:120 now
where the time goes in v1:
time: 310 us; the launch traced here: 309 us
  waiting for transfers between devices  195 us (63%)
  starting transfers between devices  59.3 us (19%)
  local copies, waits for them, and re-layouts  25.8 us (8%)
  matrix products  19.8 us (6%)
  other arithmetic  8.65 us (3%)
    ppermute x3, waiting for transfers between devices, sum_over(): value = value + lax.ppermute(value, axis, xor_pairs(count, bit))  86.4 us
    ppermute x1, waiting for transfers between devices, shards(): got_right = lax.ppermute(send_left, 'space', backward_pairs)  81.9 us
    ppermute x6, waiting for transfers between devices, gather_rows(): other = lax.ppermute(value, axis, xor_pairs(count, bit))  20.2 us
    ppermute x3, starting transfers between devices, sum_over(): value = value + lax.ppermute(value, axis, xor_pairs(count, bit))  18.7 us
    ppermute x6, starting transfers between devices, gather_rows(): other = lax.ppermute(value, axis, xor_pairs(count, bit))  16.1 us
    all_to_all x1, starting transfers between devices, shards(): lax.all_to_all(distribution, 'ky', split_axis=2, concat_axis=1, tiled=True)  15.4 us
    ppermute x1, waiting for transfers between devices, shards(): got_left = lax.ppermute(send_right, 'space', forward_pairs)  6.82 us
  transfers between devices with their start and end apart: 13, of which 11 were waited for; matrix products, arithmetic and copies ran while one was open for 10% of the time, Pallas kernels for 0%

profile of v1, /device:TPU:120, one launch (start us, length us, event | category | flops | bytes accessed | tf_op | source)
XLA Modules:
  0.0 309.3 jit_solution(8371180670047887962)
XLA Ops:
  0.0 4.2 %copy.40 = f32[1,16,256,128]{3,1,0,2:T(8,128)} copy(f32[1,16,256,128]{3,2,1,0:T(8,128)} %param.7) | data formatting | bytes 4194304 | tf_op args[0]
  4.2 15.4 %all-to-all-start = ((f32[1,16,256,128]{3,1,0,2:T(8,128)}), f32[1,16,256,128]{3,1,0,2:T(8,128)}, u32[]{:S(2)}, u32[]{:S(2)}) async-start(f32[1,16,256,128]{3,1,0,2:T(8,128)} %copy.40), calls=%async_computation | async-start | bytes 4194304 | tf_op jit(solution)/shard_map/all_to_all | solution.py:110
  19.6 0.2 reduce_sum.29
  19.8 2.8 collective-permute-start.2
  22.5 9.6 %collective-permute-done.2 = f32[1,256]{1,0:T(1,128)S(1)} collective-permute-done((f32[1,256]{1,0:T(1,128)S(1)}, f32[1,256]{1,0:T(1,128)S(1)}, u32[]{:S(2)}, u32[]{:S(2)}) %collective-permute-start.2) | collective-permute-done | bytes 1056 | tf_op jit(solution)/shard_map/ppermute | solution.py:63
  32.1 3.1 %collective-permute-start.3 = (f32[1,256]{1,0:T(1,128)S(1)}, f32[1,256]{1,0:T(1,128)S(1)}, u32[]{:S(2)}, u32[]{:S(2)}) collective-permute-start(f32[1,256]{1,0:T(1,128)S(1)} %add.168), channel_id=1, source_target_pairs={{0,2},{1,3},{2,0},{3,1},{4,6},{5,7},{6,4},{7,5},{8,10},{9,11},{10,... | collective-permute-start | bytes 3080 | tf_op jit(solution)/shard_map/ppermute | solution.py:63
  35.4 3.7 %collective-permute-done.3 = f32[1,256]{1,0:T(1,128)S(1)} collective-permute-done((f32[1,256]{1,0:T(1,128)S(1)}, f32[1,256]{1,0:T(1,128)S(1)}, u32[]{:S(2)}, u32[]{:S(2)}) %collective-permute-start.3) | collective-permute-done | bytes 1056 | tf_op jit(solution)/shard_map/ppermute | solution.py:63
  39.1 12.9 %collective-permute-start.4 = (f32[1,256]{1,0:T(1,128)S(1)}, f32[1,256]{1,0:T(1,128)S(1)}, u32[]{:S(2)}, u32[]{:S(2)}) collective-permute-start(f32[1,256]{1,0:T(1,128)S(1)} %add.169), channel_id=1, source_target_pairs={{0,4},{1,5},{2,6},{3,7},{4,0},{5,1},{6,2},{7,3},{8,12},{9,13},{10,... | collective-permute-start | bytes 3080 | tf_op jit(solution)/shard_map/ppermute | solution.py:63
  52.0 73.0 %collective-permute-done.4 = f32[1,256]{1,0:T(1,128)S(1)} collective-permute-done((f32[1,256]{1,0:T(1,128)S(1)}, f32[1,256]{1,0:T(1,128)S(1)}, u32[]{:S(2)}, u32[]{:S(2)}) %collective-permute-start.4) | collective-permute-done | bytes 1056 | tf_op jit(solution)/shard_map/ppermute | solution.py:63
  125.0 1.9 collective-permute-start.5
  127.0 0.3 fusion.66
  127.3 0.8 collective-permute-done.5
  128.1 3.4 %collective-permute-start.6 = (f32[2,256]{1,0:T(2,128)S(1)}, f32[2,256]{1,0:T(2,128)S(1)}, u32[]{:S(2)}, u32[]{:S(2)}) collective-permute-start(f32[2,256]{1,0:T(2,128)S(1)} %maximum_select_fusion.6), channel_id=1, source_target_pairs={{0,16},{8,24},{16,0},{24,8},{32,48},{40,56},{48,32},{56,40},{64,80... | collective-permute-start | bytes 6152 | tf_op jit(solution)/shard_map/ppermute | solution.py:73
  131.5 0.2 fusion.83
  131.7 1.8 collective-permute-done.6
  133.6 4.9 %collective-permute-start.7 = (f32[4,256]{1,0:T(4,128)S(1)}, f32[4,256]{1,0:T(4,128)S(1)}, u32[]{:S(2)}, u32[]{:S(2)}) collective-permute-start(f32[4,256]{1,0:T(4,128)S(1)} %maximum_select_fusion.5), channel_id=1, source_target_pairs={{0,32},{8,40},{16,48},{24,56},{32,0},{40,8},{48,16},{56,24},{64,96... | collective-permute-start | bytes 12296 | tf_op jit(solution)/shard_map/ppermute | solution.py:73
  138.5 0.2 fusion.63
  138.7 1.8 collective-permute-done.7
  140.6 1.9 collective-permute-start.8
  142.5 3.6 %collective-permute-done.8 = f32[8,256]{1,0:T(8,128)S(1)} collective-permute-done((f32[8,256]{1,0:T(8,128)S(1)}, f32[8,256]{1,0:T(8,128)S(1)}, u32[]{:S(2)}, u32[]{:S(2)}) %collective-permute-start.8) | collective-permute-done | bytes 8224 | tf_op jit(solution)/shard_map/ppermute | solution.py:73
  146.1 1.9 collective-permute-start.9
  148.1 4.6 %collective-permute-done.9 = f32[16,256]{1,0:T(8,128)S(1)} collective-permute-done((f32[16,256]{1,0:T(8,128)S(1)}, f32[16,256]{1,0:T(8,128)S(1)}, u32[]{:S(2)}, u32[]{:S(2)}) %collective-permute-start.9) | collective-permute-done | bytes 16416 | tf_op jit(solution)/shard_map/ppermute | solution.py:73
  152.6 2.1 collective-permute-start.10
  154.8 7.6 %collective-permute-done.10 = f32[32,256]{1,0:T(8,128)S(1)} collective-permute-done((f32[32,256]{1,0:T(8,128)S(1)}, f32[32,256]{1,0:T(8,128)S(1)}, u32[]{:S(2)}, u32[]{:S(2)}) %collective-permute-start.10) | collective-permute-done | bytes 32800 | tf_op jit(solution)/shard_map/ppermute | solution.py:73
  162.3 0.4 fusion.35
  162.7 1.3 convolution_divide_fusion
  164.1 1.3 fusion.14
  173.1 0.3 stack.259
  173.7 1.9 mul.263
  175.6 2.7 mul.264
  178.3 2.4 copy.41
  180.7 2.2 fusion.1
  182.9 3.2 %fusion.41 = f32[4096,128]{1,0:T(8,128)} fusion(f32[128,4096]{1,0:T(8,128)S(1)} %fusion.1, f32[128,64]{1,0:T(8,128)S(1)} %get-tuple-element.80, f32[128,64]{1,0:T(8,128)S(1)} %get-tuple-element.79), kind=kOutput, calls=%fused_computation.51 | convolution fusion | flops 402669568 | bytes 4259840 | tf_op jit(solution)/shard_map/ab,rbm->ram/dot_general | solution.py:118
  186.1 3.1 copy.107
  189.1 4.7 %all-to-all-start.1 = ((f32[1,128,32,128]{3,2,0,1:T(8,128)}), f32[1,128,32,128]{3,2,0,1:T(8,128)}, u32[]{:S(2)}, u32[]{:S(2)}) async-start(f32[1,128,32,128]{3,2,0,1:T(8,128)} %copy.107), calls=%async_computation.1 | async-start | bytes 4194304 | tf_op jit(solution)/shard_map/all_to_all | solution.py:125
  194.2 2.4 convolution_bitcast_fusion.1
  196.6 2.0 collective-permute-start.1
  199.0 2.5 convolution_bitcast_fusion.2
  201.5 2.4 collective-permute-start
  203.9 2.4 fusion.233
  206.4 81.9 %collective-permute-done.1 = f32[4096,64]{0,1:T(8,128)S(1)} collective-permute-done((f32[4096,64]{0,1:T(8,128)}, f32[4096,64]{0,1:T(8,128)S(1)}, u32[]{:S(2)}, u32[]{:S(2)}) %collective-permute-start.1) | collective-permute-done | bytes 1048608 | tf_op jit(solution)/shard_map/ppermute | solution.py:140
  288.3 1.9 fusion.52
  290.2 6.8 %collective-permute-done = f32[4096,64]{0,1:T(8,128)} collective-permute-done((f32[4096,64]{0,1:T(8,128)}, f32[4096,64]{0,1:T(8,128)}, u32[]{:S(2)}, u32[]{:S(2)}) %collective-permute-start) | collective-permute-done | bytes 1048608 | tf_op jit(solution)/shard_map/ppermute | solution.py:139
  297.0 4.5 %convolution_add_fusion = f32[4096,128]{1,0:T(8,128)} fusion(f32[4096,128]{1,0:T(8,128)S(1)} %fusion.52, f32[4096,64]{0,1:T(8,128)} %collective-permute-done, s32[128]{0:T(128)S(1)} %add_reduce_fusion.1, pred[128]{0:T(512)(128)(4,1)S(1)} %get-tuple-element.75), kind=kOutput, calls=%fused_computation.1 | convolution fusion | flops 403193856 | bytes 5243520 | tf_op jit(solution)/shard_map/dot_general | solution.py:141
  301.5 1.9 copy.108
  303.5 0.3 copy-done.1
  303.8 0.6 copy-done.3
  304.4 4.9 %fusion.6 = f32[1,16,256,128]{3,2,1,0:T(8,128)} fusion(f32[1,16,256,128]{3,2,1,0:T(8,128)S(1)} %copy-done, f32[1,16,8,32,128]{4,3,2,1,0:T(8,128)S(1)} %copy.108, f32[1,16,255,128]{3,2,1,0:T(8,128)} %get-tuple-element.10, f32[1,16,255,128]{3,2,1,0:T(8,128)S(1)} %copy-done.3, f32[1,16,256,128]{3,2,1,0:T(8,128)S(1)} %bitcast.195, f32[16,128]{1,0:T(8,128)S(1)} %copy-done.4, ...), kind=kLoop, calls=%fused_computation.11 | loop fusion | flops 6815744 | bytes 12577360 | tf_op jit(solution)/shard_map/add | solution.py:158
  (129 shorter events, 8.9 us)
Async XLA Ops:
  4.2 15.4 %copy-start = (f32[1,16,256,128]{3,2,1,0:T(8,128)S(1)}, f32[1,16,256,128]{3,2,1,0:T(8,128)}, u32[]{:S(2)}) copy-start(f32[1,16,256,128]{3,2,1,0:T(8,128)} %param.7) | copy-start | bytes 6291460
  4.2 174.1 %all-to-all-start = ((f32[1,16,256,128]{3,1,0,2:T(8,128)}), f32[1,16,256,128]{3,1,0,2:T(8,128)}, u32[]{:S(2)}, u32[]{:S(2)}) async-start(f32[1,16,256,128]{3,1,0,2:T(8,128)} %copy.40), calls=%async_computation | async-start | bytes 4194304 | tf_op jit(solution)/shard_map/all_to_all | solution.py:110
  19.5 15.7 %copy-start.5 = (s32[1,256]{1,0:T(1,128)S(1)}, s32[1,256]{1,0:T(1,128)}, u32[]{:S(2)}) copy-start(s32[1,256]{1,0:T(1,128)} %param.8) | copy-start | bytes 3076
  19.6 15.7 %copy-start.7 = (f32[6]{0:T(128)S(1)}, f32[6]{0:T(128)}, u32[]{:S(2)}) copy-start(f32[6]{0:T(128)} %param.10) | copy-start | bytes 76
  19.6 15.7 %copy-start.8 = (f32[6]{0:T(128)S(1)}, f32[6]{0:T(128)}, u32[]{:S(2)}) copy-start(f32[6]{0:T(128)} %param.9) | copy-start | bytes 76
  19.8 12.4 %collective-permute-start.2 = (f32[1,256]{1,0:T(1,128)S(1)}, f32[1,256]{1,0:T(1,128)S(1)}, u32[]{:S(2)}, u32[]{:S(2)}) collective-permute-start(f32[1,256]{1,0:T(1,128)S(1)} %bitcast.216), channel_id=1, source_target_pairs={{0,1},{1,0},{2,3},{3,2},{4,5},{5,4},{6,7},{7,6},{8,9},{9,8},{10,11... | collective-permute-start | bytes 3080 | tf_op jit(solution)/shard_map/ppermute | solution.py:63
  32.1 7.0 %collective-permute-start.3 = (f32[1,256]{1,0:T(1,128)S(1)}, f32[1,256]{1,0:T(1,128)S(1)}, u32[]{:S(2)}, u32[]{:S(2)}) collective-permute-start(f32[1,256]{1,0:T(1,128)S(1)} %add.168), channel_id=1, source_target_pairs={{0,2},{1,3},{2,0},{3,1},{4,6},{5,7},{6,4},{7,5},{8,10},{9,11},{10,... | collective-permute-start | bytes 3080 | tf_op jit(solution)/shard_map/ppermute | solution.py:63
  39.1 85.9 %collective-permute-start.4 = (f32[1,256]{1,0:T(1,128)S(1)}, f32[1,256]{1,0:T(1,128)S(1)}, u32[]{:S(2)}, u32[]{:S(2)}) collective-permute-start(f32[1,256]{1,0:T(1,128)S(1)} %add.169), channel_id=1, source_target_pairs={{0,4},{1,5},{2,6},{3,7},{4,0},{5,1},{6,2},{7,3},{8,12},{9,13},{10,... | collective-permute-start | bytes 3080 | tf_op jit(solution)/shard_map/ppermute | solution.py:63
  125.0 3.0 collective-permute-start.5
  128.1 5.5 %collective-permute-start.6 = (f32[2,256]{1,0:T(2,128)S(1)}, f32[2,256]{1,0:T(2,128)S(1)}, u32[]{:S(2)}, u32[]{:S(2)}) collective-permute-start(f32[2,256]{1,0:T(2,128)S(1)} %maximum_select_fusion.6), channel_id=1, source_target_pairs={{0,16},{8,24},{16,0},{24,8},{32,48},{40,56},{48,32},{56,40},{64,80... | collective-permute-start | bytes 6152 | tf_op jit(solution)/shard_map/ppermute | solution.py:73
  133.6 7.0 %collective-permute-start.7 = (f32[4,256]{1,0:T(4,128)S(1)}, f32[4,256]{1,0:T(4,128)S(1)}, u32[]{:S(2)}, u32[]{:S(2)}) collective-permute-start(f32[4,256]{1,0:T(4,128)S(1)} %maximum_select_fusion.5), channel_id=1, source_target_pairs={{0,32},{8,40},{16,48},{24,56},{32,0},{40,8},{48,16},{56,24},{64,96... | collective-permute-start | bytes 12296 | tf_op jit(solution)/shard_map/ppermute | solution.py:73
  140.6 5.5 %collective-permute-start.8 = (f32[8,256]{1,0:T(8,128)S(1)}, f32[8,256]{1,0:T(8,128)S(1)}, u32[]{:S(2)}, u32[]{:S(2)}) collective-permute-start(f32[8,256]{1,0:T(8,128)S(1)} %maximum_select_fusion.4), channel_id=1, source_target_pairs={{0,64},{8,72},{16,80},{24,88},{32,96},{40,104},{48,112},{56,120},{... | collective-permute-start | bytes 24584 | tf_op jit(solution)/shard_map/ppermute | solution.py:73
  146.1 6.5 %collective-permute-start.9 = (f32[16,256]{1,0:T(8,128)S(1)}, f32[16,256]{1,0:T(8,128)S(1)}, u32[]{:S(2)}, u32[]{:S(2)}) collective-permute-start(f32[16,256]{1,0:T(8,128)S(1)} %maximum_select_fusion.3), channel_id=1, source_target_pairs={{0,128},{8,136},{16,144},{24,152},{32,160},{40,168},{48,176},{56,1... | collective-permute-start | bytes 49160 | tf_op jit(solution)/shard_map/ppermute | solution.py:73
  152.6 9.7 %collective-permute-start.10 = (f32[32,256]{1,0:T(8,128)S(1)}, f32[32,256]{1,0:T(8,128)S(1)}, u32[]{:S(2)}, u32[]{:S(2)}) collective-permute-start(f32[32,256]{1,0:T(8,128)S(1)} %maximum_select_fusion.2), channel_id=1, source_target_pairs={{0,256},{8,264},{16,272},{24,280},{32,288},{40,296},{48,304},{56,3... | collective-permute-start | bytes 98312 | tf_op jit(solution)/shard_map/ppermute | solution.py:73
  178.3 2.4 copy-start.2
  189.1 4.7 %copy-start.6 = (s32[128]{0:T(128)S(1)}, s32[128]{0:T(128)}, u32[]{:S(2)}) copy-start(s32[128]{0:T(128)} %param.13) | copy-start | bytes 1540
  189.1 112.4 %all-to-all-start.1 = ((f32[1,128,32,128]{3,2,0,1:T(8,128)}), f32[1,128,32,128]{3,2,0,1:T(8,128)}, u32[]{:S(2)}, u32[]{:S(2)}) async-start(f32[1,128,32,128]{3,2,0,1:T(8,128)} %copy.107), calls=%async_computation.1 | async-start | bytes 4194304 | tf_op jit(solution)/shard_map/all_to_all | solution.py:125
  196.6 7.3 %copy-start.9 = (f32[128]{0:T(128)S(1)}, f32[128]{0:T(128)}, u32[]{:S(2)}) copy-start(f32[128]{0:T(128)} %param.12) | copy-start | bytes 1540
  196.6 91.7 %collective-permute-start.1 = (f32[4096,64]{0,1:T(8,128)}, f32[4096,64]{0,1:T(8,128)S(1)}, u32[]{:S(2)}, u32[]{:S(2)}) collective-permute-start(f32[4096,64]{0,1:T(8,128)} %convolution_bitcast_fusion.1), channel_id=1, source_target_pairs={{8,0},{16,8},{24,16},{32,24},{40,32},{48,40},{56,48},{64,56},{72,6... | collective-permute-start | bytes 3145736 | tf_op jit(solution)/shard_map/ppermute | solution.py:140
  201.5 95.5 %collective-permute-start = (f32[4096,64]{0,1:T(8,128)}, f32[4096,64]{0,1:T(8,128)}, u32[]{:S(2)}, u32[]{:S(2)}) collective-permute-start(f32[4096,64]{0,1:T(8,128)} %convolution_bitcast_fusion.2), channel_id=1, source_target_pairs={{0,8},{8,16},{16,24},{24,32},{32,40},{40,48},{48,56},{56,64},{64,7... | collective-permute-start | bytes 3145736 | tf_op jit(solution)/shard_map/ppermute | solution.py:139
  301.5 2.2 copy-start.1
  301.5 2.9 copy-start.3
  301.5 2.9 copy-start.4

commit v2 on v1

--- a/solution.py
+++ b/solution.py
@@ -65,19 +65,24 @@
     return value
 
 
-def gather_rows(value, axis):
+def gather_rows(value, axis, bits):
     count = lax.axis_size(axis)
     index = lax.axis_index(axis)
-    bit, level = 1, 0
-    while bit < count:
+    for bit in bits:
         other = lax.ppermute(value, axis, xor_pairs(count, bit))
-        low = ((index >> level) & 1) == 0
+        low = (index & bit) == 0
         value = jnp.where(
             low, jnp.concatenate([value, other], 0), jnp.concatenate([other, value], 0)
         )
-        bit *= 2
-        level += 1
     return value
+
+
+def in_row_order(value, bits, count):
+    levels = len(bits)
+    shaped = value.reshape((2,) * levels + (-1,) + value.shape[1:])
+    order = sorted(range(levels), key=lambda axis: -bits[levels - 1 - axis])
+    shaped = jnp.transpose(shaped, order + list(range(levels, shaped.ndim)))
+    return shaped.reshape((count,) + value.shape[1:])
 
 
 def shards(distribution, region, region_doping, region_relax, equilibrium, kx_speed, upwind_sign):
@@ -95,7 +100,12 @@
     doping = lookup(region, region_doping)
     relax_rate = lookup(region, region_relax)
     charge = density - doping
-    every_row = gather_rows(charge, "space")
+    far_bits = [bit for bit in (8, 16, 32) if bit < space_count]
+    near_bits = [bit for bit in (1, 2, 4) if bit < space_count]
+    far_rows = gather_rows(charge, "space", far_bits)
+    held, far_rows = lax.optimization_barrier((distribution, far_rows))
+    every_row = gather_rows(far_rows, "space", near_bits)
+    every_row = in_row_order(every_row, far_bits + near_bits, space_count * row_count)
 
     sine_rows = sine_table(grid_rows)
     sine_cols = sine_table(col_count)
@@ -107,7 +117,7 @@
     own_rows = lax.dynamic_slice_in_dim(sine_rows, row_start, row_count, 0)
     potential = POISSON * jnp.dot(own_rows, back_cols, precision=precise)
 
-    spread = lax.all_to_all(distribution, "ky", split_axis=2, concat_axis=1, tiled=True)
+    spread = lax.all_to_all(held, "ky", split_axis=2, concat_axis=1, tiled=True)
     local_cols = spread.shape[2]
     forward, backward = wigner_tables(ky_count)
     weights = own_differences(potential, ky_count, lax.axis_index("ky") * local_cols, local_cols)

time: 310 us -> 282 us (0.910)
  the two profiles are of different devices: /device:TPU:120 before, /device:TPU:23 now
where the time goes in v2:
time: 282 us
  starting transfers between devices  139 us (49%)
  waiting for transfers between devices  93.1 us (33%)
  local copies, waits for them, and re-layouts  19.5 us (7%)
  matrix products  19.4 us (7%)
  other arithmetic  10.4 us (4%)
    ppermute x1, waiting for transfers between devices, shards(): got_right = lax.ppermute(send_left, 'space', backward_pairs)  71.7 us
    ppermute x1, starting transfers between devices, shards(): got_left = lax.ppermute(send_right, 'space', forward_pairs)  43.8 us
    ppermute x6, starting transfers between devices, gather_rows(): other = lax.ppermute(value, axis, xor_pairs(count, bit))  27.7 us
    ppermute x1, starting transfers between devices, shards(): got_right = lax.ppermute(send_left, 'space', backward_pairs)  22.4 us
    ppermute x3, starting transfers between devices, sum_over(): value = value + lax.ppermute(value, axis, xor_pairs(count, bit))  20.3 us
    all_to_all x1, starting transfers between devices, shards(): spread = lax.all_to_all(held, 'ky', split_axis=2, concat_axis=1, tiled=True)  14.1 us
    ppermute x6, waiting for transfers between devices, gather_rows(): other = lax.ppermute(value, axis, xor_pairs(count, bit))  12.2 us
    all_to_all x1, starting transfers between devices, shards(): lax.all_to_all(mixed, 'ky', split_axis=1, concat_axis=2, tiled=True)  10.8 us
  transfers between devices with their start and end apart: 13, of which 11 were waited for; matrix products, arithmetic and copies ran while one was open for 9% of the time, Pallas kernels for 0%

profile of v2, /device:TPU:23, one launch (start us, length us, event | category | flops | bytes accessed | tf_op | source)
XLA Modules:
  0.0 281.8 jit_solution(8921907889646347725)
XLA Ops:
  0.0 1.9 reduce_sum.29
  1.9 2.9 %collective-permute-start.2 = (f32[1,256]{1,0:T(1,128)S(1)}, f32[1,256]{1,0:T(1,128)S(1)}, u32[]{:S(2)}, u32[]{:S(2)}) collective-permute-start(f32[1,256]{1,0:T(1,128)S(1)} %bitcast.221), channel_id=1, source_target_pairs={{0,1},{1,0},{2,3},{3,2},{4,5},{5,4},{6,7},{7,6},{8,9},{9,8},{10,11... | collective-permute-start | bytes 3080 | tf_op jit(solution)/shard_map/ppermute | solution.py:63
  4.9 1.4 collective-permute-done.2
  6.3 2.0 collective-permute-start.3
  8.2 3.8 %collective-permute-done.3 = f32[1,256]{1,0:T(1,128)S(1)} collective-permute-done((f32[1,256]{1,0:T(1,128)S(1)}, f32[1,256]{1,0:T(1,128)S(1)}, u32[]{:S(2)}, u32[]{:S(2)}) %collective-permute-start.3) | collective-permute-done | bytes 1056 | tf_op jit(solution)/shard_map/ppermute | solution.py:63
  12.1 15.4 %collective-permute-start.4 = (f32[1,256]{1,0:T(1,128)S(1)}, f32[1,256]{1,0:T(1,128)S(1)}, u32[]{:S(2)}, u32[]{:S(2)}) collective-permute-start(f32[1,256]{1,0:T(1,128)S(1)} %add.165), channel_id=1, source_target_pairs={{0,4},{1,5},{2,6},{3,7},{4,0},{5,1},{6,2},{7,3},{8,12},{9,13},{10,... | collective-permute-start | bytes 3080 | tf_op jit(solution)/shard_map/ppermute | solution.py:63
  27.6 0.8 collective-permute-done.4
  28.5 2.6 collective-permute-start.5
  31.1 1.6 collective-permute-done.5
  32.8 3.1 %collective-permute-start.6 = (f32[2,256]{1,0:T(2,128)S(1)}, f32[2,256]{1,0:T(2,128)S(1)}, u32[]{:S(2)}, u32[]{:S(2)}) collective-permute-start(f32[2,256]{1,0:T(2,128)S(1)} %maximum_select_fusion.5), channel_id=1, source_target_pairs={{0,128},{8,136},{16,144},{24,152},{32,160},{40,168},{48,176},{56,1... | collective-permute-start | bytes 6152 | tf_op jit(solution)/shard_map/ppermute | solution.py:72
  35.9 2.1 collective-permute-done.6
  38.0 6.3 %collective-permute-start.7 = (f32[4,256]{1,0:T(4,128)S(1)}, f32[4,256]{1,0:T(4,128)S(1)}, u32[]{:S(2)}, u32[]{:S(2)}) collective-permute-start(f32[4,256]{1,0:T(4,128)S(1)} %maximum_select_fusion.4), channel_id=1, source_target_pairs={{0,256},{8,264},{16,272},{24,280},{32,288},{40,296},{48,304},{56,3... | collective-permute-start | bytes 12296 | tf_op jit(solution)/shard_map/ppermute | solution.py:72
  44.3 2.0 collective-permute-done.7
  46.3 2.5 copy.44
  48.8 14.1 %all-to-all-start = ((f32[1,16,256,128]{3,1,0,2:T(8,128)}), f32[1,16,256,128]{3,1,0,2:T(8,128)}, u32[]{:S(2)}, u32[]{:S(2)}) async-start(f32[1,16,256,128]{3,1,0,2:T(8,128)} %copy.44), calls=%async_computation | async-start | bytes 4194304 | tf_op jit(solution)/shard_map/all_to_all | solution.py:120
  62.9 0.2 fusion.57
  63.2 0.2 fusion.76
  63.4 0.3 fusion.60
  63.7 10.0 %collective-permute-start.8 = (f32[8,256]{1,0:T(8,128)S(1)}, f32[8,256]{1,0:T(8,128)S(1)}, u32[]{:S(2)}, u32[]{:S(2)}) collective-permute-start(f32[8,256]{1,0:T(8,128)S(1)} %maximum_select_fusion.3), channel_id=1, source_target_pairs={{0,8},{8,0},{16,24},{24,16},{32,40},{40,32},{48,56},{56,48},{64,72... | collective-permute-start | bytes 24584 | tf_op jit(solution)/shard_map/ppermute | solution.py:72
  73.7 0.8 collective-permute-done.8
  74.5 2.4 collective-permute-start.9
  77.0 2.4 collective-permute-done.9
  79.4 3.2 %collective-permute-start.10 = (f32[32,256]{1,0:T(8,128)S(1)}, f32[32,256]{1,0:T(8,128)S(1)}, u32[]{:S(2)}, u32[]{:S(2)}) collective-permute-start(f32[32,256]{1,0:T(8,128)S(1)} %maximum_select_fusion.1), channel_id=1, source_target_pairs={{0,32},{8,40},{16,48},{24,56},{32,0},{40,8},{48,16},{56,24},{64,96... | collective-permute-start | bytes 98312 | tf_op jit(solution)/shard_map/ppermute | solution.py:72
  82.7 3.3 %collective-permute-done.10 = f32[32,256]{1,0:T(8,128)S(1)} collective-permute-done((f32[32,256]{1,0:T(8,128)S(1)}, f32[32,256]{1,0:T(8,128)S(1)}, u32[]{:S(2)}, u32[]{:S(2)}) %collective-permute-start.10) | collective-permute-done | bytes 32800 | tf_op jit(solution)/shard_map/ppermute | solution.py:72
  86.1 0.4 fusion.77
  86.5 1.3 convolution_divide_fusion
  87.8 1.3 fusion.14
  96.9 0.3 stack.259
  97.3 3.2 %all-to-all-done = f32[1,16,256,128]{3,1,0,2:T(8,128)} async-done(((f32[1,16,256,128]{3,1,0,2:T(8,128)}), f32[1,16,256,128]{3,1,0,2:T(8,128)}, u32[]{:S(2)}, u32[]{:S(2)}) %all-to-all-start) | async-done | bytes 2097184 | tf_op jit(solution)/shard_map/all_to_all | solution.py:120
  100.5 2.2 copy.45
  102.9 2.6 fusion.1
  105.5 2.4 fusion.35
  107.9 3.0 %copy.111 = f32[1,128,32,128]{3,2,0,1:T(8,128)} copy(f32[1,128,32,128]{1,3,2,0:T(8,128)} %bitcast.201) | data formatting | bytes 4194304 | tf_op jit(solution)/shard_map/reshape | solution.py:134
  110.9 10.8 %all-to-all-start.1 = ((f32[1,128,32,128]{3,2,0,1:T(8,128)}), f32[1,128,32,128]{3,2,0,1:T(8,128)}, u32[]{:S(2)}, u32[]{:S(2)}) async-start(f32[1,128,32,128]{3,2,0,1:T(8,128)} %copy.111), calls=%async_computation.1 | async-start | bytes 4194304 | tf_op jit(solution)/shard_map/all_to_all | solution.py:135
  121.9 0.2 reduce-window.17
  122.1 2.4 convolution_bitcast_fusion.1
  124.5 22.4 %collective-permute-start.1 = (f32[4096,64]{0,1:T(8,128)}, f32[4096,64]{0,1:T(8,128)S(1)}, u32[]{:S(2)}, u32[]{:S(2)}) collective-permute-start(f32[4096,64]{0,1:T(8,128)} %convolution_bitcast_fusion.1), channel_id=1, source_target_pairs={{8,0},{16,8},{24,16},{32,24},{40,32},{48,40},{56,48},{64,56},{72,6... | collective-permute-start | bytes 3145736 | tf_op jit(solution)/shard_map/ppermute | solution.py:150
  147.0 0.2 reduce-window.16
  147.3 2.5 convolution_bitcast_fusion.2
  149.7 43.8 %collective-permute-start = (f32[4096,64]{0,1:T(8,128)}, f32[4096,64]{0,1:T(8,128)}, u32[]{:S(2)}, u32[]{:S(2)}) collective-permute-start(f32[4096,64]{0,1:T(8,128)} %convolution_bitcast_fusion.2), channel_id=1, source_target_pairs={{0,8},{8,16},{16,24},{24,32},{32,40},{40,48},{48,56},{56,64},{64,7... | collective-permute-start | bytes 3145736 | tf_op jit(solution)/shard_map/ppermute | solution.py:149
  193.6 2.4 fusion.226
  196.0 71.7 %collective-permute-done.1 = f32[4096,64]{0,1:T(8,128)S(1)} collective-permute-done((f32[4096,64]{0,1:T(8,128)}, f32[4096,64]{0,1:T(8,128)S(1)}, u32[]{:S(2)}, u32[]{:S(2)}) %collective-permute-start.1) | collective-permute-done | bytes 1048608 | tf_op jit(solution)/shard_map/ppermute | solution.py:150
  267.7 1.9 fusion.46
  269.6 4.5 %convolution_add_fusion = f32[4096,128]{1,0:T(8,128)} fusion(f32[4096,128]{1,0:T(8,128)S(1)} %fusion.46, f32[4096,64]{0,1:T(8,128)} %collective-permute-done, s32[128]{0:T(128)S(1)} %add_reduce_fusion.1, pred[128]{0:T(512)(128)(4,1)S(1)} %get-tuple-element.79), kind=kOutput, calls=%fused_computation.1 | convolution fusion | flops 403193856 | bytes 5243520 | tf_op jit(solution)/shard_map/dot_general | solution.py:151
  274.1 1.9 copy.112
  276.0 0.3 copy-done.1
  276.3 0.6 copy-done.2
  276.9 4.9 %fusion.6 = f32[1,16,256,128]{3,2,1,0:T(8,128)} fusion(f32[1,16,256,128]{3,2,1,0:T(8,128)S(1)} %copy-done, f32[1,16,8,32,128]{4,3,2,1,0:T(8,128)S(1)} %copy.112, f32[1,16,255,128]{3,2,1,0:T(8,128)} %get-tuple-element.14, f32[1,16,255,128]{3,2,1,0:T(8,128)S(1)} %copy-done.2, f32[1,16,256,128]{3,2,1,0:T(8,128)S(1)} %bitcast.198, f32[16,128]{1,0:T(8,128)S(1)} %copy-done.3, ...), kind=kLoop, calls=%fused_computation.11 | loop fusion | flops 6815744 | bytes 12577360 | tf_op jit(solution)/shard_map/add | solution.py:168
  (129 shorter events, 8.7 us)
Async XLA Ops:
  0.0 46.3 %copy-start = (f32[1,16,256,128]{3,2,1,0:T(8,128)S(1)}, f32[1,16,256,128]{3,2,1,0:T(8,128)}, u32[]{:S(2)}) copy-start(f32[1,16,256,128]{3,2,1,0:T(8,128)} %param.7) | copy-start | bytes 6291460
  0.0 27.5 %copy-start.6 = (f32[6]{0:T(128)S(1)}, f32[6]{0:T(128)}, u32[]{:S(2)}) copy-start(f32[6]{0:T(128)} %param.10) | copy-start | bytes 76
  0.0 27.5 %copy-start.7 = (f32[6]{0:T(128)S(1)}, f32[6]{0:T(128)}, u32[]{:S(2)}) copy-start(f32[6]{0:T(128)} %param.9) | copy-start | bytes 76
  0.0 27.5 %copy-start.4 = (s32[1,256]{1,0:T(1,128)S(1)}, s32[1,256]{1,0:T(1,128)}, u32[]{:S(2)}) copy-start(s32[1,256]{1,0:T(1,128)} %param.8) | copy-start | bytes 3076
  1.9 4.3 %collective-permute-start.2 = (f32[1,256]{1,0:T(1,128)S(1)}, f32[1,256]{1,0:T(1,128)S(1)}, u32[]{:S(2)}, u32[]{:S(2)}) collective-permute-start(f32[1,256]{1,0:T(1,128)S(1)} %bitcast.221), channel_id=1, source_target_pairs={{0,1},{1,0},{2,3},{3,2},{4,5},{5,4},{6,7},{7,6},{8,9},{9,8},{10,11... | collective-permute-start | bytes 3080 | tf_op jit(solution)/shard_map/ppermute | solution.py:63
  6.3 5.8 %collective-permute-start.3 = (f32[1,256]{1,0:T(1,128)S(1)}, f32[1,256]{1,0:T(1,128)S(1)}, u32[]{:S(2)}, u32[]{:S(2)}) collective-permute-start(f32[1,256]{1,0:T(1,128)S(1)} %add.164), channel_id=1, source_target_pairs={{0,2},{1,3},{2,0},{3,1},{4,6},{5,7},{6,4},{7,5},{8,10},{9,11},{10,... | collective-permute-start | bytes 3080 | tf_op jit(solution)/shard_map/ppermute | solution.py:63
  12.1 16.4 %collective-permute-start.4 = (f32[1,256]{1,0:T(1,128)S(1)}, f32[1,256]{1,0:T(1,128)S(1)}, u32[]{:S(2)}, u32[]{:S(2)}) collective-permute-start(f32[1,256]{1,0:T(1,128)S(1)} %add.165), channel_id=1, source_target_pairs={{0,4},{1,5},{2,6},{3,7},{4,0},{5,1},{6,2},{7,3},{8,12},{9,13},{10,... | collective-permute-start | bytes 3080 | tf_op jit(solution)/shard_map/ppermute | solution.py:63
  28.5 4.3 %collective-permute-start.5 = (f32[1,256]{1,0:T(1,128)S(1)}, f32[1,256]{1,0:T(1,128)S(1)}, u32[]{:S(2)}, u32[]{:S(2)}) collective-permute-start(f32[1,256]{1,0:T(1,128)S(1)} %get-tuple-element.11), channel_id=1, source_target_pairs={{0,64},{8,72},{16,80},{24,88},{32,96},{40,104},{48,112},{56,120},{... | collective-permute-start | bytes 3080 | tf_op jit(solution)/shard_map/ppermute | solution.py:72
  32.8 5.2 %collective-permute-start.6 = (f32[2,256]{1,0:T(2,128)S(1)}, f32[2,256]{1,0:T(2,128)S(1)}, u32[]{:S(2)}, u32[]{:S(2)}) collective-permute-start(f32[2,256]{1,0:T(2,128)S(1)} %maximum_select_fusion.5), channel_id=1, source_target_pairs={{0,128},{8,136},{16,144},{24,152},{32,160},{40,168},{48,176},{56,1... | collective-permute-start | bytes 6152 | tf_op jit(solution)/shard_map/ppermute | solution.py:72
  38.0 8.3 %collective-permute-start.7 = (f32[4,256]{1,0:T(4,128)S(1)}, f32[4,256]{1,0:T(4,128)S(1)}, u32[]{:S(2)}, u32[]{:S(2)}) collective-permute-start(f32[4,256]{1,0:T(4,128)S(1)} %maximum_select_fusion.4), channel_id=1, source_target_pairs={{0,256},{8,264},{16,272},{24,280},{32,288},{40,296},{48,304},{56,3... | collective-permute-start | bytes 12296 | tf_op jit(solution)/shard_map/ppermute | solution.py:72
  48.8 51.7 %all-to-all-start = ((f32[1,16,256,128]{3,1,0,2:T(8,128)}), f32[1,16,256,128]{3,1,0,2:T(8,128)}, u32[]{:S(2)}, u32[]{:S(2)}) async-start(f32[1,16,256,128]{3,1,0,2:T(8,128)} %copy.44), calls=%async_computation | async-start | bytes 4194304 | tf_op jit(solution)/shard_map/all_to_all | solution.py:120
  63.7 10.9 %collective-permute-start.8 = (f32[8,256]{1,0:T(8,128)S(1)}, f32[8,256]{1,0:T(8,128)S(1)}, u32[]{:S(2)}, u32[]{:S(2)}) collective-permute-start(f32[8,256]{1,0:T(8,128)S(1)} %maximum_select_fusion.3), channel_id=1, source_target_pairs={{0,8},{8,0},{16,24},{24,16},{32,40},{40,32},{48,56},{56,48},{64,72... | collective-permute-start | bytes 24584 | tf_op jit(solution)/shard_map/ppermute | solution.py:72
  74.5 4.9 %collective-permute-start.9 = (f32[16,256]{1,0:T(8,128)S(1)}, f32[16,256]{1,0:T(8,128)S(1)}, u32[]{:S(2)}, u32[]{:S(2)}) collective-permute-start(f32[16,256]{1,0:T(8,128)S(1)} %maximum_select_fusion.2), channel_id=1, source_target_pairs={{0,16},{8,24},{16,0},{24,8},{32,48},{40,56},{48,32},{56,40},{64,80... | collective-permute-start | bytes 49160 | tf_op jit(solution)/shard_map/ppermute | solution.py:72
  79.4 6.6 %collective-permute-start.10 = (f32[32,256]{1,0:T(8,128)S(1)}, f32[32,256]{1,0:T(8,128)S(1)}, u32[]{:S(2)}, u32[]{:S(2)}) collective-permute-start(f32[32,256]{1,0:T(8,128)S(1)} %maximum_select_fusion.1), channel_id=1, source_target_pairs={{0,32},{8,40},{16,48},{24,56},{32,0},{40,8},{48,16},{56,24},{64,96... | collective-permute-start | bytes 98312 | tf_op jit(solution)/shard_map/ppermute | solution.py:72
  110.9 10.8 %copy-start.5 = (s32[128]{0:T(128)S(1)}, s32[128]{0:T(128)}, u32[]{:S(2)}) copy-start(s32[128]{0:T(128)} %param.13) | copy-start | bytes 1540
  110.9 163.1 %all-to-all-start.1 = ((f32[1,128,32,128]{3,2,0,1:T(8,128)}), f32[1,128,32,128]{3,2,0,1:T(8,128)}, u32[]{:S(2)}, u32[]{:S(2)}) async-start(f32[1,128,32,128]{3,2,0,1:T(8,128)} %copy.111), calls=%async_computation.1 | async-start | bytes 4194304 | tf_op jit(solution)/shard_map/all_to_all | solution.py:135
  124.5 69.0 %copy-start.8 = (f32[128]{0:T(128)S(1)}, f32[128]{0:T(128)}, u32[]{:S(2)}) copy-start(f32[128]{0:T(128)} %param.12) | copy-start | bytes 1540
  124.5 143.2 %collective-permute-start.1 = (f32[4096,64]{0,1:T(8,128)}, f32[4096,64]{0,1:T(8,128)S(1)}, u32[]{:S(2)}, u32[]{:S(2)}) collective-permute-start(f32[4096,64]{0,1:T(8,128)} %convolution_bitcast_fusion.1), channel_id=1, source_target_pairs={{8,0},{16,8},{24,16},{32,24},{40,32},{48,40},{56,48},{64,56},{72,6... | collective-permute-start | bytes 3145736 | tf_op jit(solution)/shard_map/ppermute | solution.py:150
  149.7 119.8 %collective-permute-start = (f32[4096,64]{0,1:T(8,128)}, f32[4096,64]{0,1:T(8,128)}, u32[]{:S(2)}, u32[]{:S(2)}) collective-permute-start(f32[4096,64]{0,1:T(8,128)} %convolution_bitcast_fusion.2), channel_id=1, source_target_pairs={{0,8},{8,16},{16,24},{24,32},{32,40},{40,48},{48,56},{56,64},{64,7... | collective-permute-start | bytes 3145736 | tf_op jit(solution)/shard_map/ppermute | solution.py:149
  274.1 2.2 copy-start.1
  274.1 2.9 %copy-start.2 = (f32[1,16,255,128]{3,2,1,0:T(8,128)S(1)}, f32[1,16,255,128]{3,2,1,0:T(8,128)}, u32[]{:S(2)}) copy-start(f32[1,16,255,128]{3,2,1,0:T(8,128)} %get-tuple-element.13) | copy-start | bytes 6266884
  274.1 2.9 %copy-start.3 = (f32[16,128]{1,0:T(8,128)S(1)}, f32[16,128]{1,0:T(8,128)}, u32[]{:S(2)}) copy-start(f32[16,128]{1,0:T(8,128)} %param.11) | copy-start | bytes 24580

commit v3 on v2

--- a/solution.py
+++ b/solution.py
@@ -102,8 +102,24 @@
     charge = density - doping
     far_bits = [bit for bit in (8, 16, 32) if bit < space_count]
     near_bits = [bit for bit in (1, 2, 4) if bit < space_count]
+    positive_kx = upwind_sign > 0
+    half_kx = kx_count // 2
+    rank_pos = jnp.cumsum(positive_kx.astype(jnp.int32)) - 1
+    rank_neg = jnp.cumsum((~positive_kx).astype(jnp.int32)) - 1
+    slots = jnp.arange(half_kx, dtype=jnp.int32)
+    pick_pos = (positive_kx[:, None] & (rank_pos[:, None] == slots[None, :])).astype(jnp.float32)
+    pick_neg = ((~positive_kx)[:, None] & (rank_neg[:, None] == slots[None, :])).astype(jnp.float32)
+    flat = distribution.reshape(-1, kx_count)
+    send_right = jnp.dot(flat, pick_pos, precision=precise)
+    send_left = jnp.dot(flat, pick_neg, precision=precise)
+    forward_pairs = [(i, i + 1) for i in range(space_count - 1)]
+    backward_pairs = [(i + 1, i) for i in range(space_count - 1)]
+    got_left = lax.ppermute(send_right, "space", forward_pairs)
+    got_right = lax.ppermute(send_left, "space", backward_pairs)
     far_rows = gather_rows(charge, "space", far_bits)
-    held, far_rows = lax.optimization_barrier((distribution, far_rows))
+    held, far_rows, got_left, got_right = lax.optimization_barrier(
+        (distribution, far_rows, got_left, got_right)
+    )
     every_row = gather_rows(far_rows, "space", near_bits)
     every_row = in_row_order(every_row, far_bits + near_bits, space_count * row_count)
 
@@ -134,20 +150,6 @@
     mixed = mixed.reshape(row_count, ky_count, local_cols, kx_count)
     wigner = lax.all_to_all(mixed, "ky", split_axis=1, concat_axis=2, tiled=True)
 
-    positive_kx = upwind_sign > 0
-    half_kx = kx_count // 2
-    rank_pos = jnp.cumsum(positive_kx.astype(jnp.int32)) - 1
-    rank_neg = jnp.cumsum((~positive_kx).astype(jnp.int32)) - 1
-    slots = jnp.arange(half_kx, dtype=jnp.int32)
-    pick_pos = (positive_kx[:, None] & (rank_pos[:, None] == slots[None, :])).astype(jnp.float32)
-    pick_neg = ((~positive_kx)[:, None] & (rank_neg[:, None] == slots[None, :])).astype(jnp.float32)
-    flat = distribution.reshape(-1, kx_count)
-    send_right = jnp.dot(flat, pick_pos, precision=precise)
-    send_left = jnp.dot(flat, pick_neg, precision=precise)
-    forward_pairs = [(i, i + 1) for i in range(space_count - 1)]
-    backward_pairs = [(i + 1, i) for i in range(space_count - 1)]
-    got_left = lax.ppermute(send_right, "space", forward_pairs)
-    got_right = lax.ppermute(send_left, "space", backward_pairs)
     upstream_x = jnp.dot(got_left, pick_pos.T, precision=precise) + jnp.dot(
         got_right, pick_neg.T, precision=precise
     )

time: 282 us -> 327 us (1.16)
  the two profiles are of different devices: /device:TPU:23 before, /device:TPU:120 now
where the time goes in v3:
time: 327 us; the launch traced here: 326 us
  waiting for transfers between devices  117 us (36%)
  local copies, waits for them, and re-layouts  85.8 us (26%)
  starting transfers between devices  76.8 us (23%)
  matrix products  23.1 us (7%)
  other arithmetic  22.5 us (7%)
    all_to_all x1, waiting for transfers between devices, shards(): lax.all_to_all(mixed, 'ky', split_axis=1, concat_axis=2, tiled=True)  95.5 us
    another operation x65, local copies, waits for them, and re-layouts, own_differences(): return COUPLING * jnp.stack(pieces, axis=1)  72.1 us
    ppermute x6, starting transfers between devices, gather_rows(): other = lax.ppermute(value, axis, xor_pairs(count, bit))  21.8 us
    ppermute x3, starting transfers between devices, sum_over(): value = value + lax.ppermute(value, axis, xor_pairs(count, bit))  18.8 us
    all_to_all x1, starting transfers between devices, shards(): lax.all_to_all(mixed, 'ky', split_axis=1, concat_axis=2, tiled=True)  14.6 us
    ppermute x6, waiting for transfers between devices, gather_rows(): other = lax.ppermute(value, axis, xor_pairs(count, bit))  14.4 us
    all_to_all x1, starting transfers between devices, shards(): spread = lax.all_to_all(held, 'ky', split_axis=2, concat_axis=1, tiled=True)  14 us
    another operation x16, other arithmetic, own_differences(): return COUPLING * jnp.stack(pieces, axis=1)  10.7 us
  transfers between devices with their start and end apart: 13, of which 10 were waited for; matrix products, arithmetic and copies ran while one was open for 32% of the time, Pallas kernels for 0%

profile of v3, /device:TPU:120, one launch (start us, length us, event | category | flops | bytes accessed | tf_op | source)
XLA Modules:
  0.0 325.9 jit_solution(9576286693437130309)
XLA Ops:
  1.2 4.0 %convolution_bitcast_fusion.2 = f32[4096,64]{0,1:T(8,128)} fusion(f32[4096,128]{1,0:T(8,128)} %bitcast.196, s32[128]{0:T(128)S(1)} %add_reduce_fusion.1, pred[128]{0:T(512)(128)(4,1)S(1)} %get-tuple-element.90), kind=kOutput, calls=%fused_computation.5 | convolution fusion | flops 402677760 | bytes 3146368 | tf_op jit(solution)/shard_map/dot_general | solution.py:113
  5.2 1.9 collective-permute-start.6
  7.6 2.4 convolution_bitcast_fusion.1
  9.9 5.7 %collective-permute-start.7 = (f32[4096,64]{0,1:T(8,128)}, f32[4096,64]{0,1:T(8,128)S(1)}, u32[]{:S(2)}, u32[]{:S(2)}) collective-permute-start(f32[4096,64]{0,1:T(8,128)} %convolution_bitcast_fusion.1), channel_id=1, source_target_pairs={{8,0},{16,8},{24,16},{32,24},{40,32},{48,40},{56,48},{64,56},{72,6... | collective-permute-start | bytes 3145736 | tf_op jit(solution)/shard_map/ppermute | solution.py:118
  15.9 2.7 collective-permute-start
  18.5 2.8 collective-permute-done
  21.3 3.1 collective-permute-start.1
  24.5 3.8 %collective-permute-done.1 = f32[1,256]{1,0:T(1,128)S(1)} collective-permute-done((f32[1,256]{1,0:T(1,128)S(1)}, f32[1,256]{1,0:T(1,128)S(1)}, u32[]{:S(2)}, u32[]{:S(2)}) %collective-permute-start.1) | collective-permute-done | bytes 1056 | tf_op jit(solution)/shard_map/ppermute | solution.py:63
  28.3 13.0 %collective-permute-start.2 = (f32[1,256]{1,0:T(1,128)S(1)}, f32[1,256]{1,0:T(1,128)S(1)}, u32[]{:S(2)}, u32[]{:S(2)}) collective-permute-start(f32[1,256]{1,0:T(1,128)S(1)} %add.161), channel_id=1, source_target_pairs={{0,4},{1,5},{2,6},{3,7},{4,0},{5,1},{6,2},{7,3},{8,12},{9,13},{10,... | collective-permute-start | bytes 3080 | tf_op jit(solution)/shard_map/ppermute | solution.py:63
  43.4 2.9 collective-permute-start.3
  46.3 2.5 collective-permute-done.3
  48.9 3.4 %collective-permute-start.4 = (f32[2,256]{1,0:T(2,128)S(1)}, f32[2,256]{1,0:T(2,128)S(1)}, u32[]{:S(2)}, u32[]{:S(2)}) collective-permute-start(f32[2,256]{1,0:T(2,128)S(1)} %maximum_select_fusion.5), channel_id=1, source_target_pairs={{0,128},{8,136},{16,144},{24,152},{32,160},{40,168},{48,176},{56,1... | collective-permute-start | bytes 6152 | tf_op jit(solution)/shard_map/ppermute | solution.py:72
  52.2 3.0 collective-permute-done.4
  55.3 8.7 %collective-permute-start.5 = (f32[4,256]{1,0:T(4,128)S(1)}, f32[4,256]{1,0:T(4,128)S(1)}, u32[]{:S(2)}, u32[]{:S(2)}) collective-permute-start(f32[4,256]{1,0:T(4,128)S(1)} %maximum_select_fusion.4), channel_id=1, source_target_pairs={{0,256},{8,264},{16,272},{24,280},{32,288},{40,296},{48,304},{56,3... | collective-permute-start | bytes 12296 | tf_op jit(solution)/shard_map/ppermute | solution.py:72
  64.0 1.6 collective-permute-done.5
  65.6 2.5 copy.44
  68.1 14.0 %all-to-all-start = ((f32[1,16,256,128]{3,1,0,2:T(8,128)}), f32[1,16,256,128]{3,1,0,2:T(8,128)}, u32[]{:S(2)}, u32[]{:S(2)}) async-start(f32[1,16,256,128]{3,1,0,2:T(8,128)} %copy.44), calls=%async_computation | async-start | bytes 4194304 | tf_op jit(solution)/shard_map/all_to_all | solution.py:136
  83.4 1.9 collective-permute-start.8
  86.5 1.9 collective-permute-start.9
  89.0 3.1 collective-permute-done.9
  92.1 3.0 collective-permute-start.10
  95.7 3.7 %collective-permute-done.10 = f32[32,256]{1,0:T(8,128)S(1)} collective-permute-done((f32[32,256]{1,0:T(8,128)S(1)}, f32[32,256]{1,0:T(8,128)S(1)}, u32[]{:S(2)}, u32[]{:S(2)}) %collective-permute-start.10) | collective-permute-done | bytes 32800 | tf_op jit(solution)/shard_map/ppermute | solution.py:72
  100.0 2.1 convolution_divide_fusion
  102.0 2.1 fusion.14
  121.4 1.4 copy.110
  129.3 1.3 copy.72
  134.5 1.4 copy.94
  139.8 1.4 copy.49
  143.7 1.4 copy.73
  145.1 1.3 copy.74
  154.3 1.4 copy.90
  155.6 1.4 copy.63
  157.0 1.4 copy.64
  162.2 1.4 copy.80
  172.6 1.4 copy.58
  183.1 1.3 copy.89
  185.8 2.1 stack.259
  188.7 2.2 copy.45
  191.0 2.6 fusion.1
  193.6 2.4 fusion.35
  196.0 3.1 copy.111
  199.2 14.6 %all-to-all-start.1 = ((f32[1,128,32,128]{3,2,0,1:T(8,128)}), f32[1,128,32,128]{3,2,0,1:T(8,128)}, u32[]{:S(2)}, u32[]{:S(2)}) async-start(f32[1,128,32,128]{3,2,0,1:T(8,128)} %copy.111), calls=%async_computation.1 | async-start | bytes 4194304 | tf_op jit(solution)/shard_map/all_to_all | solution.py:151
  213.8 2.4 fusion.226
  216.2 1.9 fusion.46
  218.1 4.5 %convolution_add_fusion = f32[4096,128]{1,0:T(8,128)} fusion(f32[4096,128]{1,0:T(8,128)S(1)} %fusion.46, f32[4096,64]{0,1:T(8,128)} %collective-permute-done.6, s32[128]{0:T(128)S(1)} %add_reduce_fusion.1, pred[128]{0:T(512)(128)(4,1)S(1)} %get-tuple-element.90), kind=kOutput, calls=%fused_computation.1 | convolution fusion | flops 403193856 | bytes 5243520 | tf_op jit(solution)/shard_map/dot_general | solution.py:153
  222.6 95.5 %all-to-all-done.1 = f32[1,128,32,128]{3,2,0,1:T(8,128)} async-done(((f32[1,128,32,128]{3,2,0,1:T(8,128)}), f32[1,128,32,128]{3,2,0,1:T(8,128)}, u32[]{:S(2)}, u32[]{:S(2)}) %all-to-all-start.1) | async-done | bytes 2097184 | tf_op jit(solution)/shard_map/all_to_all | solution.py:151
  318.1 1.9 copy.112
  320.9 4.9 %fusion.6 = f32[1,16,256,128]{3,2,1,0:T(8,128)} fusion(f32[1,16,256,128]{3,2,1,0:T(8,128)S(1)} %copy-done, f32[1,16,8,32,128]{4,3,2,1,0:T(8,128)S(1)} %copy.112, f32[1,16,255,128]{3,2,1,0:T(8,128)} %get-tuple-element.18, f32[1,16,255,128]{3,2,1,0:T(8,128)S(1)} %copy-done.2, f32[1,16,256,128]{3,2,1,0:T(8,128)S(1)} %bitcast.198, f32[16,128]{1,0:T(8,128)S(1)} %copy-done.3, ...), kind=kLoop, calls=%fused_computation.11 | loop fusion | flops 6815744 | bytes 12577360 | tf_op jit(solution)/shard_map/add | solution.py:170
  (135 shorter events, 75.3 us)
Async XLA Ops:
  0.0 7.5 %copy-start = (f32[1,16,256,128]{3,2,1,0:T(8,128)S(1)}, f32[1,16,256,128]{3,2,1,0:T(8,128)}, u32[]{:S(2)}) copy-start(f32[1,16,256,128]{3,2,1,0:T(8,128)} %param.7) | copy-start | bytes 6291460
  0.8 6.7 %copy-start.4 = (pred[128]{0:T(512)(128)(4,1)}, pred[128]{0:T(512)(128)(4,1)S(1)}, u32[]{:S(2)}) copy-start(pred[128]{0:T(512)(128)(4,1)S(1)} %get-tuple-element.87) | copy-start | bytes 388
  5.2 60.4 %collective-permute-start.6 = (f32[4096,64]{0,1:T(8,128)}, f32[4096,64]{0,1:T(8,128)}, u32[]{:S(2)}, u32[]{:S(2)}) collective-permute-start(f32[4096,64]{0,1:T(8,128)} %convolution_bitcast_fusion.2), channel_id=1, source_target_pairs={{0,8},{8,16},{16,24},{24,32},{32,40},{40,48},{48,56},{56,64},{64,7... | collective-permute-start | bytes 3145736 | tf_op jit(solution)/shard_map/ppermute | solution.py:117
  7.5 33.8 %copy-start.8 = (s32[1,256]{1,0:T(1,128)S(1)}, s32[1,256]{1,0:T(1,128)}, u32[]{:S(2)}) copy-start(s32[1,256]{1,0:T(1,128)} %param.8) | copy-start | bytes 3076
  7.5 33.8 %copy-start.9 = (f32[6]{0:T(128)S(1)}, f32[6]{0:T(128)}, u32[]{:S(2)}) copy-start(f32[6]{0:T(128)} %param.10) | copy-start | bytes 76
  7.6 33.8 %copy-start.10 = (f32[6]{0:T(128)S(1)}, f32[6]{0:T(128)}, u32[]{:S(2)}) copy-start(f32[6]{0:T(128)} %param.9) | copy-start | bytes 76
  9.9 55.6 %collective-permute-start.7 = (f32[4096,64]{0,1:T(8,128)}, f32[4096,64]{0,1:T(8,128)S(1)}, u32[]{:S(2)}, u32[]{:S(2)}) collective-permute-start(f32[4096,64]{0,1:T(8,128)} %convolution_bitcast_fusion.1), channel_id=1, source_target_pairs={{8,0},{16,8},{24,16},{32,24},{40,32},{48,40},{56,48},{64,56},{72,6... | collective-permute-start | bytes 3145736 | tf_op jit(solution)/shard_map/ppermute | solution.py:118
  15.9 5.5 %collective-permute-start = (f32[1,256]{1,0:T(1,128)S(1)}, f32[1,256]{1,0:T(1,128)S(1)}, u32[]{:S(2)}, u32[]{:S(2)}) collective-permute-start(f32[1,256]{1,0:T(1,128)S(1)} %bitcast.221), channel_id=1, source_target_pairs={{0,1},{1,0},{2,3},{3,2},{4,5},{5,4},{6,7},{7,6},{8,9},{9,8},{10,11... | collective-permute-start | bytes 3080 | tf_op jit(solution)/shard_map/ppermute | solution.py:63
  21.3 7.0 %collective-permute-start.1 = (f32[1,256]{1,0:T(1,128)S(1)}, f32[1,256]{1,0:T(1,128)S(1)}, u32[]{:S(2)}, u32[]{:S(2)}) collective-permute-start(f32[1,256]{1,0:T(1,128)S(1)} %add.160), channel_id=1, source_target_pairs={{0,2},{1,3},{2,0},{3,1},{4,6},{5,7},{6,4},{7,5},{8,10},{9,11},{10,... | collective-permute-start | bytes 3080 | tf_op jit(solution)/shard_map/ppermute | solution.py:63
  28.3 14.6 %collective-permute-start.2 = (f32[1,256]{1,0:T(1,128)S(1)}, f32[1,256]{1,0:T(1,128)S(1)}, u32[]{:S(2)}, u32[]{:S(2)}) collective-permute-start(f32[1,256]{1,0:T(1,128)S(1)} %add.161), channel_id=1, source_target_pairs={{0,4},{1,5},{2,6},{3,7},{4,0},{5,1},{6,2},{7,3},{8,12},{9,13},{10,... | collective-permute-start | bytes 3080 | tf_op jit(solution)/shard_map/ppermute | solution.py:63
  43.4 5.5 %collective-permute-start.3 = (f32[1,256]{1,0:T(1,128)S(1)}, f32[1,256]{1,0:T(1,128)S(1)}, u32[]{:S(2)}, u32[]{:S(2)}) collective-permute-start(f32[1,256]{1,0:T(1,128)S(1)} %get-tuple-element.15), channel_id=1, source_target_pairs={{0,64},{8,72},{16,80},{24,88},{32,96},{40,104},{48,112},{56,120},{... | collective-permute-start | bytes 3080 | tf_op jit(solution)/shard_map/ppermute | solution.py:72
  48.9 6.4 %collective-permute-start.4 = (f32[2,256]{1,0:T(2,128)S(1)}, f32[2,256]{1,0:T(2,128)S(1)}, u32[]{:S(2)}, u32[]{:S(2)}) collective-permute-start(f32[2,256]{1,0:T(2,128)S(1)} %maximum_select_fusion.5), channel_id=1, source_target_pairs={{0,128},{8,136},{16,144},{24,152},{32,160},{40,168},{48,176},{56,1... | collective-permute-start | bytes 6152 | tf_op jit(solution)/shard_map/ppermute | solution.py:72
  55.3 10.3 %collective-permute-start.5 = (f32[4,256]{1,0:T(4,128)S(1)}, f32[4,256]{1,0:T(4,128)S(1)}, u32[]{:S(2)}, u32[]{:S(2)}) collective-permute-start(f32[4,256]{1,0:T(4,128)S(1)} %maximum_select_fusion.4), channel_id=1, source_target_pairs={{0,256},{8,264},{16,272},{24,280},{32,288},{40,296},{48,304},{56,3... | collective-permute-start | bytes 12296 | tf_op jit(solution)/shard_map/ppermute | solution.py:72
  68.1 120.6 %all-to-all-start = ((f32[1,16,256,128]{3,1,0,2:T(8,128)}), f32[1,16,256,128]{3,1,0,2:T(8,128)}, u32[]{:S(2)}, u32[]{:S(2)}) async-start(f32[1,16,256,128]{3,1,0,2:T(8,128)} %copy.44), calls=%async_computation | async-start | bytes 4194304 | tf_op jit(solution)/shard_map/all_to_all | solution.py:136
  83.4 3.1 collective-permute-start.8
  86.5 5.6 %collective-permute-start.9 = (f32[16,256]{1,0:T(8,128)S(1)}, f32[16,256]{1,0:T(8,128)S(1)}, u32[]{:S(2)}, u32[]{:S(2)}) collective-permute-start(f32[16,256]{1,0:T(8,128)S(1)} %maximum_select_fusion.2), channel_id=1, source_target_pairs={{0,16},{8,24},{16,0},{24,8},{32,48},{40,56},{48,32},{56,40},{64,80... | collective-permute-start | bytes 49160 | tf_op jit(solution)/shard_map/ppermute | solution.py:72
  92.1 7.3 %collective-permute-start.10 = (f32[32,256]{1,0:T(8,128)S(1)}, f32[32,256]{1,0:T(8,128)S(1)}, u32[]{:S(2)}, u32[]{:S(2)}) collective-permute-start(f32[32,256]{1,0:T(8,128)S(1)} %maximum_select_fusion.1), channel_id=1, source_target_pairs={{0,32},{8,40},{16,48},{24,56},{32,0},{40,8},{48,16},{56,24},{64,96... | collective-permute-start | bytes 98312 | tf_op jit(solution)/shard_map/ppermute | solution.py:72
  199.2 14.6 %copy-start.11 = (f32[128]{0:T(128)S(1)}, f32[128]{0:T(128)}, u32[]{:S(2)}) copy-start(f32[128]{0:T(128)} %param.12) | copy-start | bytes 1540
  199.2 118.9 %all-to-all-start.1 = ((f32[1,128,32,128]{3,2,0,1:T(8,128)}), f32[1,128,32,128]{3,2,0,1:T(8,128)}, u32[]{:S(2)}, u32[]{:S(2)}) async-start(f32[1,128,32,128]{3,2,0,1:T(8,128)} %copy.111), calls=%async_computation.1 | async-start | bytes 4194304 | tf_op jit(solution)/shard_map/all_to_all | solution.py:151
  213.8 2.4 copy-start.5
  318.1 2.2 copy-start.1
  318.1 2.9 copy-start.2
  318.1 2.9 copy-start.3
  318.1 2.9 copy-start.6
  318.1 2.9 copy-start.7

commit v4 on v3

--- a/solution.py
+++ b/solution.py
@@ -37,14 +37,19 @@
 
 def own_differences(potential, modes, first_col, local_cols):
     half_count = modes // 2
-    padded = jnp.pad(potential, ((0, 0), (half_count, half_count)))
-    window = lax.dynamic_slice_in_dim(padded, first_col, local_cols + 2 * half_count, 1)
-    pieces = []
-    for offset in range(1, half_count + 1):
-        ahead_vals = window[:, half_count + offset : half_count + offset + local_cols]
-        behind = window[:, half_count - offset : half_count - offset + local_cols]
-        pieces.append(ahead_vals - behind)
-    return COUPLING * jnp.stack(pieces, axis=1)
+    col_count = potential.shape[1]
+    source = jnp.arange(col_count, dtype=jnp.int32)[:, None, None]
+    shift = jnp.arange(1, half_count + 1, dtype=jnp.int32)[None, :, None]
+    column = first_col + jnp.arange(local_cols, dtype=jnp.int32)[None, None, :]
+    select = (source == column + shift).astype(jnp.float32) - (source == column - shift).astype(
+        jnp.float32
+    )
+    picked = jnp.dot(
+        potential,
+        select.reshape(col_count, half_count * local_cols),
+        precision=lax.Precision.HIGHEST,
+    )
+    return COUPLING * picked.reshape(potential.shape[0], half_count, local_cols)
 
 
 def lookup(region, values_table):

time: 327 us -> 287 us (0.88)
  local copies, waits for them, and re-layouts: 85.8 us -> 13.7 us
  waiting for transfers between devices: 117 us -> 165 us
  other arithmetic: 22.5 us -> 11.6 us
  starting transfers between devices: 76.8 us -> 66.9 us
  matrix products: 23.1 us -> 28.3 us
    all_to_all x1, waiting for transfers between devices: 0.01 us -> 103 us  [shards(): spread = lax.all_to_all(held, 'ky', split_axis=2, concat_axis=1, tiled=True)]
    another operation x67 -> x2, local copies, waits for them, and re-layouts: 72.4 us -> 0.23 us  [the longest x65 72.1 us: own_differences(): return COUPLING * jnp.stack(pieces, axis=1)]
    all_to_all x1, waiting for transfers between devices: 95.5 us -> 40.3 us  [shards(): lax.all_to_all(mixed, 'ky', split_axis=1, concat_axis=2, tiled=True)]
    another operation x18 -> x2, other arithmetic: 11.1 us -> 0.34 us  [the longest x16 10.7 us: own_differences(): return COUPLING * jnp.stack(pieces, axis=1)]
    all_to_all x1, starting transfers between devices: 14.6 us -> 4.67 us  [shards(): lax.all_to_all(mixed, 'ky', split_axis=1, concat_axis=2, tiled=True)]
    dot_general x0 -> x1, matrix products: none -> 5.26 us  [own_differences(): jnp.dot(potential, select.reshape(col_count, half_count * local_cols), pr...]
  transfers between devices with their start and end apart: 13 -> 13, of which waited for: 10 -> 11; matrix products, arithmetic and copies ran while one was open for 32% -> 10% of each run, Pallas kernels for 0% -> 0%
where the time goes in v4:
time: 287 us; the launch traced here: 286 us
  waiting for transfers between devices  165 us (57%)
  starting transfers between devices  66.9 us (23%)
  matrix products  28.3 us (10%)
  local copies, waits for them, and re-layouts  13.7 us (5%)
  other arithmetic  11.6 us (4%)
    all_to_all x1, waiting for transfers between devices, shards(): spread = lax.all_to_all(held, 'ky', split_axis=2, concat_axis=1, tiled=True)  103 us
    all_to_all x1, waiting for transfers between devices, shards(): lax.all_to_all(mixed, 'ky', split_axis=1, concat_axis=2, tiled=True)  40.3 us
    ppermute x6, starting transfers between devices, gather_rows(): other = lax.ppermute(value, axis, xor_pairs(count, bit))  21.8 us
    ppermute x3, starting transfers between devices, sum_over(): value = value + lax.ppermute(value, axis, xor_pairs(count, bit))  18.8 us
    ppermute x6, waiting for transfers between devices, gather_rows(): other = lax.ppermute(value, axis, xor_pairs(count, bit))  14.5 us
    all_to_all x1, starting transfers between devices, shards(): spread = lax.all_to_all(held, 'ky', split_axis=2, concat_axis=1, tiled=True)  14 us
    ppermute x3, waiting for transfers between devices, sum_over(): value = value + lax.ppermute(value, axis, xor_pairs(count, bit))  7.46 us
  transfers between devices with their start and end apart: 13, of which 11 were waited for; matrix products, arithmetic and copies ran while one was open for 10% of the time, Pallas kernels for 0%

profile of v4, /device:TPU:120, one launch (start us, length us, event | category | flops | bytes accessed | tf_op | source)
XLA Modules:
  0.0 286.1 jit_solution(13367047954814977394)
XLA Ops:
  0.0 0.8 fusion.105
  1.2 4.0 %convolution_bitcast_fusion.2 = f32[4096,64]{0,1:T(8,128)} fusion(f32[4096,128]{1,0:T(8,128)} %bitcast.75, s32[128]{0:T(128)S(1)} %add_reduce_fusion.1, pred[128]{0:T(512)(128)(4,1)S(1)} %get-tuple-element.28), kind=kOutput, calls=%fused_computation.5 | convolution fusion | flops 402677760 | bytes 3146368 | tf_op jit(solution)/shard_map/dot_general | solution.py:118
  5.2 1.9 collective-permute-start.6
  7.5 2.4 convolution_bitcast_fusion.1
  9.9 5.7 %collective-permute-start.7 = (f32[4096,64]{0,1:T(8,128)}, f32[4096,64]{0,1:T(8,128)S(1)}, u32[]{:S(2)}, u32[]{:S(2)}) collective-permute-start(f32[4096,64]{0,1:T(8,128)} %convolution_bitcast_fusion.1), channel_id=1, source_target_pairs={{8,0},{16,8},{24,16},{32,24},{40,32},{48,40},{56,48},{64,56},{72,6... | collective-permute-start | bytes 3145736 | tf_op jit(solution)/shard_map/ppermute | solution.py:123
  15.8 2.7 collective-permute-start
  18.5 2.8 collective-permute-done
  21.3 3.1 %collective-permute-start.1 = (f32[1,256]{1,0:T(1,128)S(1)}, f32[1,256]{1,0:T(1,128)S(1)}, u32[]{:S(2)}, u32[]{:S(2)}) collective-permute-start(f32[1,256]{1,0:T(1,128)S(1)} %add.196), channel_id=1, source_target_pairs={{0,2},{1,3},{2,0},{3,1},{4,6},{5,7},{6,4},{7,5},{8,10},{9,11},{10,... | collective-permute-start | bytes 3080 | tf_op jit(solution)/shard_map/ppermute | solution.py:68
  24.4 3.8 %collective-permute-done.1 = f32[1,256]{1,0:T(1,128)S(1)} collective-permute-done((f32[1,256]{1,0:T(1,128)S(1)}, f32[1,256]{1,0:T(1,128)S(1)}, u32[]{:S(2)}, u32[]{:S(2)}) %collective-permute-start.1) | collective-permute-done | bytes 1056 | tf_op jit(solution)/shard_map/ppermute | solution.py:68
  28.2 13.0 %collective-permute-start.2 = (f32[1,256]{1,0:T(1,128)S(1)}, f32[1,256]{1,0:T(1,128)S(1)}, u32[]{:S(2)}, u32[]{:S(2)}) collective-permute-start(f32[1,256]{1,0:T(1,128)S(1)} %add.197), channel_id=1, source_target_pairs={{0,4},{1,5},{2,6},{3,7},{4,0},{5,1},{6,2},{7,3},{8,12},{9,13},{10,... | collective-permute-start | bytes 3080 | tf_op jit(solution)/shard_map/ppermute | solution.py:68
  41.3 0.7 fusion.85
  42.0 0.8 collective-permute-done.2
  43.3 2.9 %collective-permute-start.3 = (f32[1,256]{1,0:T(1,128)S(1)}, f32[1,256]{1,0:T(1,128)S(1)}, u32[]{:S(2)}, u32[]{:S(2)}) collective-permute-start(f32[1,256]{1,0:T(1,128)S(1)} %get-tuple-element.15), channel_id=1, source_target_pairs={{0,64},{8,72},{16,80},{24,88},{32,96},{40,104},{48,112},{56,120},{... | collective-permute-start | bytes 3080 | tf_op jit(solution)/shard_map/ppermute | solution.py:77
  46.3 2.5 collective-permute-done.3
  48.8 3.4 %collective-permute-start.4 = (f32[2,256]{1,0:T(2,128)S(1)}, f32[2,256]{1,0:T(2,128)S(1)}, u32[]{:S(2)}, u32[]{:S(2)}) collective-permute-start(f32[2,256]{1,0:T(2,128)S(1)} %maximum_select_fusion.5), channel_id=1, source_target_pairs={{0,128},{8,136},{16,144},{24,152},{32,160},{40,168},{48,176},{56,1... | collective-permute-start | bytes 6152 | tf_op jit(solution)/shard_map/ppermute | solution.py:77
  52.2 3.0 %collective-permute-done.4 = f32[2,256]{1,0:T(2,128)S(1)} collective-permute-done((f32[2,256]{1,0:T(2,128)S(1)}, f32[2,256]{1,0:T(2,128)S(1)}, u32[]{:S(2)}, u32[]{:S(2)}) %collective-permute-start.4) | collective-permute-done | bytes 2080 | tf_op jit(solution)/shard_map/ppermute | solution.py:77
  55.2 8.7 %collective-permute-start.5 = (f32[4,256]{1,0:T(4,128)S(1)}, f32[4,256]{1,0:T(4,128)S(1)}, u32[]{:S(2)}, u32[]{:S(2)}) collective-permute-start(f32[4,256]{1,0:T(4,128)S(1)} %maximum_select_fusion.4), channel_id=1, source_target_pairs={{0,256},{8,264},{16,272},{24,280},{32,288},{40,296},{48,304},{56,3... | collective-permute-start | bytes 12296 | tf_op jit(solution)/shard_map/ppermute | solution.py:77
  63.9 1.6 collective-permute-done.5
  65.5 2.5 copy.30
  68.0 14.0 %all-to-all-start = ((f32[1,16,256,128]{3,1,0,2:T(8,128)}), f32[1,16,256,128]{3,1,0,2:T(8,128)}, u32[]{:S(2)}, u32[]{:S(2)}) async-start(f32[1,16,256,128]{3,1,0,2:T(8,128)} %copy.30), calls=%async_computation | async-start | bytes 4194304 | tf_op jit(solution)/shard_map/all_to_all | solution.py:141
  82.0 0.8 fusion.61
  83.0 0.7 broadcast_add_fusion
  84.0 1.9 collective-permute-start.8
  86.0 0.6 iota_add_fusion
  86.5 0.6 collective-permute-done.8
  87.1 1.9 collective-permute-start.9
  89.0 0.6 multiply_multiply_fusion
  89.6 3.1 %collective-permute-done.9 = f32[16,256]{1,0:T(8,128)S(1)} collective-permute-done((f32[16,256]{1,0:T(8,128)S(1)}, f32[16,256]{1,0:T(8,128)S(1)}, u32[]{:S(2)}, u32[]{:S(2)}) %collective-permute-start.9) | collective-permute-done | bytes 16416 | tf_op jit(solution)/shard_map/ppermute | solution.py:77
  92.7 3.0 %collective-permute-start.10 = (f32[32,256]{1,0:T(8,128)S(1)}, f32[32,256]{1,0:T(8,128)S(1)}, u32[]{:S(2)}, u32[]{:S(2)}) collective-permute-start(f32[32,256]{1,0:T(8,128)S(1)} %maximum_select_fusion.1), channel_id=1, source_target_pairs={{0,32},{8,40},{16,48},{24,56},{32,0},{40,8},{48,16},{56,24},{64,96... | collective-permute-start | bytes 98312 | tf_op jit(solution)/shard_map/ppermute | solution.py:77
  95.7 0.6 multiply_multiply_fusion.1
  96.3 3.8 %collective-permute-done.10 = f32[32,256]{1,0:T(8,128)S(1)} collective-permute-done((f32[32,256]{1,0:T(8,128)S(1)}, f32[32,256]{1,0:T(8,128)S(1)}, u32[]{:S(2)}, u32[]{:S(2)}) %collective-permute-start.10) | collective-permute-done | bytes 32800 | tf_op jit(solution)/shard_map/ppermute | solution.py:77
  100.6 2.1 convolution_divide_fusion
  102.7 2.1 fusion.20
  104.8 0.8 fusion.86
  105.6 5.3 %fusion.7 = f32[1,64,32]{2,0,1:T(1,128)S(1)} fusion(f32[256,1,1]{0,1,2:T(1,128)S(1)} %bitcast.87, s32[64,32]{1,0:T(8,128)} %get-tuple-element.20, s32[64,32]{1,0:T(8,128)} %get-tuple-element.19), kind=kOutput, calls=%fused_computation.12 | convolution fusion | flops 8912896 | bytes 25600 | tf_op jit(solution)/shard_map/dot_general | solution.py:47
  111.0 103.0 %all-to-all-done = f32[1,16,256,128]{3,1,0,2:T(8,128)} async-done(((f32[1,16,256,128]{3,1,0,2:T(8,128)}), f32[1,16,256,128]{3,1,0,2:T(8,128)}, u32[]{:S(2)}, u32[]{:S(2)}) %all-to-all-start) | async-done | bytes 2097184 | tf_op jit(solution)/shard_map/all_to_all | solution.py:141
  214.0 2.2 copy.31
  216.4 2.6 fusion.1
  219.0 2.4 fusion.41
  221.4 3.1 %copy.33 = f32[1,128,32,128]{3,2,0,1:T(8,128)} copy(f32[1,128,32,128]{1,3,2,0:T(8,128)} %bitcast.80) | data formatting | bytes 4194304 | tf_op jit(solution)/shard_map/reshape | solution.py:155
  224.6 4.7 %all-to-all-start.1 = ((f32[1,128,32,128]{3,2,0,1:T(8,128)}), f32[1,128,32,128]{3,2,0,1:T(8,128)}, u32[]{:S(2)}, u32[]{:S(2)}) async-start(f32[1,128,32,128]{3,2,0,1:T(8,128)} %copy.33), calls=%async_computation.1 | async-start | bytes 4194304 | tf_op jit(solution)/shard_map/all_to_all | solution.py:156
  229.3 2.4 fusion.107
  231.7 1.9 fusion.52
  233.6 4.5 %convolution_add_fusion = f32[4096,128]{1,0:T(8,128)} fusion(f32[4096,128]{1,0:T(8,128)S(1)} %fusion.52, f32[4096,64]{0,1:T(8,128)} %collective-permute-done.6, s32[128]{0:T(128)S(1)} %add_reduce_fusion.1, pred[128]{0:T(512)(128)(4,1)S(1)} %get-tuple-element.28), kind=kOutput, calls=%fused_computation.1 | convolution fusion | flops 403193856 | bytes 5243520 | tf_op jit(solution)/shard_map/dot_general | solution.py:158
  238.0 40.3 %all-to-all-done.1 = f32[1,128,32,128]{3,2,0,1:T(8,128)} async-done(((f32[1,128,32,128]{3,2,0,1:T(8,128)}), f32[1,128,32,128]{3,2,0,1:T(8,128)}, u32[]{:S(2)}, u32[]{:S(2)}) %all-to-all-start.1) | async-done | bytes 2097184 | tf_op jit(solution)/shard_map/all_to_all | solution.py:156
  278.3 1.9 copy.34
  280.5 0.6 copy-done.2
  281.2 4.9 %fusion.6 = f32[1,16,256,128]{3,2,1,0:T(8,128)} fusion(f32[1,16,256,128]{3,2,1,0:T(8,128)S(1)} %copy-done, f32[1,16,8,32,128]{4,3,2,1,0:T(8,128)S(1)} %copy.34, f32[1,16,255,128]{3,2,1,0:T(8,128)} %get-tuple-element.18, f32[1,16,255,128]{3,2,1,0:T(8,128)S(1)} %copy-done.2, f32[1,16,256,128]{3,2,1,0:T(8,128)S(1)} %bitcast.77, f32[16,128]{1,0:T(8,128)S(1)} %copy-done.3, ...), kind=kLoop, calls=%fused_computation.11 | loop fusion | flops 6815744 | bytes 12577360 | tf_op jit(solution)/shard_map/add | solution.py:175
  (58 shorter events, 3.2 us)
Async XLA Ops:
  0.0 7.5 %copy-start = (f32[1,16,256,128]{3,2,1,0:T(8,128)S(1)}, f32[1,16,256,128]{3,2,1,0:T(8,128)}, u32[]{:S(2)}) copy-start(f32[1,16,256,128]{3,2,1,0:T(8,128)} %param.7) | copy-start | bytes 6291460
  0.8 6.7 %copy-start.4 = (pred[128]{0:T(512)(128)(4,1)}, pred[128]{0:T(512)(128)(4,1)S(1)}, u32[]{:S(2)}) copy-start(pred[128]{0:T(512)(128)(4,1)S(1)} %get-tuple-element.25) | copy-start | bytes 388
  5.2 60.3 %collective-permute-start.6 = (f32[4096,64]{0,1:T(8,128)}, f32[4096,64]{0,1:T(8,128)}, u32[]{:S(2)}, u32[]{:S(2)}) collective-permute-start(f32[4096,64]{0,1:T(8,128)} %convolution_bitcast_fusion.2), channel_id=1, source_target_pairs={{0,8},{8,16},{16,24},{24,32},{32,40},{40,48},{48,56},{56,64},{64,7... | collective-permute-start | bytes 3145736 | tf_op jit(solution)/shard_map/ppermute | solution.py:122
  7.5 33.8 %copy-start.8 = (s32[1,256]{1,0:T(1,128)S(1)}, s32[1,256]{1,0:T(1,128)}, u32[]{:S(2)}) copy-start(s32[1,256]{1,0:T(1,128)} %param.8) | copy-start | bytes 3076
  7.5 33.8 %copy-start.9 = (f32[6]{0:T(128)S(1)}, f32[6]{0:T(128)}, u32[]{:S(2)}) copy-start(f32[6]{0:T(128)} %param.10) | copy-start | bytes 76
  7.5 33.8 %copy-start.10 = (f32[6]{0:T(128)S(1)}, f32[6]{0:T(128)}, u32[]{:S(2)}) copy-start(f32[6]{0:T(128)} %param.9) | copy-start | bytes 76
  9.9 55.6 %collective-permute-start.7 = (f32[4096,64]{0,1:T(8,128)}, f32[4096,64]{0,1:T(8,128)S(1)}, u32[]{:S(2)}, u32[]{:S(2)}) collective-permute-start(f32[4096,64]{0,1:T(8,128)} %convolution_bitcast_fusion.1), channel_id=1, source_target_pairs={{8,0},{16,8},{24,16},{32,24},{40,32},{48,40},{56,48},{64,56},{72,6... | collective-permute-start | bytes 3145736 | tf_op jit(solution)/shard_map/ppermute | solution.py:123
  15.8 5.5 %collective-permute-start = (f32[1,256]{1,0:T(1,128)S(1)}, f32[1,256]{1,0:T(1,128)S(1)}, u32[]{:S(2)}, u32[]{:S(2)}) collective-permute-start(f32[1,256]{1,0:T(1,128)S(1)} %bitcast.84), channel_id=1, source_target_pairs={{0,1},{1,0},{2,3},{3,2},{4,5},{5,4},{6,7},{7,6},{8,9},{9,8},{10,11... | collective-permute-start | bytes 3080 | tf_op jit(solution)/shard_map/ppermute | solution.py:68
  21.3 7.0 %collective-permute-start.1 = (f32[1,256]{1,0:T(1,128)S(1)}, f32[1,256]{1,0:T(1,128)S(1)}, u32[]{:S(2)}, u32[]{:S(2)}) collective-permute-start(f32[1,256]{1,0:T(1,128)S(1)} %add.196), channel_id=1, source_target_pairs={{0,2},{1,3},{2,0},{3,1},{4,6},{5,7},{6,4},{7,5},{8,10},{9,11},{10,... | collective-permute-start | bytes 3080 | tf_op jit(solution)/shard_map/ppermute | solution.py:68
  28.2 14.6 %collective-permute-start.2 = (f32[1,256]{1,0:T(1,128)S(1)}, f32[1,256]{1,0:T(1,128)S(1)}, u32[]{:S(2)}, u32[]{:S(2)}) collective-permute-start(f32[1,256]{1,0:T(1,128)S(1)} %add.197), channel_id=1, source_target_pairs={{0,4},{1,5},{2,6},{3,7},{4,0},{5,1},{6,2},{7,3},{8,12},{9,13},{10,... | collective-permute-start | bytes 3080 | tf_op jit(solution)/shard_map/ppermute | solution.py:68
  43.3 5.5 %collective-permute-start.3 = (f32[1,256]{1,0:T(1,128)S(1)}, f32[1,256]{1,0:T(1,128)S(1)}, u32[]{:S(2)}, u32[]{:S(2)}) collective-permute-start(f32[1,256]{1,0:T(1,128)S(1)} %get-tuple-element.15), channel_id=1, source_target_pairs={{0,64},{8,72},{16,80},{24,88},{32,96},{40,104},{48,112},{56,120},{... | collective-permute-start | bytes 3080 | tf_op jit(solution)/shard_map/ppermute | solution.py:77
  48.8 6.4 %collective-permute-start.4 = (f32[2,256]{1,0:T(2,128)S(1)}, f32[2,256]{1,0:T(2,128)S(1)}, u32[]{:S(2)}, u32[]{:S(2)}) collective-permute-start(f32[2,256]{1,0:T(2,128)S(1)} %maximum_select_fusion.5), channel_id=1, source_target_pairs={{0,128},{8,136},{16,144},{24,152},{32,160},{40,168},{48,176},{56,1... | collective-permute-start | bytes 6152 | tf_op jit(solution)/shard_map/ppermute | solution.py:77
  55.2 10.3 %collective-permute-start.5 = (f32[4,256]{1,0:T(4,128)S(1)}, f32[4,256]{1,0:T(4,128)S(1)}, u32[]{:S(2)}, u32[]{:S(2)}) collective-permute-start(f32[4,256]{1,0:T(4,128)S(1)} %maximum_select_fusion.4), channel_id=1, source_target_pairs={{0,256},{8,264},{16,272},{24,280},{32,288},{40,296},{48,304},{56,3... | collective-permute-start | bytes 12296 | tf_op jit(solution)/shard_map/ppermute | solution.py:77
  68.0 146.0 %all-to-all-start = ((f32[1,16,256,128]{3,1,0,2:T(8,128)}), f32[1,16,256,128]{3,1,0,2:T(8,128)}, u32[]{:S(2)}, u32[]{:S(2)}) async-start(f32[1,16,256,128]{3,1,0,2:T(8,128)} %copy.30), calls=%async_computation | async-start | bytes 4194304 | tf_op jit(solution)/shard_map/all_to_all | solution.py:141
  84.0 3.1 %collective-permute-start.8 = (f32[8,256]{1,0:T(8,128)S(1)}, f32[8,256]{1,0:T(8,128)S(1)}, u32[]{:S(2)}, u32[]{:S(2)}) collective-permute-start(f32[8,256]{1,0:T(8,128)S(1)} %maximum_select_fusion.3), channel_id=1, source_target_pairs={{0,8},{8,0},{16,24},{24,16},{32,40},{40,32},{48,56},{56,48},{64,72... | collective-permute-start | bytes 24584 | tf_op jit(solution)/shard_map/ppermute | solution.py:77
  87.1 5.6 %collective-permute-start.9 = (f32[16,256]{1,0:T(8,128)S(1)}, f32[16,256]{1,0:T(8,128)S(1)}, u32[]{:S(2)}, u32[]{:S(2)}) collective-permute-start(f32[16,256]{1,0:T(8,128)S(1)} %maximum_select_fusion.2), channel_id=1, source_target_pairs={{0,16},{8,24},{16,0},{24,8},{32,48},{40,56},{48,32},{56,40},{64,80... | collective-permute-start | bytes 49160 | tf_op jit(solution)/shard_map/ppermute | solution.py:77
  92.7 7.3 %collective-permute-start.10 = (f32[32,256]{1,0:T(8,128)S(1)}, f32[32,256]{1,0:T(8,128)S(1)}, u32[]{:S(2)}, u32[]{:S(2)}) collective-permute-start(f32[32,256]{1,0:T(8,128)S(1)} %maximum_select_fusion.1), channel_id=1, source_target_pairs={{0,32},{8,40},{16,48},{24,56},{32,0},{40,8},{48,16},{56,24},{64,96... | collective-permute-start | bytes 98312 | tf_op jit(solution)/shard_map/ppermute | solution.py:77
  224.6 4.7 %copy-start.11 = (f32[128]{0:T(128)S(1)}, f32[128]{0:T(128)}, u32[]{:S(2)}) copy-start(f32[128]{0:T(128)} %param.12) | copy-start | bytes 1540
  224.6 53.7 %all-to-all-start.1 = ((f32[1,128,32,128]{3,2,0,1:T(8,128)}), f32[1,128,32,128]{3,2,0,1:T(8,128)}, u32[]{:S(2)}, u32[]{:S(2)}) async-start(f32[1,128,32,128]{3,2,0,1:T(8,128)} %copy.33), calls=%async_computation.1 | async-start | bytes 4194304 | tf_op jit(solution)/shard_map/all_to_all | solution.py:156
  229.3 2.4 copy-start.5
  278.3 2.2 copy-start.1
  278.3 2.9 copy-start.2
  278.3 2.9 copy-start.3
  278.3 2.9 copy-start.6
  278.3 2.9 copy-start.7

commit v5 on v4

--- a/solution.py
+++ b/solution.py
@@ -122,9 +122,6 @@
     got_left = lax.ppermute(send_right, "space", forward_pairs)
     got_right = lax.ppermute(send_left, "space", backward_pairs)
     far_rows = gather_rows(charge, "space", far_bits)
-    held, far_rows, got_left, got_right = lax.optimization_barrier(
-        (distribution, far_rows, got_left, got_right)
-    )
     every_row = gather_rows(far_rows, "space", near_bits)
     every_row = in_row_order(every_row, far_bits + near_bits, space_count * row_count)
 
@@ -138,7 +135,7 @@
     own_rows = lax.dynamic_slice_in_dim(sine_rows, row_start, row_count, 0)
     potential = POISSON * jnp.dot(own_rows, back_cols, precision=precise)
 
-    spread = lax.all_to_all(held, "ky", split_axis=2, concat_axis=1, tiled=True)
+    spread = lax.all_to_all(distribution, "ky", split_axis=2, concat_axis=1, tiled=True)
     local_cols = spread.shape[2]
     forward, backward = wigner_tables(ky_count)
     weights = own_differences(potential, ky_count, lax.axis_index("ky") * local_cols, local_cols)
@@ -153,6 +150,7 @@
         precision=triple,
     )
     mixed = mixed.reshape(row_count, ky_count, local_cols, kx_count)
+    mixed, got_left, got_right = lax.optimization_barrier((mixed, got_left, got_right))
     wigner = lax.all_to_all(mixed, "ky", split_axis=1, concat_axis=2, tiled=True)
 
     upstream_x = jnp.dot(got_left, pick_pos.T, precision=precise) + jnp.dot(

time: 287 us -> 318 us (1.11)
  the two profiles are of different devices: /device:TPU:120 before, /device:TPU:99 now
where the time goes in v5:
time: 318 us; the launch traced here: 317 us
  waiting for transfers between devices  180 us (57%)
  starting transfers between devices  78.7 us (25%)
  matrix products  27.1 us (9%)
  local copies, waits for them, and re-layouts  20.1 us (6%)
  other arithmetic  10.9 us (3%)
    all_to_all x1, waiting for transfers between devices, shards(): lax.all_to_all(mixed, 'ky', split_axis=1, concat_axis=2, tiled=True)  99.1 us
    ppermute x3, waiting for transfers between devices, sum_over(): value = value + lax.ppermute(value, axis, xor_pairs(count, bit))  67.9 us
    ppermute x6, starting transfers between devices, gather_rows(): other = lax.ppermute(value, axis, xor_pairs(count, bit))  30.3 us
    ppermute x3, starting transfers between devices, sum_over(): value = value + lax.ppermute(value, axis, xor_pairs(count, bit))  19.9 us
    all_to_all x1, starting transfers between devices, shards(): lax.all_to_all(distribution, 'ky', split_axis=2, concat_axis=1, tiled=True)  14.9 us
    ppermute x6, waiting for transfers between devices, gather_rows(): other = lax.ppermute(value, axis, xor_pairs(count, bit))  12.8 us
    all_to_all x1, starting transfers between devices, shards(): lax.all_to_all(mixed, 'ky', split_axis=1, concat_axis=2, tiled=True)  7.04 us
  transfers between devices with their start and end apart: 13, of which 9 were waited for; matrix products, arithmetic and copies ran while one was open for 14% of the time, Pallas kernels for 0%

profile of v5, /device:TPU:99, one launch (start us, length us, event | category | flops | bytes accessed | tf_op | source)
XLA Modules:
  0.0 317.1 jit_solution(17096878581126627119)
XLA Ops:
  0.0 4.1 %copy.29 = f32[1,16,256,128]{3,1,0,2:T(8,128)} copy(f32[1,16,256,128]{3,2,1,0:T(8,128)} %param.7) | data formatting | bytes 4194304 | tf_op args[0]
  4.1 14.9 %all-to-all-start = ((f32[1,16,256,128]{3,1,0,2:T(8,128)}), f32[1,16,256,128]{3,1,0,2:T(8,128)}, u32[]{:S(2)}, u32[]{:S(2)}) async-start(f32[1,16,256,128]{3,1,0,2:T(8,128)} %copy.29), calls=%async_computation | async-start | bytes 4194304 | tf_op jit(solution)/shard_map/all_to_all | solution.py:138
  19.2 3.4 %collective-permute-start = (f32[1,256]{1,0:T(1,128)S(1)}, f32[1,256]{1,0:T(1,128)S(1)}, u32[]{:S(2)}, u32[]{:S(2)}) collective-permute-start(f32[1,256]{1,0:T(1,128)S(1)} %bitcast.84), channel_id=1, source_target_pairs={{0,1},{1,0},{2,3},{3,2},{4,5},{5,4},{6,7},{7,6},{8,9},{9,8},{10,11... | collective-permute-start | bytes 3080 | tf_op jit(solution)/shard_map/ppermute | solution.py:68
  23.0 2.4 convolution_bitcast_fusion.2
  25.4 4.6 %collective-permute-start.9 = (f32[4096,64]{0,1:T(8,128)}, f32[4096,64]{0,1:T(8,128)}, u32[]{:S(2)}, u32[]{:S(2)}) collective-permute-start(f32[4096,64]{0,1:T(8,128)} %convolution_bitcast_fusion.2), channel_id=1, source_target_pairs={{0,8},{8,16},{16,24},{24,32},{32,40},{40,48},{48,56},{56,64},{64,7... | collective-permute-start | bytes 3145736 | tf_op jit(solution)/shard_map/ppermute | solution.py:122
  30.5 2.4 convolution_bitcast_fusion.1
  32.9 1.9 collective-permute-start.10
  35.1 4.3 %collective-permute-start.1 = (f32[1,256]{1,0:T(1,128)S(1)}, f32[1,256]{1,0:T(1,128)S(1)}, u32[]{:S(2)}, u32[]{:S(2)}) collective-permute-start(f32[1,256]{1,0:T(1,128)S(1)} %add.200), channel_id=1, source_target_pairs={{0,2},{1,3},{2,0},{3,1},{4,6},{5,7},{6,4},{7,5},{8,10},{9,11},{10,... | collective-permute-start | bytes 3080 | tf_op jit(solution)/shard_map/ppermute | solution.py:68
  39.4 0.7 fusion.85
  40.1 0.8 collective-permute-done.1
  40.9 12.2 %collective-permute-start.2 = (f32[1,256]{1,0:T(1,128)S(1)}, f32[1,256]{1,0:T(1,128)S(1)}, u32[]{:S(2)}, u32[]{:S(2)}) collective-permute-start(f32[1,256]{1,0:T(1,128)S(1)} %add.201), channel_id=1, source_target_pairs={{0,4},{1,5},{2,6},{3,7},{4,0},{5,1},{6,2},{7,3},{8,12},{9,13},{10,... | collective-permute-start | bytes 3080 | tf_op jit(solution)/shard_map/ppermute | solution.py:68
  53.1 67.1 %collective-permute-done.2 = f32[1,256]{1,0:T(1,128)S(1)} collective-permute-done((f32[1,256]{1,0:T(1,128)S(1)}, f32[1,256]{1,0:T(1,128)S(1)}, u32[]{:S(2)}, u32[]{:S(2)}) %collective-permute-start.2) | collective-permute-done | bytes 1056 | tf_op jit(solution)/shard_map/ppermute | solution.py:68
  120.2 0.6 fusion.106
  120.8 1.9 collective-permute-start.3
  122.7 0.7 broadcast_add_fusion
  123.4 1.7 collective-permute-done.3
  125.1 1.9 collective-permute-start.4
  127.2 3.1 collective-permute-done.4
  130.3 3.5 %collective-permute-start.5 = (f32[4,256]{1,0:T(4,128)S(1)}, f32[4,256]{1,0:T(4,128)S(1)}, u32[]{:S(2)}, u32[]{:S(2)}) collective-permute-start(f32[4,256]{1,0:T(4,128)S(1)} %maximum_select_fusion.4), channel_id=1, source_target_pairs={{0,256},{8,264},{16,272},{24,280},{32,288},{40,296},{48,304},{56,3... | collective-permute-start | bytes 12296 | tf_op jit(solution)/shard_map/ppermute | solution.py:77
  133.8 0.8 fusion.61
  134.6 3.9 %collective-permute-done.5 = f32[4,256]{1,0:T(4,128)S(1)} collective-permute-done((f32[4,256]{1,0:T(4,128)S(1)}, f32[4,256]{1,0:T(4,128)S(1)}, u32[]{:S(2)}, u32[]{:S(2)}) %collective-permute-start.5) | collective-permute-done | bytes 4128 | tf_op jit(solution)/shard_map/ppermute | solution.py:77
  138.6 7.6 %collective-permute-start.6 = (f32[8,256]{1,0:T(8,128)S(1)}, f32[8,256]{1,0:T(8,128)S(1)}, u32[]{:S(2)}, u32[]{:S(2)}) collective-permute-start(f32[8,256]{1,0:T(8,128)S(1)} %maximum_select_fusion.3), channel_id=1, source_target_pairs={{0,8},{8,0},{16,24},{24,16},{32,40},{40,32},{48,56},{56,48},{64,72... | collective-permute-start | bytes 24584 | tf_op jit(solution)/shard_map/ppermute | solution.py:77
  146.2 0.6 iota_add_fusion
  147.0 13.4 %collective-permute-start.7 = (f32[16,256]{1,0:T(8,128)S(1)}, f32[16,256]{1,0:T(8,128)S(1)}, u32[]{:S(2)}, u32[]{:S(2)}) collective-permute-start(f32[16,256]{1,0:T(8,128)S(1)} %maximum_select_fusion.2), channel_id=1, source_target_pairs={{0,16},{8,24},{16,0},{24,8},{32,48},{40,56},{48,32},{56,40},{64,80... | collective-permute-start | bytes 49160 | tf_op jit(solution)/shard_map/ppermute | solution.py:77
  160.3 0.6 multiply_multiply_fusion
  161.0 0.5 collective-permute-done.7
  161.5 2.1 collective-permute-start.8
  163.6 0.6 multiply_multiply_fusion.1
  164.2 3.4 %collective-permute-done.8 = f32[32,256]{1,0:T(8,128)S(1)} collective-permute-done((f32[32,256]{1,0:T(8,128)S(1)}, f32[32,256]{1,0:T(8,128)S(1)}, u32[]{:S(2)}, u32[]{:S(2)}) %collective-permute-start.8) | collective-permute-done | bytes 32800 | tf_op jit(solution)/shard_map/ppermute | solution.py:77
  167.8 0.4 fusion.82
  168.2 2.1 convolution_divide_fusion
  170.2 2.1 fusion.20
  172.3 0.8 fusion.86
  173.2 5.3 %fusion.7 = f32[1,64,32]{2,0,1:T(1,128)S(1)} fusion(f32[256,1,1]{0,1,2:T(1,128)S(1)} %bitcast.87, s32[64,32]{1,0:T(8,128)} %get-tuple-element.18, s32[64,32]{1,0:T(8,128)} %get-tuple-element.17), kind=kOutput, calls=%fused_computation.12 | convolution fusion | flops 8912896 | bytes 25600 | tf_op jit(solution)/shard_map/dot_general | solution.py:47
  178.7 1.9 mul.252
  180.6 2.8 mul.253
  183.4 2.4 copy.30
  185.8 2.2 fusion.1
  187.9 3.2 %fusion.41 = f32[4096,128]{1,0:T(8,128)} fusion(f32[128,4096]{1,0:T(8,128)S(1)} %fusion.1, f32[128,64]{1,0:T(8,128)S(1)} %get-tuple-element.24, f32[128,64]{1,0:T(8,128)S(1)} %get-tuple-element.23), kind=kOutput, calls=%fused_computation.53 | convolution fusion | flops 402669568 | bytes 4259840 | tf_op jit(solution)/shard_map/ab,rbm->ram/dot_general | solution.py:146
  191.2 3.2 copy.35
  194.3 7.0 %all-to-all-start.1 = ((f32[1,128,32,128]{3,2,0,1:T(8,128)}), f32[1,128,32,128]{3,2,0,1:T(8,128)}, u32[]{:S(2)}, u32[]{:S(2)}) async-start(f32[1,128,32,128]{3,2,0,1:T(8,128)} %copy.35), calls=%async_computation.1 | async-start | bytes 4194304 | tf_op jit(solution)/shard_map/all_to_all | solution.py:154
  201.4 2.4 fusion.107
  203.8 1.9 fusion.52
  205.7 4.5 %convolution_add_fusion = f32[4096,128]{1,0:T(8,128)} fusion(f32[4096,128]{1,0:T(8,128)S(1)} %fusion.52, f32[4096,64]{0,1:T(8,128)} %collective-permute-done.9, s32[128]{0:T(128)S(1)} %add_reduce_fusion.1, pred[128]{0:T(512)(128)(4,1)S(1)} %get-tuple-element.22), kind=kOutput, calls=%fused_computation | convolution fusion | flops 403193856 | bytes 5243520 | tf_op jit(solution)/shard_map/dot_general | solution.py:156
  210.2 99.1 %all-to-all-done.1 = f32[1,128,32,128]{3,2,0,1:T(8,128)} async-done(((f32[1,128,32,128]{3,2,0,1:T(8,128)}), f32[1,128,32,128]{3,2,0,1:T(8,128)}, u32[]{:S(2)}, u32[]{:S(2)}) %all-to-all-start.1) | async-done | bytes 2097184 | tf_op jit(solution)/shard_map/all_to_all | solution.py:154
  309.3 1.9 copy.36
  311.5 0.6 copy-done.3
  312.1 4.9 %fusion.6 = f32[1,16,256,128]{3,2,1,0:T(8,128)} fusion(f32[1,16,256,128]{3,2,1,0:T(8,128)S(1)} %copy-done, f32[1,16,8,32,128]{4,3,2,1,0:T(8,128)S(1)} %copy.36, f32[1,16,255,128]{3,2,1,0:T(8,128)} %get-tuple-element.16, f32[1,16,255,128]{3,2,1,0:T(8,128)S(1)} %copy-done.3, f32[1,16,256,128]{3,2,1,0:T(8,128)S(1)} %bitcast.78, f32[16,128]{1,0:T(8,128)S(1)} %copy-done.4, ...), kind=kLoop, calls=%fused_computation.11 | loop fusion | flops 6815744 | bytes 12577360 | tf_op jit(solution)/shard_map/add | solution.py:173
  (64 shorter events, 2.5 us)
Async XLA Ops:
  4.1 14.9 %copy-start = (f32[1,16,256,128]{3,2,1,0:T(8,128)S(1)}, f32[1,16,256,128]{3,2,1,0:T(8,128)}, u32[]{:S(2)}) copy-start(f32[1,16,256,128]{3,2,1,0:T(8,128)} %param.7) | copy-start | bytes 6291460
  4.1 179.3 %all-to-all-start = ((f32[1,16,256,128]{3,1,0,2:T(8,128)}), f32[1,16,256,128]{3,1,0,2:T(8,128)}, u32[]{:S(2)}, u32[]{:S(2)}) async-start(f32[1,16,256,128]{3,1,0,2:T(8,128)} %copy.29), calls=%async_computation | async-start | bytes 4194304 | tf_op jit(solution)/shard_map/all_to_all | solution.py:138
  19.0 3.6 %copy-start.10 = (s32[128]{0:T(128)S(1)}, s32[128]{0:T(128)}, u32[]{:S(2)}) copy-start(s32[128]{0:T(128)} %param.13) | copy-start | bytes 1540
  19.2 15.9 %collective-permute-start = (f32[1,256]{1,0:T(1,128)S(1)}, f32[1,256]{1,0:T(1,128)S(1)}, u32[]{:S(2)}, u32[]{:S(2)}) collective-permute-start(f32[1,256]{1,0:T(1,128)S(1)} %bitcast.84), channel_id=1, source_target_pairs={{0,1},{1,0},{2,3},{3,2},{4,5},{5,4},{6,7},{7,6},{8,9},{9,8},{10,11... | collective-permute-start | bytes 3080 | tf_op jit(solution)/shard_map/ppermute | solution.py:68
  22.6 7.9 %copy-start.5 = (pred[128]{0:T(512)(128)(4,1)}, pred[128]{0:T(512)(128)(4,1)S(1)}, u32[]{:S(2)}) copy-start(pred[128]{0:T(512)(128)(4,1)S(1)} %get-tuple-element.19) | copy-start | bytes 388
  25.4 14.0 %copy-start.9 = (s32[1,256]{1,0:T(1,128)S(1)}, s32[1,256]{1,0:T(1,128)}, u32[]{:S(2)}) copy-start(s32[1,256]{1,0:T(1,128)} %param.8) | copy-start | bytes 3076
  25.4 14.0 %copy-start.11 = (f32[6]{0:T(128)S(1)}, f32[6]{0:T(128)}, u32[]{:S(2)}) copy-start(f32[6]{0:T(128)} %param.10) | copy-start | bytes 76
  25.4 14.0 %copy-start.12 = (f32[6]{0:T(128)S(1)}, f32[6]{0:T(128)}, u32[]{:S(2)}) copy-start(f32[6]{0:T(128)} %param.9) | copy-start | bytes 76
  25.4 165.7 %collective-permute-start.9 = (f32[4096,64]{0,1:T(8,128)}, f32[4096,64]{0,1:T(8,128)}, u32[]{:S(2)}, u32[]{:S(2)}) collective-permute-start(f32[4096,64]{0,1:T(8,128)} %convolution_bitcast_fusion.2), channel_id=1, source_target_pairs={{0,8},{8,16},{16,24},{24,32},{32,40},{40,48},{48,56},{56,64},{64,7... | collective-permute-start | bytes 3145736 | tf_op jit(solution)/shard_map/ppermute | solution.py:122
  32.9 158.3 %collective-permute-start.10 = (f32[4096,64]{0,1:T(8,128)}, f32[4096,64]{0,1:T(8,128)S(1)}, u32[]{:S(2)}, u32[]{:S(2)}) collective-permute-start(f32[4096,64]{0,1:T(8,128)} %convolution_bitcast_fusion.1), channel_id=1, source_target_pairs={{8,0},{16,8},{24,16},{32,24},{40,32},{48,40},{56,48},{64,56},{72,6... | collective-permute-start | bytes 3145736 | tf_op jit(solution)/shard_map/ppermute | solution.py:123
  35.1 5.8 %collective-permute-start.1 = (f32[1,256]{1,0:T(1,128)S(1)}, f32[1,256]{1,0:T(1,128)S(1)}, u32[]{:S(2)}, u32[]{:S(2)}) collective-permute-start(f32[1,256]{1,0:T(1,128)S(1)} %add.200), channel_id=1, source_target_pairs={{0,2},{1,3},{2,0},{3,1},{4,6},{5,7},{6,4},{7,5},{8,10},{9,11},{10,... | collective-permute-start | bytes 3080 | tf_op jit(solution)/shard_map/ppermute | solution.py:68
  40.9 79.3 %collective-permute-start.2 = (f32[1,256]{1,0:T(1,128)S(1)}, f32[1,256]{1,0:T(1,128)S(1)}, u32[]{:S(2)}, u32[]{:S(2)}) collective-permute-start(f32[1,256]{1,0:T(1,128)S(1)} %add.201), channel_id=1, source_target_pairs={{0,4},{1,5},{2,6},{3,7},{4,0},{5,1},{6,2},{7,3},{8,12},{9,13},{10,... | collective-permute-start | bytes 3080 | tf_op jit(solution)/shard_map/ppermute | solution.py:68
  120.8 4.3 %collective-permute-start.3 = (f32[1,256]{1,0:T(1,128)S(1)}, f32[1,256]{1,0:T(1,128)S(1)}, u32[]{:S(2)}, u32[]{:S(2)}) collective-permute-start(f32[1,256]{1,0:T(1,128)S(1)} %get-tuple-element.13), channel_id=1, source_target_pairs={{0,64},{8,72},{16,80},{24,88},{32,96},{40,104},{48,112},{56,120},{... | collective-permute-start | bytes 3080 | tf_op jit(solution)/shard_map/ppermute | solution.py:77
  125.1 5.2 %collective-permute-start.4 = (f32[2,256]{1,0:T(2,128)S(1)}, f32[2,256]{1,0:T(2,128)S(1)}, u32[]{:S(2)}, u32[]{:S(2)}) collective-permute-start(f32[2,256]{1,0:T(2,128)S(1)} %maximum_select_fusion.5), channel_id=1, source_target_pairs={{0,128},{8,136},{16,144},{24,152},{32,160},{40,168},{48,176},{56,1... | collective-permute-start | bytes 6152 | tf_op jit(solution)/shard_map/ppermute | solution.py:77
  130.3 8.3 %collective-permute-start.5 = (f32[4,256]{1,0:T(4,128)S(1)}, f32[4,256]{1,0:T(4,128)S(1)}, u32[]{:S(2)}, u32[]{:S(2)}) collective-permute-start(f32[4,256]{1,0:T(4,128)S(1)} %maximum_select_fusion.4), channel_id=1, source_target_pairs={{0,256},{8,264},{16,272},{24,280},{32,288},{40,296},{48,304},{56,3... | collective-permute-start | bytes 12296 | tf_op jit(solution)/shard_map/ppermute | solution.py:77
  138.6 8.4 %collective-permute-start.6 = (f32[8,256]{1,0:T(8,128)S(1)}, f32[8,256]{1,0:T(8,128)S(1)}, u32[]{:S(2)}, u32[]{:S(2)}) collective-permute-start(f32[8,256]{1,0:T(8,128)S(1)} %maximum_select_fusion.3), channel_id=1, source_target_pairs={{0,8},{8,0},{16,24},{24,16},{32,40},{40,32},{48,56},{56,48},{64,72... | collective-permute-start | bytes 24584 | tf_op jit(solution)/shard_map/ppermute | solution.py:77
  147.0 14.5 %collective-permute-start.7 = (f32[16,256]{1,0:T(8,128)S(1)}, f32[16,256]{1,0:T(8,128)S(1)}, u32[]{:S(2)}, u32[]{:S(2)}) collective-permute-start(f32[16,256]{1,0:T(8,128)S(1)} %maximum_select_fusion.2), channel_id=1, source_target_pairs={{0,16},{8,24},{16,0},{24,8},{32,48},{40,56},{48,32},{56,40},{64,80... | collective-permute-start | bytes 49160 | tf_op jit(solution)/shard_map/ppermute | solution.py:77
  161.5 6.2 %collective-permute-start.8 = (f32[32,256]{1,0:T(8,128)S(1)}, f32[32,256]{1,0:T(8,128)S(1)}, u32[]{:S(2)}, u32[]{:S(2)}) collective-permute-start(f32[32,256]{1,0:T(8,128)S(1)} %maximum_select_fusion.1), channel_id=1, source_target_pairs={{0,32},{8,40},{16,48},{24,56},{32,0},{40,8},{48,16},{56,24},{64,96... | collective-permute-start | bytes 98312 | tf_op jit(solution)/shard_map/ppermute | solution.py:77
  183.4 2.4 copy-start.2
  194.3 7.0 %copy-start.13 = (f32[128]{0:T(128)S(1)}, f32[128]{0:T(128)}, u32[]{:S(2)}) copy-start(f32[128]{0:T(128)} %param.12) | copy-start | bytes 1540
  194.3 114.9 %all-to-all-start.1 = ((f32[1,128,32,128]{3,2,0,1:T(8,128)}), f32[1,128,32,128]{3,2,0,1:T(8,128)}, u32[]{:S(2)}, u32[]{:S(2)}) async-start(f32[1,128,32,128]{3,2,0,1:T(8,128)} %copy.35), calls=%async_computation.1 | async-start | bytes 4194304 | tf_op jit(solution)/shard_map/all_to_all | solution.py:154
  201.4 2.4 copy-start.6
  309.3 2.2 copy-start.1
  309.3 2.9 copy-start.3
  309.3 2.9 copy-start.4
  309.3 2.9 copy-start.7
  309.3 2.9 copy-start.8

commit v6 on v4

--- a/solution.py
+++ b/solution.py
@@ -61,12 +61,10 @@
     return [(i, i ^ bit) for i in range(count)]
 
 
-def sum_over(value, axis):
+def sum_over(value, axis, bits):
     count = lax.axis_size(axis)
-    bit = 1
-    while bit < count:
+    for bit in bits:
         value = value + lax.ppermute(value, axis, xor_pairs(count, bit))
-        bit *= 2
     return value
 
 
@@ -101,10 +99,13 @@
     row_start = space_index * row_count
 
     partial_value = jnp.sum(distribution, axis=(1, 3)) / (ky_count * kx_count)
-    density = sum_over(partial_value, "ky")
     doping = lookup(region, region_doping)
     relax_rate = lookup(region, region_relax)
-    charge = density - doping
+    ky_size = lax.axis_size("ky")
+    z_bits = [ky_size // 2] if ky_size > 1 else []
+    y_bits = [bit for bit in (1, 2, 4, 8, 16) if bit < ky_size // 2]
+    partial_charge = partial_value - jnp.where(lax.axis_index("ky") == 0, doping, 0.0)
+    charge = sum_over(jnp.stack([partial_value, partial_charge], axis=1), "ky", z_bits)
     far_bits = [bit for bit in (8, 16, 32) if bit < space_count]
     near_bits = [bit for bit in (1, 2, 4) if bit < space_count]
     positive_kx = upwind_sign > 0
@@ -127,6 +128,9 @@
     )
     every_row = gather_rows(far_rows, "space", near_bits)
     every_row = in_row_order(every_row, far_bits + near_bits, space_count * row_count)
+    every_row = sum_over(every_row, "ky", y_bits)
+    density = lax.dynamic_slice_in_dim(every_row[:, 0], row_start, row_count, 0)
+    every_row = every_row[:, 1]
 
     sine_rows = sine_table(grid_rows)
     sine_cols = sine_table(col_count)

time: 287 us -> 273 us (0.951)
  the two profiles are of different devices: /device:TPU:120 before, /device:TPU:110 now
where the time goes in v6:
time: 273 us
  waiting for transfers between devices  152 us (56%)
  starting transfers between devices  68.5 us (25%)
  matrix products  26.8 us (10%)
  local copies, waits for them, and re-layouts  13.8 us (5%)
  other arithmetic  11 us (4%)
    all_to_all x1, waiting for transfers between devices, shards(): lax.all_to_all(mixed, 'ky', split_axis=1, concat_axis=2, tiled=True)  65.1 us
    all_to_all x1, waiting for transfers between devices, shards(): spread = lax.all_to_all(held, 'ky', split_axis=2, concat_axis=1, tiled=True)  63.7 us
    ppermute x6, starting transfers between devices, gather_rows(): other = lax.ppermute(value, axis, xor_pairs(count, bit))  23.8 us
    ppermute x3, starting transfers between devices, sum_over(): value = value + lax.ppermute(value, axis, xor_pairs(count, bit))  19.1 us
    all_to_all x1, starting transfers between devices, shards(): spread = lax.all_to_all(held, 'ky', split_axis=2, concat_axis=1, tiled=True)  14.2 us
    ppermute x6, waiting for transfers between devices, gather_rows(): other = lax.ppermute(value, axis, xor_pairs(count, bit))  14 us
    ppermute x3, waiting for transfers between devices, sum_over(): value = value + lax.ppermute(value, axis, xor_pairs(count, bit))  9.4 us
    all_to_all x1, starting transfers between devices, shards(): lax.all_to_all(mixed, 'ky', split_axis=1, concat_axis=2, tiled=True)  5.93 us
  transfers between devices with their start and end apart: 13, of which 11 were waited for; matrix products, arithmetic and copies ran while one was open for 9% of the time, Pallas kernels for 0%

profile of v6, /device:TPU:110, one launch (start us, length us, event | category | flops | bytes accessed | tf_op | source)
XLA Modules:
  0.0 272.7 jit_solution(16073289007624803408)
XLA Ops:
  0.0 0.8 fusion.108
  1.2 4.0 %convolution_bitcast_fusion.2 = f32[4096,64]{0,1:T(8,128)} fusion(f32[4096,128]{1,0:T(8,128)} %bitcast.79, s32[128]{0:T(128)S(1)} %add_reduce_fusion.1, pred[128]{0:T(512)(128)(4,1)S(1)} %get-tuple-element.28), kind=kOutput, calls=%fused_computation.5 | convolution fusion | flops 402677760 | bytes 3146368 | tf_op jit(solution)/shard_map/dot_general | solution.py:119
  5.2 1.9 collective-permute-start.4
  7.5 2.4 convolution_bitcast_fusion.1
  9.9 3.6 %collective-permute-start.5 = (f32[4096,64]{0,1:T(8,128)}, f32[4096,64]{0,1:T(8,128)S(1)}, u32[]{:S(2)}, u32[]{:S(2)}) collective-permute-start(f32[4096,64]{0,1:T(8,128)} %convolution_bitcast_fusion.1), channel_id=1, source_target_pairs={{8,0},{16,8},{24,16},{32,24},{40,32},{48,40},{56,48},{64,56},{72,6... | collective-permute-start | bytes 3145736 | tf_op jit(solution)/shard_map/ppermute | solution.py:124
  13.7 0.7 fusion.87
  14.4 13.0 %collective-permute-start = (f32[1,2,256]{2,1,0:T(2,128)S(1)}, f32[1,2,256]{2,1,0:T(2,128)S(1)}, u32[]{:S(2)}, u32[]{:S(2)}) collective-permute-start(f32[1,2,256]{2,1,0:T(2,128)S(1)} %pad_maximum_fusion), channel_id=1, source_target_pairs={{0,4},{1,5},{2,6},{3,7},{4,0},{5,1},{6,2},{7,3},{8,12},{9,13},{10,... | collective-permute-start | bytes 6152 | tf_op jit(solution)/shard_map/ppermute | solution.py:67
  27.5 1.5 collective-permute-done
  29.0 3.0 %collective-permute-start.1 = (f32[1,2,256]{2,1,0:T(2,128)S(1)}, f32[1,2,256]{2,1,0:T(2,128)S(1)}, u32[]{:S(2)}, u32[]{:S(2)}) collective-permute-start(f32[1,2,256]{2,1,0:T(2,128)S(1)} %fusion.107), channel_id=1, source_target_pairs={{0,64},{8,72},{16,80},{24,88},{32,96},{40,104},{48,112},{56,120},{... | collective-permute-start | bytes 6152 | tf_op jit(solution)/shard_map/ppermute | solution.py:75
  32.0 2.5 collective-permute-done.1
  34.5 3.4 %collective-permute-start.2 = (f32[2,2,256]{2,1,0:T(2,128)S(1)}, f32[2,2,256]{2,1,0:T(2,128)S(1)}, u32[]{:S(2)}, u32[]{:S(2)}) collective-permute-start(f32[2,2,256]{2,1,0:T(2,128)S(1)} %maximum_select_fusion.5), channel_id=1, source_target_pairs={{0,128},{8,136},{16,144},{24,152},{32,160},{40,168},{48,176},{56,1... | collective-permute-start | bytes 12296 | tf_op jit(solution)/shard_map/ppermute | solution.py:75
  37.9 3.0 %collective-permute-done.2 = f32[2,2,256]{2,1,0:T(2,128)S(1)} collective-permute-done((f32[2,2,256]{2,1,0:T(2,128)S(1)}, f32[2,2,256]{2,1,0:T(2,128)S(1)}, u32[]{:S(2)}, u32[]{:S(2)}) %collective-permute-start.2) | collective-permute-done | bytes 4128 | tf_op jit(solution)/shard_map/ppermute | solution.py:75
  40.9 8.7 %collective-permute-start.3 = (f32[4,2,256]{2,1,0:T(2,128)S(1)}, f32[4,2,256]{2,1,0:T(2,128)S(1)}, u32[]{:S(2)}, u32[]{:S(2)}) collective-permute-start(f32[4,2,256]{2,1,0:T(2,128)S(1)} %maximum_select_fusion.4), channel_id=1, source_target_pairs={{0,256},{8,264},{16,272},{24,280},{32,288},{40,296},{48,304},{56,3... | collective-permute-start | bytes 24584 | tf_op jit(solution)/shard_map/ppermute | solution.py:75
  49.6 1.6 collective-permute-done.3
  51.2 2.5 copy.30
  53.8 14.2 %all-to-all-start = ((f32[1,16,256,128]{3,1,0,2:T(8,128)}), f32[1,16,256,128]{3,1,0,2:T(8,128)}, u32[]{:S(2)}, u32[]{:S(2)}) async-start(f32[1,16,256,128]{3,1,0,2:T(8,128)} %copy.30), calls=%async_computation | async-start | bytes 4194304 | tf_op jit(solution)/shard_map/all_to_all | solution.py:145
  68.0 0.3 fusion.67
  68.3 1.9 collective-permute-start.6
  70.2 1.1 collective-permute-done.6
  71.4 2.7 %collective-permute-start.7 = (f32[16,2,256]{2,1,0:T(2,128)S(1)}, f32[16,2,256]{2,1,0:T(2,128)S(1)}, u32[]{:S(2)}, u32[]{:S(2)}) collective-permute-start(f32[16,2,256]{2,1,0:T(2,128)S(1)} %maximum_select_fusion.2), channel_id=1, source_target_pairs={{0,16},{8,24},{16,0},{24,8},{32,48},{40,56},{48,32},{56,40},{64,80... | collective-permute-start | bytes 98312 | tf_op jit(solution)/shard_map/ppermute | solution.py:75
  74.1 0.7 broadcast_add_fusion
  74.8 2.4 collective-permute-done.7
  77.2 4.1 %collective-permute-start.8 = (f32[32,2,256]{2,1,0:T(2,128)S(1)}, f32[32,2,256]{2,1,0:T(2,128)S(1)}, u32[]{:S(2)}, u32[]{:S(2)}) collective-permute-start(f32[32,2,256]{2,1,0:T(2,128)S(1)} %maximum_select_fusion.1), channel_id=1, source_target_pairs={{0,32},{8,40},{16,48},{24,56},{32,0},{40,8},{48,16},{56,24},{64,96... | collective-permute-start | bytes 196616 | tf_op jit(solution)/shard_map/ppermute | solution.py:75
  81.5 3.4 %collective-permute-done.8 = f32[32,2,256]{2,1,0:T(2,128)S(1)} collective-permute-done((f32[32,2,256]{2,1,0:T(2,128)S(1)}, f32[32,2,256]{2,1,0:T(2,128)S(1)}, u32[]{:S(2)}, u32[]{:S(2)}) %collective-permute-start.8) | collective-permute-done | bytes 65568 | tf_op jit(solution)/shard_map/ppermute | solution.py:75
  85.0 1.9 collective-permute-start.9
  87.1 0.6 iota_add_fusion
  87.7 4.1 %collective-permute-done.9 = f32[64,2,256]{2,1,0:T(2,128)S(1)} collective-permute-done((f32[64,2,256]{2,1,0:T(2,128)S(1)}, f32[64,2,256]{2,1,0:T(2,128)S(1)}, u32[]{:S(2)}, u32[]{:S(2)}) %collective-permute-start.9) | collective-permute-done | bytes 131104 | tf_op jit(solution)/shard_map/ppermute | solution.py:67
  91.9 4.2 %collective-permute-start.10 = (f32[64,2,256]{2,1,0:T(2,128)S(1)}, f32[64,2,256]{2,1,0:T(2,128)}, u32[]{:S(2)}, u32[]{:S(2)}) collective-permute-start(f32[64,2,256]{2,1,0:T(2,128)S(1)} %bitcast_add_fusion.1), channel_id=1, source_target_pairs={{0,2},{1,3},{2,0},{3,1},{4,6},{5,7},{6,4},{7,5},{8,10},{9,11},{10,... | collective-permute-start | bytes 393224 | tf_op jit(solution)/shard_map/ppermute | solution.py:67
  96.1 0.6 multiply_multiply_fusion.1
  96.7 3.7 %collective-permute-done.10 = f32[64,2,256]{2,1,0:T(2,128)} collective-permute-done((f32[64,2,256]{2,1,0:T(2,128)S(1)}, f32[64,2,256]{2,1,0:T(2,128)}, u32[]{:S(2)}, u32[]{:S(2)}) %collective-permute-start.10) | collective-permute-done | bytes 131104 | tf_op jit(solution)/shard_map/ppermute | solution.py:67
  100.4 1.0 add.207
  101.5 0.4 fusion.45
  101.9 2.1 convolution_divide_fusion
  104.0 2.1 fusion.20
  106.2 4.5 %fusion.7 = f32[1,64,32]{2,0,1:T(1,128)S(1)} fusion(f32[256,1,1]{0,1,2:T(1,128)S(1)} %bitcast.93, s32[64,32]{1,0:T(8,128)S(1)} %copy-done.3, s32[64,32]{1,0:T(8,128)S(1)} %get-tuple-element.19), kind=kOutput, calls=%fused_computation.12 | convolution fusion | flops 8912896 | bytes 25600 | tf_op jit(solution)/shard_map/dot_general | solution.py:47
  110.9 63.7 %all-to-all-done = f32[1,16,256,128]{3,1,0,2:T(8,128)} async-done(((f32[1,16,256,128]{3,1,0,2:T(8,128)}), f32[1,16,256,128]{3,1,0,2:T(8,128)}, u32[]{:S(2)}, u32[]{:S(2)}) %all-to-all-start) | async-done | bytes 2097184 | tf_op jit(solution)/shard_map/all_to_all | solution.py:145
  174.6 2.2 copy.31
  176.9 2.6 fusion.1
  179.5 2.4 fusion.41
  181.9 3.1 %copy.33 = f32[1,128,32,128]{3,2,0,1:T(8,128)} copy(f32[1,128,32,128]{1,3,2,0:T(8,128)} %bitcast.84) | data formatting | bytes 4194304 | tf_op jit(solution)/shard_map/reshape | solution.py:159
  185.1 5.9 %all-to-all-start.1 = ((f32[1,128,32,128]{3,2,0,1:T(8,128)}), f32[1,128,32,128]{3,2,0,1:T(8,128)}, u32[]{:S(2)}, u32[]{:S(2)}) async-start(f32[1,128,32,128]{3,2,0,1:T(8,128)} %copy.33), calls=%async_computation.1 | async-start | bytes 4194304 | tf_op jit(solution)/shard_map/all_to_all | solution.py:160
  191.0 2.4 fusion.109
  193.4 1.9 fusion.55
  195.3 4.5 %convolution_add_fusion = f32[4096,128]{1,0:T(8,128)} fusion(f32[4096,128]{1,0:T(8,128)S(1)} %fusion.55, f32[4096,64]{0,1:T(8,128)} %collective-permute-done.4, s32[128]{0:T(128)S(1)} %add_reduce_fusion.1, pred[128]{0:T(512)(128)(4,1)S(1)} %get-tuple-element.28), kind=kOutput, calls=%fused_computation.1 | convolution fusion | flops 403193856 | bytes 5243520 | tf_op jit(solution)/shard_map/dot_general | solution.py:162
  199.8 65.1 %all-to-all-done.1 = f32[1,128,32,128]{3,2,0,1:T(8,128)} async-done(((f32[1,128,32,128]{3,2,0,1:T(8,128)}), f32[1,128,32,128]{3,2,0,1:T(8,128)}, u32[]{:S(2)}, u32[]{:S(2)}) %all-to-all-start.1) | async-done | bytes 2097184 | tf_op jit(solution)/shard_map/all_to_all | solution.py:160
  264.9 1.9 copy.34
  267.2 0.6 copy-done.2
  267.8 4.9 %fusion.6 = f32[1,16,256,128]{3,2,1,0:T(8,128)} fusion(f32[1,16,256,128]{3,2,1,0:T(8,128)S(1)} %copy-done, f32[1,16,8,32,128]{4,3,2,1,0:T(8,128)S(1)} %copy.34, f32[1,16,255,128]{3,2,1,0:T(8,128)} %get-tuple-element.16, f32[1,16,255,128]{3,2,1,0:T(8,128)S(1)} %copy-done.2, f32[1,16,256,128]{3,2,1,0:T(8,128)S(1)} %bitcast.81, f32[16,128]{1,0:T(8,128)S(1)} %copy-done.4, ...), kind=kLoop, calls=%fused_computation.11 | loop fusion | flops 6815744 | bytes 12577360 | tf_op jit(solution)/shard_map/add | solution.py:179
  (61 shorter events, 2.6 us)
Async XLA Ops:
  0.0 7.5 %copy-start = (f32[1,16,256,128]{3,2,1,0:T(8,128)S(1)}, f32[1,16,256,128]{3,2,1,0:T(8,128)}, u32[]{:S(2)}) copy-start(f32[1,16,256,128]{3,2,1,0:T(8,128)} %param.7) | copy-start | bytes 6291460
  0.8 6.7 %copy-start.5 = (pred[128]{0:T(512)(128)(4,1)}, pred[128]{0:T(512)(128)(4,1)S(1)}, u32[]{:S(2)}) copy-start(pred[128]{0:T(512)(128)(4,1)S(1)} %get-tuple-element.25) | copy-start | bytes 388
  5.2 46.1 %collective-permute-start.4 = (f32[4096,64]{0,1:T(8,128)}, f32[4096,64]{0,1:T(8,128)}, u32[]{:S(2)}, u32[]{:S(2)}) collective-permute-start(f32[4096,64]{0,1:T(8,128)} %convolution_bitcast_fusion.2), channel_id=1, source_target_pairs={{0,8},{8,16},{16,24},{24,32},{32,40},{40,48},{48,56},{56,64},{64,7... | collective-permute-start | bytes 3145736 | tf_op jit(solution)/shard_map/ppermute | solution.py:123
  7.5 6.2 %copy-start.8 = (s32[1,256]{1,0:T(1,128)S(1)}, s32[1,256]{1,0:T(1,128)}, u32[]{:S(2)}) copy-start(s32[1,256]{1,0:T(1,128)} %param.8) | copy-start | bytes 3076
  7.5 6.2 %copy-start.9 = (f32[6]{0:T(128)S(1)}, f32[6]{0:T(128)}, u32[]{:S(2)}) copy-start(f32[6]{0:T(128)} %param.10) | copy-start | bytes 76
  7.5 6.2 %copy-start.10 = (f32[6]{0:T(128)S(1)}, f32[6]{0:T(128)}, u32[]{:S(2)}) copy-start(f32[6]{0:T(128)} %param.9) | copy-start | bytes 76
  9.9 41.4 %collective-permute-start.5 = (f32[4096,64]{0,1:T(8,128)}, f32[4096,64]{0,1:T(8,128)S(1)}, u32[]{:S(2)}, u32[]{:S(2)}) collective-permute-start(f32[4096,64]{0,1:T(8,128)} %convolution_bitcast_fusion.1), channel_id=1, source_target_pairs={{8,0},{16,8},{24,16},{32,24},{40,32},{48,40},{56,48},{64,56},{72,6... | collective-permute-start | bytes 3145736 | tf_op jit(solution)/shard_map/ppermute | solution.py:124
  14.4 14.6 %collective-permute-start = (f32[1,2,256]{2,1,0:T(2,128)S(1)}, f32[1,2,256]{2,1,0:T(2,128)S(1)}, u32[]{:S(2)}, u32[]{:S(2)}) collective-permute-start(f32[1,2,256]{2,1,0:T(2,128)S(1)} %pad_maximum_fusion), channel_id=1, source_target_pairs={{0,4},{1,5},{2,6},{3,7},{4,0},{5,1},{6,2},{7,3},{8,12},{9,13},{10,... | collective-permute-start | bytes 6152 | tf_op jit(solution)/shard_map/ppermute | solution.py:67
  29.0 5.5 %collective-permute-start.1 = (f32[1,2,256]{2,1,0:T(2,128)S(1)}, f32[1,2,256]{2,1,0:T(2,128)S(1)}, u32[]{:S(2)}, u32[]{:S(2)}) collective-permute-start(f32[1,2,256]{2,1,0:T(2,128)S(1)} %fusion.107), channel_id=1, source_target_pairs={{0,64},{8,72},{16,80},{24,88},{32,96},{40,104},{48,112},{56,120},{... | collective-permute-start | bytes 6152 | tf_op jit(solution)/shard_map/ppermute | solution.py:75
  34.5 6.4 %collective-permute-start.2 = (f32[2,2,256]{2,1,0:T(2,128)S(1)}, f32[2,2,256]{2,1,0:T(2,128)S(1)}, u32[]{:S(2)}, u32[]{:S(2)}) collective-permute-start(f32[2,2,256]{2,1,0:T(2,128)S(1)} %maximum_select_fusion.5), channel_id=1, source_target_pairs={{0,128},{8,136},{16,144},{24,152},{32,160},{40,168},{48,176},{56,1... | collective-permute-start | bytes 12296 | tf_op jit(solution)/shard_map/ppermute | solution.py:75
  40.9 10.3 %collective-permute-start.3 = (f32[4,2,256]{2,1,0:T(2,128)S(1)}, f32[4,2,256]{2,1,0:T(2,128)S(1)}, u32[]{:S(2)}, u32[]{:S(2)}) collective-permute-start(f32[4,2,256]{2,1,0:T(2,128)S(1)} %maximum_select_fusion.4), channel_id=1, source_target_pairs={{0,256},{8,264},{16,272},{24,280},{32,288},{40,296},{48,304},{56,3... | collective-permute-start | bytes 24584 | tf_op jit(solution)/shard_map/ppermute | solution.py:75
  53.8 120.8 %all-to-all-start = ((f32[1,16,256,128]{3,1,0,2:T(8,128)}), f32[1,16,256,128]{3,1,0,2:T(8,128)}, u32[]{:S(2)}, u32[]{:S(2)}) async-start(f32[1,16,256,128]{3,1,0,2:T(8,128)} %copy.30), calls=%async_computation | async-start | bytes 4194304 | tf_op jit(solution)/shard_map/all_to_all | solution.py:145
  68.3 3.1 %collective-permute-start.6 = (f32[8,2,256]{2,1,0:T(2,128)S(1)}, f32[8,2,256]{2,1,0:T(2,128)S(1)}, u32[]{:S(2)}, u32[]{:S(2)}) collective-permute-start(f32[8,2,256]{2,1,0:T(2,128)S(1)} %maximum_select_fusion.3), channel_id=1, source_target_pairs={{0,8},{8,0},{16,24},{24,16},{32,40},{40,32},{48,56},{56,48},{64,72... | collective-permute-start | bytes 49160 | tf_op jit(solution)/shard_map/ppermute | solution.py:75
  71.4 5.8 %collective-permute-start.7 = (f32[16,2,256]{2,1,0:T(2,128)S(1)}, f32[16,2,256]{2,1,0:T(2,128)S(1)}, u32[]{:S(2)}, u32[]{:S(2)}) collective-permute-start(f32[16,2,256]{2,1,0:T(2,128)S(1)} %maximum_select_fusion.2), channel_id=1, source_target_pairs={{0,16},{8,24},{16,0},{24,8},{32,48},{40,56},{48,32},{56,40},{64,80... | collective-permute-start | bytes 98312 | tf_op jit(solution)/shard_map/ppermute | solution.py:75
  77.2 7.7 %collective-permute-start.8 = (f32[32,2,256]{2,1,0:T(2,128)S(1)}, f32[32,2,256]{2,1,0:T(2,128)S(1)}, u32[]{:S(2)}, u32[]{:S(2)}) collective-permute-start(f32[32,2,256]{2,1,0:T(2,128)S(1)} %maximum_select_fusion.1), channel_id=1, source_target_pairs={{0,32},{8,40},{16,48},{24,56},{32,0},{40,8},{48,16},{56,24},{64,96... | collective-permute-start | bytes 196616 | tf_op jit(solution)/shard_map/ppermute | solution.py:75
  85.0 6.9 %collective-permute-start.9 = (f32[64,2,256]{2,1,0:T(2,128)S(1)}, f32[64,2,256]{2,1,0:T(2,128)S(1)}, u32[]{:S(2)}, u32[]{:S(2)}) collective-permute-start(f32[64,2,256]{2,1,0:T(2,128)S(1)} %bitcast.85), channel_id=1, source_target_pairs={{0,1},{1,0},{2,3},{3,2},{4,5},{5,4},{6,7},{7,6},{8,9},{9,8},{10,11... | collective-permute-start | bytes 393224 | tf_op jit(solution)/shard_map/ppermute | solution.py:67
  91.9 8.5 %collective-permute-start.10 = (f32[64,2,256]{2,1,0:T(2,128)S(1)}, f32[64,2,256]{2,1,0:T(2,128)}, u32[]{:S(2)}, u32[]{:S(2)}) collective-permute-start(f32[64,2,256]{2,1,0:T(2,128)S(1)} %bitcast_add_fusion.1), channel_id=1, source_target_pairs={{0,2},{1,3},{2,0},{3,1},{4,6},{5,7},{6,4},{7,5},{8,10},{9,11},{10,... | collective-permute-start | bytes 393224 | tf_op jit(solution)/shard_map/ppermute | solution.py:67
  96.6 9.6 %copy-start.3 = (s32[64,32]{1,0:T(8,128)S(1)}, s32[64,32]{1,0:T(8,128)}, u32[]{:S(2)}) copy-start(s32[64,32]{1,0:T(8,128)} %get-tuple-element.20) | copy-start | bytes 24580
  185.1 5.9 %copy-start.11 = (f32[128]{0:T(128)S(1)}, f32[128]{0:T(128)}, u32[]{:S(2)}) copy-start(f32[128]{0:T(128)} %param.12) | copy-start | bytes 1540
  185.1 79.9 %all-to-all-start.1 = ((f32[1,128,32,128]{3,2,0,1:T(8,128)}), f32[1,128,32,128]{3,2,0,1:T(8,128)}, u32[]{:S(2)}, u32[]{:S(2)}) async-start(f32[1,128,32,128]{3,2,0,1:T(8,128)} %copy.33), calls=%async_computation.1 | async-start | bytes 4194304 | tf_op jit(solution)/shard_map/all_to_all | solution.py:160
  191.0 2.4 copy-start.6
  264.9 2.2 copy-start.1
  264.9 2.9 %copy-start.2 = (f32[1,16,255,128]{3,2,1,0:T(8,128)S(1)}, f32[1,16,255,128]{3,2,1,0:T(8,128)}, u32[]{:S(2)}) copy-start(f32[1,16,255,128]{3,2,1,0:T(8,128)} %get-tuple-element.15) | copy-start | bytes 6266884
  264.9 2.9 %copy-start.4 = (f32[16,128]{1,0:T(8,128)S(1)}, f32[16,128]{1,0:T(8,128)}, u32[]{:S(2)}) copy-start(f32[16,128]{1,0:T(8,128)} %param.11) | copy-start | bytes 24580
  264.9 2.9 %copy-start.7 = (f32[256]{0:T(256)S(1)}, f32[256]{0:T(256)}, u32[]{:S(2)}) copy-start(f32[256]{0:T(256)} %get-tuple-element.13) | copy-start | bytes 3076

commit v7 on v6

--- a/solution.py
+++ b/solution.py
@@ -86,6 +86,35 @@
     order = sorted(range(levels), key=lambda axis: -bits[levels - 1 - axis])
     shaped = jnp.transpose(shaped, order + list(range(levels, shaped.ndim)))
     return shaped.reshape((count,) + value.shape[1:])
+
+
+def spread_columns(block, first):
+    ky_size = lax.axis_size("ky")
+    quad = ky_size // 2
+    index = lax.axis_index("ky")
+    half, place = index // quad, index % quad
+    rows, ky_local, col_count, kx_count = block.shape
+    width = col_count // ky_size
+    blocks = block.reshape(rows, ky_local, 2, quad, width, kx_count)
+    received = []
+    for shift in range(quad):
+        piece = lax.dynamic_index_in_dim(blocks, (place + shift) % quad, 3, keepdims=False)
+        if shift:
+            pairs = [(h * quad + i, h * quad + (i + shift) % quad) for h in range(2) for i in range(quad)]
+            piece = lax.ppermute(piece, "ky", pairs)
+        received.append(piece)
+    stacked = jnp.stack(received, 0)
+    stacked = jnp.take(stacked, (place - jnp.arange(quad)) % quad, axis=0)
+    stacked = jnp.moveaxis(stacked, 3, 0)
+    stacked = lax.optimization_barrier((stacked, first))[0]
+    keep = lax.dynamic_index_in_dim(stacked, half, 0, keepdims=False)
+    send = lax.dynamic_index_in_dim(stacked, 1 - half, 0, keepdims=False)
+    got = lax.ppermute(send, "ky", [(i, i ^ quad) for i in range(ky_size)])
+    low = jnp.where(half == 0, keep, got)
+    high = jnp.where(half == 0, got, keep)
+    whole = jnp.concatenate([low, high], 0)
+    whole = jnp.moveaxis(whole, 1, 0)
+    return whole.reshape(rows, 2 * quad * ky_local, width, kx_count)
 
 
 def shards(distribution, region, region_doping, region_relax, equilibrium, kx_speed, upwind_sign):
@@ -123,9 +152,7 @@
     got_left = lax.ppermute(send_right, "space", forward_pairs)
     got_right = lax.ppermute(send_left, "space", backward_pairs)
     far_rows = gather_rows(charge, "space", far_bits)
-    held, far_rows, got_left, got_right = lax.optimization_barrier(
-        (distribution, far_rows, got_left, got_right)
-    )
+    far_rows, got_left, got_right = lax.optimization_barrier((far_rows, got_left, got_right))
     every_row = gather_rows(far_rows, "space", near_bits)
     every_row = in_row_order(every_row, far_bits + near_bits, space_count * row_count)
     every_row = sum_over(every_row, "ky", y_bits)
@@ -142,7 +169,7 @@
     own_rows = lax.dynamic_slice_in_dim(sine_rows, row_start, row_count, 0)
     potential = POISSON * jnp.dot(own_rows, back_cols, precision=precise)
 
-    spread = lax.all_to_all(held, "ky", split_axis=2, concat_axis=1, tiled=True)
+    spread = spread_columns(distribution, far_rows)
     local_cols = spread.shape[2]
     forward, backward = wigner_tables(ky_count)
     weights = own_differences(potential, ky_count, lax.axis_index("ky") * local_cols, local_cols)

time: 273 us -> 309 us (1.13)
  the two profiles are of different devices: /device:TPU:110 before, /device:TPU:104 now
where the time goes in v7:
time: 309 us; the launch traced here: 308 us
  waiting for transfers between devices  174 us (56%)
  starting transfers between devices  74.6 us (24%)
  matrix products  25.1 us (8%)
  other arithmetic  18.8 us (6%)
  local copies, waits for them, and re-layouts  15 us (5%)
    all_to_all x1, waiting for transfers between devices, shards(): lax.all_to_all(mixed, 'ky', split_axis=1, concat_axis=2, tiled=True)  81 us
    ppermute x1, waiting for transfers between devices, spread_columns(): got = lax.ppermute(send, 'ky', [(i, i ^ quad) for i in range(ky_size)])  75.6 us
    ppermute x3, starting transfers between devices, sum_over(): value = value + lax.ppermute(value, axis, xor_pairs(count, bit))  18.2 us
    all_to_all x1, starting transfers between devices, shards(): lax.all_to_all(mixed, 'ky', split_axis=1, concat_axis=2, tiled=True)  18 us
    ppermute x6, starting transfers between devices, gather_rows(): other = lax.ppermute(value, axis, xor_pairs(count, bit))  17.2 us
    ppermute x6, waiting for transfers between devices, gather_rows(): other = lax.ppermute(value, axis, xor_pairs(count, bit))  13.4 us
    ppermute x3, starting transfers between devices, spread_columns(): piece = lax.ppermute(piece, 'ky', pairs)  10.6 us
  transfers between devices with their start and end apart: 16, of which 9 were waited for; matrix products, arithmetic and copies ran while one was open for 12% of the time, Pallas kernels for 0%

profile of v7, /device:TPU:104, one launch (start us, length us, event | category | flops | bytes accessed | tf_op | source)
XLA Modules:
  0.0 308.2 jit_solution(11496615003378983258)
XLA Ops:
  0.0 1.9 reduce_sum.27
  2.0 0.7 fusion.88
  2.7 13.0 %collective-permute-start = (f32[1,2,256]{2,1,0:T(2,128)S(1)}, f32[1,2,256]{2,1,0:T(2,128)S(1)}, u32[]{:S(2)}, u32[]{:S(2)}) collective-permute-start(f32[1,2,256]{2,1,0:T(2,128)S(1)} %pad_maximum_fusion.1), channel_id=1, source_target_pairs={{0,4},{1,5},{2,6},{3,7},{4,0},{5,1},{6,2},{7,3},{8,12},{9,13},{10,... | collective-permute-start | bytes 6152 | tf_op jit(solution)/shard_map/ppermute | solution.py:67
  16.2 2.5 convolution_bitcast_fusion.2
  18.6 1.9 collective-permute-start.4
  20.9 2.4 convolution_bitcast_fusion.1
  23.3 5.7 %collective-permute-start.5 = (f32[4096,64]{0,1:T(8,128)}, f32[4096,64]{0,1:T(8,128)}, u32[]{:S(2)}, u32[]{:S(2)}) collective-permute-start(f32[4096,64]{0,1:T(8,128)} %convolution_bitcast_fusion.1), channel_id=1, source_target_pairs={{8,0},{16,8},{24,16},{32,24},{40,32},{48,40},{56,48},{64,56},{72,6... | collective-permute-start | bytes 3145736 | tf_op jit(solution)/shard_map/ppermute | solution.py:153
  29.2 1.2 dynamic-slice_bitcast_fusion.4
  30.4 2.3 collective-permute-start.8
  32.7 4.5 %collective-permute-start.7 = (f32[1,16,2,32,128]{4,3,2,1,0:T(8,128)}, f32[1,16,2,32,128]{4,3,2,1,0:T(8,128)}, u32[]{:S(2)}, u32[]{:S(2)}) collective-permute-start(f32[1,16,2,32,128]{4,3,2,1,0:T(8,128)} %get-tuple-element.21), channel_id=1, source_target_pairs={{0,2},{1,3},{2,0},{3,1},{4,6},{5,7},{6,4},{7,5},{8,10},{9,11},{10,... | collective-permute-start | bytes 1572872 | tf_op jit(solution)/shard_map/ppermute | solution.py:104
  37.8 0.7 broadcast_add_fusion
  38.7 2.9 collective-permute-start.1
  41.7 2.5 collective-permute-done.1
  44.2 3.4 %collective-permute-start.2 = (f32[2,2,256]{2,1,0:T(2,128)S(1)}, f32[2,2,256]{2,1,0:T(2,128)S(1)}, u32[]{:S(2)}, u32[]{:S(2)}) collective-permute-start(f32[2,2,256]{2,1,0:T(2,128)S(1)} %maximum_select_fusion.5), channel_id=1, source_target_pairs={{0,128},{8,136},{16,144},{24,152},{32,160},{40,168},{48,176},{56,1... | collective-permute-start | bytes 12296 | tf_op jit(solution)/shard_map/ppermute | solution.py:75
  48.1 2.5 collective-permute-done.2
  50.6 4.3 %collective-permute-start.3 = (f32[4,2,256]{2,1,0:T(2,128)S(1)}, f32[4,2,256]{2,1,0:T(2,128)S(1)}, u32[]{:S(2)}, u32[]{:S(2)}) collective-permute-start(f32[4,2,256]{2,1,0:T(2,128)S(1)} %maximum_select_fusion.4), channel_id=1, source_target_pairs={{0,256},{8,264},{16,272},{24,280},{32,288},{40,296},{48,304},{56,3... | collective-permute-start | bytes 24584 | tf_op jit(solution)/shard_map/ppermute | solution.py:75
  54.9 0.6 multiply_multiply_fusion
  55.5 4.5 %collective-permute-done.3 = f32[4,2,256]{2,1,0:T(2,128)S(1)} collective-permute-done((f32[4,2,256]{2,1,0:T(2,128)S(1)}, f32[4,2,256]{2,1,0:T(2,128)S(1)}, u32[]{:S(2)}, u32[]{:S(2)}) %collective-permute-start.3) | collective-permute-done | bytes 8224 | tf_op jit(solution)/shard_map/ppermute | solution.py:75
  60.0 3.8 %collective-permute-start.6 = (f32[1,16,2,32,128]{4,3,2,1,0:T(8,128)S(1)}, f32[1,16,2,32,128]{4,3,2,1,0:T(8,128)}, u32[]{:S(2)}, u32[]{:S(2)}) collective-permute-start(f32[1,16,2,32,128]{4,3,2,1,0:T(8,128)S(1)} %get-tuple-element.22), channel_id=1, source_target_pairs={{0,1},{1,2},{2,3},{3,0},{4,5},{5,6},{6,7},{7,4},{8,9},{9,10},{10,1... | collective-permute-start | bytes 1572872 | tf_op jit(solution)/shard_map/ppermute | solution.py:104
  63.9 1.9 collective-permute-start.10
  67.0 1.9 collective-permute-start.11
  68.9 0.6 multiply_multiply_fusion.1
  69.5 3.2 %collective-permute-done.11 = f32[16,2,256]{2,1,0:T(2,128)S(1)} collective-permute-done((f32[16,2,256]{2,1,0:T(2,128)S(1)}, f32[16,2,256]{2,1,0:T(2,128)S(1)}, u32[]{:S(2)}, u32[]{:S(2)}) %collective-permute-start.11) | collective-permute-done | bytes 32800 | tf_op jit(solution)/shard_map/ppermute | solution.py:75
  72.8 2.8 collective-permute-start.12
  75.7 3.0 maximum_bitcast_fusion
  78.6 3.6 %gather_fusion = f32[4,16,2,32,128]{4,3,2,1,0:T(8,128)} fusion(f32[4,16,2,32,128]{4,3,2,1,0:T(8,128)} %maximum_bitcast_fusion, s32[1024]{0:T(1024)S(1)} %pad_clamp_fusion), kind=kCustom, calls=%fused_computation | custom fusion | bytes 4194320 | tf_op jit(solution)/shard_map/jit(_take)/gather | solution.py:107
  82.3 2.0 collective-permute-start.13
  84.4 1.9 fusion.7
  86.4 2.8 collective-permute-done.13
  89.3 3.1 %collective-permute-start.14 = (f32[64,2,256]{2,1,0:T(2,128)S(1)}, f32[64,2,256]{2,1,0:T(2,128)S(1)}, u32[]{:S(2)}, u32[]{:S(2)}) collective-permute-start(f32[64,2,256]{2,1,0:T(2,128)S(1)} %bitcast_add_fusion.1), channel_id=1, source_target_pairs={{0,2},{1,3},{2,0},{3,1},{4,6},{5,7},{6,4},{7,5},{8,10},{9,11},{10,... | collective-permute-start | bytes 393224 | tf_op jit(solution)/shard_map/ppermute | solution.py:67
  92.4 1.2 dynamic-slice_bitcast_fusion
  93.6 3.0 collective-permute-start.9
  96.6 1.1 collective-permute-done.14
  98.3 1.3 convolution_divide_fusion
  99.6 1.3 fusion.21
  101.1 4.5 %fusion.8 = f32[1,64,32]{2,0,1:T(1,128)S(1)} fusion(f32[256,1,1]{0,1,2:T(1,128)S(1)} %bitcast.120, s32[64,32]{1,0:T(8,128)S(1)} %copy-done.4, s32[64,32]{1,0:T(8,128)S(1)} %get-tuple-element.25), kind=kOutput, calls=%fused_computation.17 | convolution fusion | flops 8912896 | bytes 25600 | tf_op jit(solution)/shard_map/dot_general | solution.py:47
  105.8 75.6 %collective-permute-done.9 = f32[4,1,16,32,128]{4,3,2,0,1:T(8,128)S(1)} collective-permute-done((f32[4,1,16,32,128]{4,3,2,0,1:T(8,128)}, f32[4,1,16,32,128]{4,3,2,0,1:T(8,128)S(1)}, u32[]{:S(2)}, u32[]{:S(2)}) %collective-permute-start.9) | collective-permute-done | bytes 1048608 | tf_op jit(solution)/shard_map/ppermute | solution.py:112
  181.4 1.5 bitcast_select_fusion.2
  183.2 2.6 fusion.1
  185.8 2.4 fusion.42
  188.2 3.1 %copy.27 = f32[1,128,32,128]{3,2,0,1:T(8,128)} copy(f32[1,128,32,128]{1,3,2,0:T(8,128)} %bitcast.111) | data formatting | bytes 4194304 | tf_op jit(solution)/shard_map/reshape | solution.py:186
  191.4 18.0 %all-to-all-start = ((f32[1,128,32,128]{3,2,0,1:T(8,128)}), f32[1,128,32,128]{3,2,0,1:T(8,128)}, u32[]{:S(2)}, u32[]{:S(2)}) async-start(f32[1,128,32,128]{3,2,0,1:T(8,128)} %copy.27), calls=%async_computation | async-start | bytes 4194304 | tf_op jit(solution)/shard_map/all_to_all | solution.py:187
  209.4 2.4 fusion.112
  211.8 3.1 %fusion.56 = f32[4096,128]{1,0:T(8,128)S(1)} fusion(f32[4096,64]{0,1:T(8,128)} %collective-permute-done.5, s32[128]{0:T(128)S(1)} %add_reduce_fusion, pred[128]{0:T(512)(128)(4,1)S(1)} %copy-done.9), kind=kOutput, calls=%fused_computation.84 | convolution fusion | flops 402669568 | bytes 3146368 | tf_op jit(solution)/shard_map/dot_general | solution.py:189
  214.9 4.5 %convolution_add_fusion = f32[4096,128]{1,0:T(8,128)} fusion(f32[4096,128]{1,0:T(8,128)S(1)} %fusion.56, f32[4096,64]{0,1:T(8,128)} %collective-permute-done.4, s32[128]{0:T(128)S(1)} %add_reduce_fusion.1, pred[128]{0:T(512)(128)(4,1)S(1)} %copy-done.7), kind=kOutput, calls=%fused_computation.2 | convolution fusion | flops 403193856 | bytes 5243520 | tf_op jit(solution)/shard_map/dot_general | solution.py:189
  219.4 81.0 %all-to-all-done = f32[1,128,32,128]{3,2,0,1:T(8,128)} async-done(((f32[1,128,32,128]{3,2,0,1:T(8,128)}), f32[1,128,32,128]{3,2,0,1:T(8,128)}, u32[]{:S(2)}, u32[]{:S(2)}) %all-to-all-start) | async-done | bytes 2097184 | tf_op jit(solution)/shard_map/all_to_all | solution.py:187
  300.4 1.9 copy.28
  303.2 4.9 %fusion.6 = f32[1,16,256,128]{3,2,1,0:T(8,128)} fusion(f32[1,16,256,128]{3,2,1,0:T(8,128)S(1)} %copy-done, f32[1,16,8,32,128]{4,3,2,1,0:T(8,128)S(1)} %copy.28, f32[1,16,255,128]{3,2,1,0:T(8,128)} %get-tuple-element.18, f32[1,16,255,128]{3,2,1,0:T(8,128)S(1)} %copy-done.3, f32[1,16,256,128]{3,2,1,0:T(8,128)S(1)} %bitcast.108, f32[16,128]{1,0:T(8,128)S(1)} %copy-done.5, ...), kind=kLoop, calls=%fused_computation.14 | loop fusion | flops 6815744 | bytes 12577360 | tf_op jit(solution)/shard_map/add | solution.py:206
  (91 shorter events, 5.7 us)
Async XLA Ops:
  0.0 16.2 %copy-start = (f32[1,16,256,128]{3,2,1,0:T(8,128)S(1)}, f32[1,16,256,128]{3,2,1,0:T(8,128)}, u32[]{:S(2)}) copy-start(f32[1,16,256,128]{3,2,1,0:T(8,128)} %param.7) | copy-start | bytes 6291460
  0.0 2.0 copy-start.14
  0.0 2.0 copy-start.15
  0.0 2.0 copy-start.11
  0.0 15.7 %copy-start.13 = (s32[128]{0:T(128)S(1)}, s32[128]{0:T(128)}, u32[]{:S(2)}) copy-start(s32[128]{0:T(128)} %param.13) | copy-start | bytes 1540
  2.7 36.0 %collective-permute-start = (f32[1,2,256]{2,1,0:T(2,128)S(1)}, f32[1,2,256]{2,1,0:T(2,128)S(1)}, u32[]{:S(2)}, u32[]{:S(2)}) collective-permute-start(f32[1,2,256]{2,1,0:T(2,128)S(1)} %pad_maximum_fusion.1), channel_id=1, source_target_pairs={{0,4},{1,5},{2,6},{3,7},{4,0},{5,1},{6,2},{7,3},{8,12},{9,13},{10,... | collective-permute-start | bytes 6152 | tf_op jit(solution)/shard_map/ppermute | solution.py:67
  15.8 7.6 %copy-start.6 = (pred[128]{0:T(512)(128)(4,1)}, pred[128]{0:T(512)(128)(4,1)S(1)}, u32[]{:S(2)}) copy-start(pred[128]{0:T(512)(128)(4,1)S(1)} %get-tuple-element.34) | copy-start | bytes 388
  15.8 7.5 %copy-start.8 = (pred[128]{0:T(512)(128)(4,1)}, pred[128]{0:T(512)(128)(4,1)S(1)}, u32[]{:S(2)}) copy-start(pred[128]{0:T(512)(128)(4,1)S(1)} %get-tuple-element.31) | copy-start | bytes 388
  18.6 45.2 %collective-permute-start.4 = (f32[4096,64]{0,1:T(8,128)}, f32[4096,64]{0,1:T(8,128)}, u32[]{:S(2)}, u32[]{:S(2)}) collective-permute-start(f32[4096,64]{0,1:T(8,128)} %convolution_bitcast_fusion.2), channel_id=1, source_target_pairs={{0,8},{8,16},{16,24},{24,32},{32,40},{40,48},{48,56},{56,64},{64,7... | collective-permute-start | bytes 3145736 | tf_op jit(solution)/shard_map/ppermute | solution.py:152
  23.3 40.5 %collective-permute-start.5 = (f32[4096,64]{0,1:T(8,128)}, f32[4096,64]{0,1:T(8,128)}, u32[]{:S(2)}, u32[]{:S(2)}) collective-permute-start(f32[4096,64]{0,1:T(8,128)} %convolution_bitcast_fusion.1), channel_id=1, source_target_pairs={{8,0},{16,8},{24,16},{32,24},{40,32},{48,40},{56,48},{64,56},{72,6... | collective-permute-start | bytes 3145736 | tf_op jit(solution)/shard_map/ppermute | solution.py:153
  30.4 45.3 %collective-permute-start.8 = (f32[1,16,2,32,128]{4,3,2,1,0:T(8,128)}, f32[1,16,2,32,128]{4,3,2,1,0:T(8,128)}, u32[]{:S(2)}, u32[]{:S(2)}) collective-permute-start(f32[1,16,2,32,128]{4,3,2,1,0:T(8,128)} %get-tuple-element.20), channel_id=1, source_target_pairs={{0,3},{1,0},{2,1},{3,2},{4,7},{5,4},{6,5},{7,6},{8,11},{9,8},{10,9... | collective-permute-start | bytes 1572872 | tf_op jit(solution)/shard_map/ppermute | solution.py:104
  32.7 42.9 %collective-permute-start.7 = (f32[1,16,2,32,128]{4,3,2,1,0:T(8,128)}, f32[1,16,2,32,128]{4,3,2,1,0:T(8,128)}, u32[]{:S(2)}, u32[]{:S(2)}) collective-permute-start(f32[1,16,2,32,128]{4,3,2,1,0:T(8,128)} %get-tuple-element.21), channel_id=1, source_target_pairs={{0,2},{1,3},{2,0},{3,1},{4,6},{5,7},{6,4},{7,5},{8,10},{9,11},{10,... | collective-permute-start | bytes 1572872 | tf_op jit(solution)/shard_map/ppermute | solution.py:104
  38.7 5.5 %collective-permute-start.1 = (f32[1,2,256]{2,1,0:T(2,128)S(1)}, f32[1,2,256]{2,1,0:T(2,128)S(1)}, u32[]{:S(2)}, u32[]{:S(2)}) collective-permute-start(f32[1,2,256]{2,1,0:T(2,128)S(1)} %fusion.110), channel_id=1, source_target_pairs={{0,64},{8,72},{16,80},{24,88},{32,96},{40,104},{48,112},{56,120},{... | collective-permute-start | bytes 6152 | tf_op jit(solution)/shard_map/ppermute | solution.py:75
  44.2 6.4 %collective-permute-start.2 = (f32[2,2,256]{2,1,0:T(2,128)S(1)}, f32[2,2,256]{2,1,0:T(2,128)S(1)}, u32[]{:S(2)}, u32[]{:S(2)}) collective-permute-start(f32[2,2,256]{2,1,0:T(2,128)S(1)} %maximum_select_fusion.5), channel_id=1, source_target_pairs={{0,128},{8,136},{16,144},{24,152},{32,160},{40,168},{48,176},{56,1... | collective-permute-start | bytes 12296 | tf_op jit(solution)/shard_map/ppermute | solution.py:75
  50.6 9.4 %collective-permute-start.3 = (f32[4,2,256]{2,1,0:T(2,128)S(1)}, f32[4,2,256]{2,1,0:T(2,128)S(1)}, u32[]{:S(2)}, u32[]{:S(2)}) collective-permute-start(f32[4,2,256]{2,1,0:T(2,128)S(1)} %maximum_select_fusion.4), channel_id=1, source_target_pairs={{0,256},{8,264},{16,272},{24,280},{32,288},{40,296},{48,304},{56,3... | collective-permute-start | bytes 24584 | tf_op jit(solution)/shard_map/ppermute | solution.py:75
  60.0 15.6 %collective-permute-start.6 = (f32[1,16,2,32,128]{4,3,2,1,0:T(8,128)S(1)}, f32[1,16,2,32,128]{4,3,2,1,0:T(8,128)}, u32[]{:S(2)}, u32[]{:S(2)}) collective-permute-start(f32[1,16,2,32,128]{4,3,2,1,0:T(8,128)S(1)} %get-tuple-element.22), channel_id=1, source_target_pairs={{0,1},{1,2},{2,3},{3,0},{4,5},{5,6},{6,7},{7,4},{8,9},{9,10},{10,1... | collective-permute-start | bytes 1572872 | tf_op jit(solution)/shard_map/ppermute | solution.py:104
  63.9 3.1 collective-permute-start.10
  67.0 5.8 %collective-permute-start.11 = (f32[16,2,256]{2,1,0:T(2,128)S(1)}, f32[16,2,256]{2,1,0:T(2,128)S(1)}, u32[]{:S(2)}, u32[]{:S(2)}) collective-permute-start(f32[16,2,256]{2,1,0:T(2,128)S(1)} %maximum_select_fusion.2), channel_id=1, source_target_pairs={{0,16},{8,24},{16,0},{24,8},{32,48},{40,56},{48,32},{56,40},{64,80... | collective-permute-start | bytes 98312 | tf_op jit(solution)/shard_map/ppermute | solution.py:75
  72.8 9.4 %collective-permute-start.12 = (f32[32,2,256]{2,1,0:T(2,128)S(1)}, f32[32,2,256]{2,1,0:T(2,128)S(1)}, u32[]{:S(2)}, u32[]{:S(2)}) collective-permute-start(f32[32,2,256]{2,1,0:T(2,128)S(1)} %maximum_select_fusion.1), channel_id=1, source_target_pairs={{0,32},{8,40},{16,48},{24,56},{32,0},{40,8},{48,16},{56,24},{64,96... | collective-permute-start | bytes 196616 | tf_op jit(solution)/shard_map/ppermute | solution.py:75
  78.6 5.8 %copy-start.12 = (pred[4]{0:T(512)(128)(4,1)S(1)}, pred[4]{0:T(512)(128)(4,1)}, u32[]{:S(2)}) copy-start(pred[4]{0:T(512)(128)(4,1)} %compare_and_fusion) | copy-start | bytes 16
  82.3 6.9 %collective-permute-start.13 = (f32[64,2,256]{2,1,0:T(2,128)S(1)}, f32[64,2,256]{2,1,0:T(2,128)S(1)}, u32[]{:S(2)}, u32[]{:S(2)}) collective-permute-start(f32[64,2,256]{2,1,0:T(2,128)S(1)} %bitcast.112), channel_id=1, source_target_pairs={{0,1},{1,0},{2,3},{3,2},{4,5},{5,4},{6,7},{7,6},{8,9},{9,8},{10,11... | collective-permute-start | bytes 393224 | tf_op jit(solution)/shard_map/ppermute | solution.py:67
  86.3 13.3 %copy-start.1 = (f32[2,4,1,16,32,128]{5,4,0,3,1,2:T(8,128)}, f32[2,4,1,16,32,128]{5,4,0,3,1,2:T(8,128)S(1)}, u32[]{:S(2)}) copy-start(f32[2,4,1,16,32,128]{5,4,0,3,1,2:T(8,128)S(1)} %fusion.7) | copy-start | bytes 6291460
  86.3 11.9 %copy-start.17 = (s32[256]{0:T(256)S(1)}, s32[256]{0:T(256)}, u32[]{:S(2)}) copy-start(s32[256]{0:T(256)} %iota_add_fusion) | copy-start | bytes 3076
  86.3 11.9 %copy-start.18 = (f32[256]{0:T(256)S(1)}, f32[256]{0:T(256)}, u32[]{:S(2)}) copy-start(f32[256]{0:T(256)} %multiply_multiply_fusion) | copy-start | bytes 3076
  86.3 11.9 %copy-start.19 = (f32[64]{0:T(128)S(1)}, f32[64]{0:T(128)}, u32[]{:S(2)}) copy-start(f32[64]{0:T(128)} %multiply_multiply_fusion.1) | copy-start | bytes 772
  89.3 11.8 %copy-start.4 = (s32[64,32]{1,0:T(8,128)S(1)}, s32[64,32]{1,0:T(8,128)}, u32[]{:S(2)}) copy-start(s32[64,32]{1,0:T(8,128)} %get-tuple-element.26) | copy-start | bytes 24580
  89.3 8.4 %collective-permute-start.14 = (f32[64,2,256]{2,1,0:T(2,128)S(1)}, f32[64,2,256]{2,1,0:T(2,128)S(1)}, u32[]{:S(2)}, u32[]{:S(2)}) collective-permute-start(f32[64,2,256]{2,1,0:T(2,128)S(1)} %bitcast_add_fusion.1), channel_id=1, source_target_pairs={{0,2},{1,3},{2,0},{3,1},{4,6},{5,7},{6,4},{7,5},{8,10},{9,11},{10,... | collective-permute-start | bytes 393224 | tf_op jit(solution)/shard_map/ppermute | solution.py:67
  93.6 87.8 %collective-permute-start.9 = (f32[4,1,16,32,128]{4,3,2,0,1:T(8,128)}, f32[4,1,16,32,128]{4,3,2,0,1:T(8,128)S(1)}, u32[]{:S(2)}, u32[]{:S(2)}) collective-permute-start(f32[4,1,16,32,128]{4,3,2,0,1:T(8,128)} %dynamic-slice_bitcast_fusion), channel_id=1, source_target_pairs={{0,4},{1,5},{2,6},{3,7},{4,0},{5,1},{6,2},{7,3},{8,12},{9,13},{10,... | collective-permute-start | bytes 3145736 | tf_op jit(solution)/shard_map/ppermute | solution.py:112
  191.3 18.0 %copy-start.16 = (f32[128]{0:T(128)S(1)}, f32[128]{0:T(128)}, u32[]{:S(2)}) copy-start(f32[128]{0:T(128)} %param.12) | copy-start | bytes 1540
  191.4 109.0 %all-to-all-start = ((f32[1,128,32,128]{3,2,0,1:T(8,128)}), f32[1,128,32,128]{3,2,0,1:T(8,128)}, u32[]{:S(2)}, u32[]{:S(2)}) async-start(f32[1,128,32,128]{3,2,0,1:T(8,128)} %copy.27), calls=%async_computation | async-start | bytes 4194304 | tf_op jit(solution)/shard_map/all_to_all | solution.py:187
  209.4 2.4 copy-start.9
  211.8 3.1 %copy-start.7 = (pred[128]{0:T(512)(128)(4,1)S(1)}, pred[128]{0:T(512)(128)(4,1)}, u32[]{:S(2)}) copy-start(pred[128]{0:T(512)(128)(4,1)} %copy-done.6) | copy-start | bytes 388
  300.4 2.2 copy-start.2
  300.4 2.9 copy-start.3
  300.4 2.9 copy-start.5
  300.4 2.9 copy-start.10

commit v8 on v6

--- a/solution.py
+++ b/solution.py
@@ -176,7 +176,9 @@
     relaxation = relax_rate[:, None, :, None] * (
         density[:, None, :, None] * equilibrium[None, :, None, :] - distribution
     )
-    return distribution + STEP * (drift_x + drift_y + wigner + relaxation)
+    base = distribution + STEP * (drift_x + drift_y + relaxation)
+    wigner, base = lax.optimization_barrier((wigner, base))
+    return base + STEP * wigner
 
 
 def solution(mesh):

time: 273 us -> 268 us (0.982)
  the two profiles are of different devices: /device:TPU:110 before, /device:TPU:123 now
where the time goes in v8:
time: 268 us
  waiting for transfers between devices  150 us (56%)
  starting transfers between devices  70.1 us (26%)
  matrix products  25.5 us (10%)
  local copies, waits for them, and re-layouts  11.3 us (4%)
  other arithmetic  10.8 us (4%)
    all_to_all x1, waiting for transfers between devices, shards(): spread = lax.all_to_all(held, 'ky', split_axis=2, concat_axis=1, tiled=True)  78.8 us
    all_to_all x1, waiting for transfers between devices, shards(): lax.all_to_all(mixed, 'ky', split_axis=1, concat_axis=2, tiled=True)  51.5 us
    ppermute x6, starting transfers between devices, gather_rows(): other = lax.ppermute(value, axis, xor_pairs(count, bit))  28.7 us
    ppermute x3, starting transfers between devices, sum_over(): value = value + lax.ppermute(value, axis, xor_pairs(count, bit))  18.1 us
    all_to_all x1, starting transfers between devices, shards(): spread = lax.all_to_all(held, 'ky', split_axis=2, concat_axis=1, tiled=True)  13.1 us
    ppermute x6, waiting for transfers between devices, gather_rows(): other = lax.ppermute(value, axis, xor_pairs(count, bit))  10.2 us
    ppermute x3, waiting for transfers between devices, sum_over(): value = value + lax.ppermute(value, axis, xor_pairs(count, bit))  9.07 us
  transfers between devices with their start and end apart: 13, of which 11 were waited for; matrix products, arithmetic and copies ran while one was open for 9% of the time, Pallas kernels for 0%

profile of v8, /device:TPU:123, one launch (start us, length us, event | category | flops | bytes accessed | tf_op | source)
XLA Modules:
  0.0 267.7 jit_solution(16485883620975166827)
XLA Ops:
  0.0 0.8 fusion.105
  1.2 4.0 %convolution_bitcast_fusion.2 = f32[4096,64]{0,1:T(8,128)} fusion(f32[4096,128]{1,0:T(8,128)} %bitcast.72, s32[128]{0:T(128)S(1)} %add_reduce_fusion.1, pred[128]{0:T(512)(128)(4,1)S(1)} %get-tuple-element.32), kind=kOutput, calls=%fused_computation.5 | convolution fusion | flops 402677760 | bytes 3146368 | tf_op jit(solution)/shard_map/dot_general | solution.py:119
  5.2 3.7 %collective-permute-start.4 = (f32[4096,64]{0,1:T(8,128)}, f32[4096,64]{0,1:T(8,128)}, u32[]{:S(2)}, u32[]{:S(2)}) collective-permute-start(f32[4096,64]{0,1:T(8,128)} %convolution_bitcast_fusion.2), channel_id=1, source_target_pairs={{0,8},{8,16},{16,24},{24,32},{32,40},{40,48},{48,56},{56,64},{64,7... | collective-permute-start | bytes 3145736 | tf_op jit(solution)/shard_map/ppermute | solution.py:123
  9.3 2.4 convolution_bitcast_fusion.1
  11.6 1.9 collective-permute-start.5
  13.8 0.7 fusion.84
  14.5 12.7 %collective-permute-start = (f32[1,2,256]{2,1,0:T(2,128)S(1)}, f32[1,2,256]{2,1,0:T(2,128)S(1)}, u32[]{:S(2)}, u32[]{:S(2)}) collective-permute-start(f32[1,2,256]{2,1,0:T(2,128)S(1)} %pad_maximum_fusion), channel_id=1, source_target_pairs={{0,4},{1,5},{2,6},{3,7},{4,0},{5,1},{6,2},{7,3},{8,12},{9,13},{10,... | collective-permute-start | bytes 6152 | tf_op jit(solution)/shard_map/ppermute | solution.py:67
  27.2 1.0 collective-permute-done
  28.2 2.6 collective-permute-start.1
  30.9 1.7 collective-permute-done.1
  32.5 3.1 %collective-permute-start.2 = (f32[2,2,256]{2,1,0:T(2,128)S(1)}, f32[2,2,256]{2,1,0:T(2,128)S(1)}, u32[]{:S(2)}, u32[]{:S(2)}) collective-permute-start(f32[2,2,256]{2,1,0:T(2,128)S(1)} %maximum_select_fusion.5), channel_id=1, source_target_pairs={{0,128},{8,136},{16,144},{24,152},{32,160},{40,168},{48,176},{56,1... | collective-permute-start | bytes 12296 | tf_op jit(solution)/shard_map/ppermute | solution.py:75
  35.6 2.2 collective-permute-done.2
  37.8 8.1 %collective-permute-start.3 = (f32[4,2,256]{2,1,0:T(2,128)S(1)}, f32[4,2,256]{2,1,0:T(2,128)S(1)}, u32[]{:S(2)}, u32[]{:S(2)}) collective-permute-start(f32[4,2,256]{2,1,0:T(2,128)S(1)} %maximum_select_fusion.4), channel_id=1, source_target_pairs={{0,256},{8,264},{16,272},{24,280},{32,288},{40,296},{48,304},{56,3... | collective-permute-start | bytes 24584 | tf_op jit(solution)/shard_map/ppermute | solution.py:75
  45.9 1.0 collective-permute-done.3
  47.0 2.5 copy.30
  49.5 13.1 %all-to-all-start = ((f32[1,16,256,128]{3,1,0,2:T(8,128)}), f32[1,16,256,128]{3,1,0,2:T(8,128)}, u32[]{:S(2)}, u32[]{:S(2)}) async-start(f32[1,16,256,128]{3,1,0,2:T(8,128)} %copy.30), calls=%async_computation | async-start | bytes 4194304 | tf_op jit(solution)/shard_map/all_to_all | solution.py:145
  62.7 0.3 fusion.64
  62.9 7.7 %collective-permute-start.6 = (f32[8,2,256]{2,1,0:T(2,128)S(1)}, f32[8,2,256]{2,1,0:T(2,128)S(1)}, u32[]{:S(2)}, u32[]{:S(2)}) collective-permute-start(f32[8,2,256]{2,1,0:T(2,128)S(1)} %maximum_select_fusion.3), channel_id=1, source_target_pairs={{0,8},{8,0},{16,24},{24,16},{32,40},{40,32},{48,56},{56,48},{64,72... | collective-permute-start | bytes 49160 | tf_op jit(solution)/shard_map/ppermute | solution.py:75
  70.7 0.8 collective-permute-done.6
  71.5 4.4 %collective-permute-start.7 = (f32[16,2,256]{2,1,0:T(2,128)S(1)}, f32[16,2,256]{2,1,0:T(2,128)S(1)}, u32[]{:S(2)}, u32[]{:S(2)}) collective-permute-start(f32[16,2,256]{2,1,0:T(2,128)S(1)} %maximum_select_fusion.2), channel_id=1, source_target_pairs={{0,16},{8,24},{16,0},{24,8},{32,48},{40,56},{48,32},{56,40},{64,80... | collective-permute-start | bytes 98312 | tf_op jit(solution)/shard_map/ppermute | solution.py:75
  75.9 0.7 broadcast_add_fusion
  76.6 1.0 collective-permute-done.7
  77.6 2.7 %collective-permute-start.8 = (f32[32,2,256]{2,1,0:T(2,128)S(1)}, f32[32,2,256]{2,1,0:T(2,128)S(1)}, u32[]{:S(2)}, u32[]{:S(2)}) collective-permute-start(f32[32,2,256]{2,1,0:T(2,128)S(1)} %maximum_select_fusion.1), channel_id=1, source_target_pairs={{0,32},{8,40},{16,48},{24,56},{32,0},{40,8},{48,16},{56,24},{64,96... | collective-permute-start | bytes 196616 | tf_op jit(solution)/shard_map/ppermute | solution.py:75
  80.6 3.5 %collective-permute-done.8 = f32[32,2,256]{2,1,0:T(2,128)S(1)} collective-permute-done((f32[32,2,256]{2,1,0:T(2,128)S(1)}, f32[32,2,256]{2,1,0:T(2,128)S(1)}, u32[]{:S(2)}, u32[]{:S(2)}) %collective-permute-start.8) | collective-permute-done | bytes 65568 | tf_op jit(solution)/shard_map/ppermute | solution.py:75
  84.2 2.1 collective-permute-start.9
  86.5 0.6 iota_add_fusion
  87.1 3.2 %collective-permute-done.9 = f32[64,2,256]{2,1,0:T(2,128)S(1)} collective-permute-done((f32[64,2,256]{2,1,0:T(2,128)S(1)}, f32[64,2,256]{2,1,0:T(2,128)S(1)}, u32[]{:S(2)}, u32[]{:S(2)}) %collective-permute-start.9) | collective-permute-done | bytes 131104 | tf_op jit(solution)/shard_map/ppermute | solution.py:67
  90.4 3.3 %collective-permute-start.10 = (f32[64,2,256]{2,1,0:T(2,128)S(1)}, f32[64,2,256]{2,1,0:T(2,128)}, u32[]{:S(2)}, u32[]{:S(2)}) collective-permute-start(f32[64,2,256]{2,1,0:T(2,128)S(1)} %bitcast_add_fusion), channel_id=1, source_target_pairs={{0,2},{1,3},{2,0},{3,1},{4,6},{5,7},{6,4},{7,5},{8,10},{9,11},{10,... | collective-permute-start | bytes 393224 | tf_op jit(solution)/shard_map/ppermute | solution.py:67
  93.7 0.6 multiply_multiply_fusion.1
  94.3 4.9 %collective-permute-done.10 = f32[64,2,256]{2,1,0:T(2,128)} collective-permute-done((f32[64,2,256]{2,1,0:T(2,128)S(1)}, f32[64,2,256]{2,1,0:T(2,128)}, u32[]{:S(2)}, u32[]{:S(2)}) %collective-permute-start.10) | collective-permute-done | bytes 131104 | tf_op jit(solution)/shard_map/ppermute | solution.py:67
  99.2 1.0 add.203
  100.3 0.4 fusion.42
  100.7 2.1 convolution_divide_fusion
  102.8 2.1 fusion.17
  105.0 4.5 %fusion.4 = f32[1,64,32]{2,0,1:T(1,128)S(1)} fusion(f32[256,1,1]{0,1,2:T(1,128)S(1)} %bitcast.87, s32[64,32]{1,0:T(8,128)S(1)} %copy-done.2, s32[64,32]{1,0:T(8,128)S(1)} %get-tuple-element.23), kind=kOutput, calls=%fused_computation.10 | convolution fusion | flops 8912896 | bytes 25600 | tf_op jit(solution)/shard_map/dot_general | solution.py:47
  109.7 78.8 %all-to-all-done = f32[1,16,256,128]{3,1,0,2:T(8,128)} async-done(((f32[1,16,256,128]{3,1,0,2:T(8,128)}), f32[1,16,256,128]{3,1,0,2:T(8,128)}, u32[]{:S(2)}, u32[]{:S(2)}) %all-to-all-start) | async-done | bytes 2097184 | tf_op jit(solution)/shard_map/all_to_all | solution.py:145
  188.5 2.2 copy.31
  190.8 2.6 fusion.1
  193.4 2.4 fusion.38
  195.8 3.1 %copy.33 = f32[1,128,32,128]{3,2,0,1:T(8,128)} copy(f32[1,128,32,128]{1,3,2,0:T(8,128)} %bitcast.77) | data formatting | bytes 4194304 | tf_op jit(solution)/shard_map/reshape | solution.py:159
  198.9 4.7 %all-to-all-start.1 = ((f32[1,128,32,128]{3,2,0,1:T(8,128)}), f32[1,128,32,128]{3,2,0,1:T(8,128)}, u32[]{:S(2)}, u32[]{:S(2)}) async-start(f32[1,128,32,128]{3,2,0,1:T(8,128)} %copy.33), calls=%async_computation.1 | async-start | bytes 4194304 | tf_op jit(solution)/shard_map/all_to_all | solution.py:160
  203.7 0.4 fusion.106
  204.3 1.9 fusion.52
  206.2 3.1 %convolution_add_fusion = f32[4096,128]{1,0:T(8,128)S(1)} fusion(f32[4096,128]{1,0:T(8,128)S(1)} %fusion.52, f32[4096,64]{0,1:T(8,128)} %collective-permute-done.4, s32[128]{0:T(128)S(1)} %add_reduce_fusion.1, pred[128]{0:T(512)(128)(4,1)S(1)} %get-tuple-element.32), kind=kOutput, calls=%fused_computation | convolution fusion | flops 403193856 | bytes 5243520 | tf_op jit(solution)/shard_map/dot_general | solution.py:162
  209.3 3.0 %multiply_add_fusion.1 = f32[1,16,256,128]{3,2,1,0:T(8,128)} fusion(f32[1,16,256,128]{3,2,1,0:T(8,128)S(1)} %copy-done, f32[1,16,255,128]{3,2,1,0:T(8,128)S(1)} %get-tuple-element.20, f32[1,16,255,128]{3,2,1,0:T(8,128)S(1)} %get-tuple-element.19, f32[1,16,256,128]{3,2,1,0:T(8,128)S(1)} %bitcast.78, f32[16,128]{1,0:T(8,128)S(1)} %copy-done.3, ...), kind=kLoop, calls=%fused_computation.9 | loop fusion | flops 6291456 | bytes 10480208 | tf_op jit(solution)/shard_map/add | solution.py:179
  212.3 51.5 %all-to-all-done.1 = f32[1,128,32,128]{3,2,0,1:T(8,128)} async-done(((f32[1,128,32,128]{3,2,0,1:T(8,128)}), f32[1,128,32,128]{3,2,0,1:T(8,128)}, u32[]{:S(2)}, u32[]{:S(2)}) %all-to-all-start.1) | async-done | bytes 2097184 | tf_op jit(solution)/shard_map/all_to_all | solution.py:160
  263.8 2.0 copy.34
  266.1 1.6 multiply_add_fusion
  (60 shorter events, 2.8 us)
Async XLA Ops:
  0.0 9.2 %copy-start = (f32[1,16,256,128]{3,2,1,0:T(8,128)S(1)}, f32[1,16,256,128]{3,2,1,0:T(8,128)}, u32[]{:S(2)}) copy-start(f32[1,16,256,128]{3,2,1,0:T(8,128)} %param.7) | copy-start | bytes 6291460
  0.8 8.4 %copy-start.4 = (pred[128]{0:T(512)(128)(4,1)}, pred[128]{0:T(512)(128)(4,1)S(1)}, u32[]{:S(2)}) copy-start(pred[128]{0:T(512)(128)(4,1)S(1)} %get-tuple-element.29) | copy-start | bytes 388
  5.2 41.8 %collective-permute-start.4 = (f32[4096,64]{0,1:T(8,128)}, f32[4096,64]{0,1:T(8,128)}, u32[]{:S(2)}, u32[]{:S(2)}) collective-permute-start(f32[4096,64]{0,1:T(8,128)} %convolution_bitcast_fusion.2), channel_id=1, source_target_pairs={{0,8},{8,16},{16,24},{24,32},{32,40},{40,48},{48,56},{56,64},{64,7... | collective-permute-start | bytes 3145736 | tf_op jit(solution)/shard_map/ppermute | solution.py:123
  9.3 4.5 %copy-start.7 = (s32[1,256]{1,0:T(1,128)S(1)}, s32[1,256]{1,0:T(1,128)}, u32[]{:S(2)}) copy-start(s32[1,256]{1,0:T(1,128)} %param.8) | copy-start | bytes 3076
  9.3 4.5 %copy-start.8 = (f32[6]{0:T(128)S(1)}, f32[6]{0:T(128)}, u32[]{:S(2)}) copy-start(f32[6]{0:T(128)} %param.10) | copy-start | bytes 76
  9.3 4.5 %copy-start.9 = (f32[6]{0:T(128)S(1)}, f32[6]{0:T(128)}, u32[]{:S(2)}) copy-start(f32[6]{0:T(128)} %param.9) | copy-start | bytes 76
  11.6 35.3 %collective-permute-start.5 = (f32[4096,64]{0,1:T(8,128)}, f32[4096,64]{0,1:T(8,128)S(1)}, u32[]{:S(2)}, u32[]{:S(2)}) collective-permute-start(f32[4096,64]{0,1:T(8,128)} %convolution_bitcast_fusion.1), channel_id=1, source_target_pairs={{8,0},{16,8},{24,16},{32,24},{40,32},{48,40},{56,48},{64,56},{72,6... | collective-permute-start | bytes 3145736 | tf_op jit(solution)/shard_map/ppermute | solution.py:124
  14.5 13.7 %collective-permute-start = (f32[1,2,256]{2,1,0:T(2,128)S(1)}, f32[1,2,256]{2,1,0:T(2,128)S(1)}, u32[]{:S(2)}, u32[]{:S(2)}) collective-permute-start(f32[1,2,256]{2,1,0:T(2,128)S(1)} %pad_maximum_fusion), channel_id=1, source_target_pairs={{0,4},{1,5},{2,6},{3,7},{4,0},{5,1},{6,2},{7,3},{8,12},{9,13},{10,... | collective-permute-start | bytes 6152 | tf_op jit(solution)/shard_map/ppermute | solution.py:67
  28.2 4.3 %collective-permute-start.1 = (f32[1,2,256]{2,1,0:T(2,128)S(1)}, f32[1,2,256]{2,1,0:T(2,128)S(1)}, u32[]{:S(2)}, u32[]{:S(2)}) collective-permute-start(f32[1,2,256]{2,1,0:T(2,128)S(1)} %fusion.104), channel_id=1, source_target_pairs={{0,64},{8,72},{16,80},{24,88},{32,96},{40,104},{48,112},{56,120},{... | collective-permute-start | bytes 6152 | tf_op jit(solution)/shard_map/ppermute | solution.py:75
  32.5 5.2 %collective-permute-start.2 = (f32[2,2,256]{2,1,0:T(2,128)S(1)}, f32[2,2,256]{2,1,0:T(2,128)S(1)}, u32[]{:S(2)}, u32[]{:S(2)}) collective-permute-start(f32[2,2,256]{2,1,0:T(2,128)S(1)} %maximum_select_fusion.5), channel_id=1, source_target_pairs={{0,128},{8,136},{16,144},{24,152},{32,160},{40,168},{48,176},{56,1... | collective-permute-start | bytes 12296 | tf_op jit(solution)/shard_map/ppermute | solution.py:75
  37.8 9.2 %collective-permute-start.3 = (f32[4,2,256]{2,1,0:T(2,128)S(1)}, f32[4,2,256]{2,1,0:T(2,128)S(1)}, u32[]{:S(2)}, u32[]{:S(2)}) collective-permute-start(f32[4,2,256]{2,1,0:T(2,128)S(1)} %maximum_select_fusion.4), channel_id=1, source_target_pairs={{0,256},{8,264},{16,272},{24,280},{32,288},{40,296},{48,304},{56,3... | collective-permute-start | bytes 24584 | tf_op jit(solution)/shard_map/ppermute | solution.py:75
  49.5 139.0 %all-to-all-start = ((f32[1,16,256,128]{3,1,0,2:T(8,128)}), f32[1,16,256,128]{3,1,0,2:T(8,128)}, u32[]{:S(2)}, u32[]{:S(2)}) async-start(f32[1,16,256,128]{3,1,0,2:T(8,128)} %copy.30), calls=%async_computation | async-start | bytes 4194304 | tf_op jit(solution)/shard_map/all_to_all | solution.py:145
  62.9 8.5 %collective-permute-start.6 = (f32[8,2,256]{2,1,0:T(2,128)S(1)}, f32[8,2,256]{2,1,0:T(2,128)S(1)}, u32[]{:S(2)}, u32[]{:S(2)}) collective-permute-start(f32[8,2,256]{2,1,0:T(2,128)S(1)} %maximum_select_fusion.3), channel_id=1, source_target_pairs={{0,8},{8,0},{16,24},{24,16},{32,40},{40,32},{48,56},{56,48},{64,72... | collective-permute-start | bytes 49160 | tf_op jit(solution)/shard_map/ppermute | solution.py:75
  71.5 6.1 %collective-permute-start.7 = (f32[16,2,256]{2,1,0:T(2,128)S(1)}, f32[16,2,256]{2,1,0:T(2,128)S(1)}, u32[]{:S(2)}, u32[]{:S(2)}) collective-permute-start(f32[16,2,256]{2,1,0:T(2,128)S(1)} %maximum_select_fusion.2), channel_id=1, source_target_pairs={{0,16},{8,24},{16,0},{24,8},{32,48},{40,56},{48,32},{56,40},{64,80... | collective-permute-start | bytes 98312 | tf_op jit(solution)/shard_map/ppermute | solution.py:75
  77.6 6.5 %collective-permute-start.8 = (f32[32,2,256]{2,1,0:T(2,128)S(1)}, f32[32,2,256]{2,1,0:T(2,128)S(1)}, u32[]{:S(2)}, u32[]{:S(2)}) collective-permute-start(f32[32,2,256]{2,1,0:T(2,128)S(1)} %maximum_select_fusion.1), channel_id=1, source_target_pairs={{0,32},{8,40},{16,48},{24,56},{32,0},{40,8},{48,16},{56,24},{64,96... | collective-permute-start | bytes 196616 | tf_op jit(solution)/shard_map/ppermute | solution.py:75
  84.2 6.1 %collective-permute-start.9 = (f32[64,2,256]{2,1,0:T(2,128)S(1)}, f32[64,2,256]{2,1,0:T(2,128)S(1)}, u32[]{:S(2)}, u32[]{:S(2)}) collective-permute-start(f32[64,2,256]{2,1,0:T(2,128)S(1)} %bitcast.79), channel_id=1, source_target_pairs={{0,1},{1,0},{2,3},{3,2},{4,5},{5,4},{6,7},{7,6},{8,9},{9,8},{10,11... | collective-permute-start | bytes 393224 | tf_op jit(solution)/shard_map/ppermute | solution.py:67
  90.4 8.8 %collective-permute-start.10 = (f32[64,2,256]{2,1,0:T(2,128)S(1)}, f32[64,2,256]{2,1,0:T(2,128)}, u32[]{:S(2)}, u32[]{:S(2)}) collective-permute-start(f32[64,2,256]{2,1,0:T(2,128)S(1)} %bitcast_add_fusion), channel_id=1, source_target_pairs={{0,2},{1,3},{2,0},{3,1},{4,6},{5,7},{6,4},{7,5},{8,10},{9,11},{10,... | collective-permute-start | bytes 393224 | tf_op jit(solution)/shard_map/ppermute | solution.py:67
  94.3 10.7 %copy-start.2 = (s32[64,32]{1,0:T(8,128)S(1)}, s32[64,32]{1,0:T(8,128)}, u32[]{:S(2)}) copy-start(s32[64,32]{1,0:T(8,128)} %get-tuple-element.24) | copy-start | bytes 24580
  198.9 4.7 %copy-start.10 = (f32[128]{0:T(128)S(1)}, f32[128]{0:T(128)}, u32[]{:S(2)}) copy-start(f32[128]{0:T(128)} %param.12) | copy-start | bytes 1540
  198.9 64.9 %all-to-all-start.1 = ((f32[1,128,32,128]{3,2,0,1:T(8,128)}), f32[1,128,32,128]{3,2,0,1:T(8,128)}, u32[]{:S(2)}, u32[]{:S(2)}) async-start(f32[1,128,32,128]{3,2,0,1:T(8,128)} %copy.33), calls=%async_computation.1 | async-start | bytes 4194304 | tf_op jit(solution)/shard_map/all_to_all | solution.py:160
  203.6 0.6 copy-start.5
  206.1 3.2 %copy-start.3 = (f32[16,128]{1,0:T(8,128)S(1)}, f32[16,128]{1,0:T(8,128)}, u32[]{:S(2)}) copy-start(f32[16,128]{1,0:T(8,128)} %param.11) | copy-start | bytes 24580
  206.2 3.2 %copy-start.6 = (f32[256]{0:T(256)S(1)}, f32[256]{0:T(256)}, u32[]{:S(2)}) copy-start(f32[256]{0:T(256)} %get-tuple-element.17) | copy-start | bytes 3076
  263.8 2.2 copy-start.1

commit v9 on v8

--- a/solution.py
+++ b/solution.py
@@ -86,6 +86,17 @@
     order = sorted(range(levels), key=lambda axis: -bits[levels - 1 - axis])
     shaped = jnp.transpose(shaped, order + list(range(levels, shaped.ndim)))
     return shaped.reshape((count,) + value.shape[1:])
+
+
+def select_exactly(values, picker):
+    top = values.astype(jnp.bfloat16)
+    remainder = values - top.astype(jnp.float32)
+    middle = remainder.astype(jnp.bfloat16)
+    rest = (remainder - middle.astype(jnp.float32)).astype(jnp.bfloat16)
+    picker = picker.astype(jnp.bfloat16)
+    total = jnp.dot(top, picker, preferred_element_type=jnp.float32)
+    total = total + jnp.dot(middle, picker, preferred_element_type=jnp.float32)
+    return total + jnp.dot(rest, picker, preferred_element_type=jnp.float32)
 
 
 def shards(distribution, region, region_doping, region_relax, equilibrium, kx_speed, upwind_sign):
@@ -116,8 +127,8 @@
     pick_pos = (positive_kx[:, None] & (rank_pos[:, None] == slots[None, :])).astype(jnp.float32)
     pick_neg = ((~positive_kx)[:, None] & (rank_neg[:, None] == slots[None, :])).astype(jnp.float32)
     flat = distribution.reshape(-1, kx_count)
-    send_right = jnp.dot(flat, pick_pos, precision=precise)
-    send_left = jnp.dot(flat, pick_neg, precision=precise)
+    send_right = select_exactly(flat, pick_pos)
+    send_left = select_exactly(flat, pick_neg)
     forward_pairs = [(i, i + 1) for i in range(space_count - 1)]
     backward_pairs = [(i + 1, i) for i in range(space_count - 1)]
     got_left = lax.ppermute(send_right, "space", forward_pairs)

time: 268 us -> 272 us (1.015)
  the two profiles are of different devices: /device:TPU:123 before, /device:TPU:158 now
where the time goes in v9:
time: 272 us
  starting transfers between devices  128 us (47%)
  waiting for transfers between devices  96.8 us (36%)
  matrix products  23.5 us (9%)
  local copies, waits for them, and re-layouts  13 us (5%)
  other arithmetic  10.3 us (4%)
    all_to_all x1, starting transfers between devices, shards(): lax.all_to_all(mixed, 'ky', split_axis=1, concat_axis=2, tiled=True)  72.2 us
    all_to_all x1, waiting for transfers between devices, shards(): spread = lax.all_to_all(held, 'ky', split_axis=2, concat_axis=1, tiled=True)  36.7 us
    all_to_all x1, waiting for transfers between devices, shards(): lax.all_to_all(mixed, 'ky', split_axis=1, concat_axis=2, tiled=True)  29.8 us
    ppermute x6, starting transfers between devices, gather_rows(): other = lax.ppermute(value, axis, xor_pairs(count, bit))  21.9 us
    ppermute x3, starting transfers between devices, sum_over(): value = value + lax.ppermute(value, axis, xor_pairs(count, bit))  17.2 us
    ppermute x6, waiting for transfers between devices, gather_rows(): other = lax.ppermute(value, axis, xor_pairs(count, bit))  16.7 us
    ppermute x3, waiting for transfers between devices, sum_over(): value = value + lax.ppermute(value, axis, xor_pairs(count, bit))  13.6 us
    all_to_all x1, starting transfers between devices, shards(): spread = lax.all_to_all(held, 'ky', split_axis=2, concat_axis=1, tiled=True)  12 us
  transfers between devices with their start and end apart: 13, of which 11 were waited for; matrix products, arithmetic and copies ran while one was open for 8% of the time, Pallas kernels for 0%

profile of v9, /device:TPU:158, one launch (start us, length us, event | category | flops | bytes accessed | tf_op | source)
XLA Modules:
  0.0 271.7 jit_solution(10525629452996431279)
XLA Ops:
  0.0 2.1 bitcast_convert_fusion
  2.2 1.6 subtract_convert_fusion
  4.3 0.6 convolution_bitcast_fusion.1
  4.9 0.5 copy-done.3
  5.4 0.6 convolution_add_fusion.2
  6.2 1.6 convolution_add_fusion.1
  7.7 2.2 collective-permute-start.5
  10.3 0.6 convolution_bitcast_fusion.2
  10.9 0.5 copy-done.4
  11.4 0.6 convolution_add_fusion.4
  12.0 0.6 copy-done.2
  12.7 0.6 convolution_add_fusion.3
  13.3 2.2 collective-permute-start.4
  15.6 10.9 %collective-permute-start = (f32[1,2,256]{2,1,0:T(2,128)S(1)}, f32[1,2,256]{2,1,0:T(2,128)S(1)}, u32[]{:S(2)}, u32[]{:S(2)}) collective-permute-start(f32[1,2,256]{2,1,0:T(2,128)S(1)} %pad_maximum_fusion), channel_id=1, source_target_pairs={{0,4},{1,5},{2,6},{3,7},{4,0},{5,1},{6,2},{7,3},{8,12},{9,13},{10,... | collective-permute-start | bytes 6152 | tf_op jit(solution)/shard_map/ppermute | solution.py:67
  26.5 3.3 %collective-permute-done = f32[1,2,256]{2,1,0:T(2,128)S(1)} collective-permute-done((f32[1,2,256]{2,1,0:T(2,128)S(1)}, f32[1,2,256]{2,1,0:T(2,128)S(1)}, u32[]{:S(2)}, u32[]{:S(2)}) %collective-permute-start) | collective-permute-done | bytes 2080 | tf_op jit(solution)/shard_map/ppermute | solution.py:67
  29.9 3.7 %collective-permute-start.1 = (f32[1,2,256]{2,1,0:T(2,128)S(1)}, f32[1,2,256]{2,1,0:T(2,128)S(1)}, u32[]{:S(2)}, u32[]{:S(2)}) collective-permute-start(f32[1,2,256]{2,1,0:T(2,128)S(1)} %fusion.109), channel_id=1, source_target_pairs={{0,64},{8,72},{16,80},{24,88},{32,96},{40,104},{48,112},{56,120},{... | collective-permute-start | bytes 6152 | tf_op jit(solution)/shard_map/ppermute | solution.py:75
  33.6 1.7 collective-permute-done.1
  35.4 6.0 %collective-permute-start.2 = (f32[2,2,256]{2,1,0:T(2,128)S(1)}, f32[2,2,256]{2,1,0:T(2,128)S(1)}, u32[]{:S(2)}, u32[]{:S(2)}) collective-permute-start(f32[2,2,256]{2,1,0:T(2,128)S(1)} %maximum_select_fusion.5), channel_id=1, source_target_pairs={{0,128},{8,136},{16,144},{24,152},{32,160},{40,168},{48,176},{56,1... | collective-permute-start | bytes 12296 | tf_op jit(solution)/shard_map/ppermute | solution.py:75
  41.3 1.6 collective-permute-done.2
  42.9 2.6 collective-permute-start.3
  45.5 6.8 %collective-permute-done.3 = f32[4,2,256]{2,1,0:T(2,128)S(1)} collective-permute-done((f32[4,2,256]{2,1,0:T(2,128)S(1)}, f32[4,2,256]{2,1,0:T(2,128)S(1)}, u32[]{:S(2)}, u32[]{:S(2)}) %collective-permute-start.3) | collective-permute-done | bytes 8224 | tf_op jit(solution)/shard_map/ppermute | solution.py:75
  52.4 2.5 copy.30
  54.9 12.0 %all-to-all-start = ((f32[1,16,256,128]{3,1,0,2:T(8,128)}), f32[1,16,256,128]{3,1,0,2:T(8,128)}, u32[]{:S(2)}, u32[]{:S(2)}) async-start(f32[1,16,256,128]{3,1,0,2:T(8,128)} %copy.30), calls=%async_computation | async-start | bytes 4194304 | tf_op jit(solution)/shard_map/all_to_all | solution.py:156
  67.2 1.9 collective-permute-start.6
  69.2 1.1 collective-permute-done.6
  70.3 2.6 collective-permute-start.7
  73.0 3.1 %collective-permute-done.7 = f32[16,2,256]{2,1,0:T(2,128)S(1)} collective-permute-done((f32[16,2,256]{2,1,0:T(2,128)S(1)}, f32[16,2,256]{2,1,0:T(2,128)S(1)}, u32[]{:S(2)}, u32[]{:S(2)}) %collective-permute-start.7) | collective-permute-done | bytes 32800 | tf_op jit(solution)/shard_map/ppermute | solution.py:75
  76.2 5.1 %collective-permute-start.8 = (f32[32,2,256]{2,1,0:T(2,128)S(1)}, f32[32,2,256]{2,1,0:T(2,128)S(1)}, u32[]{:S(2)}, u32[]{:S(2)}) collective-permute-start(f32[32,2,256]{2,1,0:T(2,128)S(1)} %maximum_select_fusion.1), channel_id=1, source_target_pairs={{0,32},{8,40},{16,48},{24,56},{32,0},{40,8},{48,16},{56,24},{64,96... | collective-permute-start | bytes 196616 | tf_op jit(solution)/shard_map/ppermute | solution.py:75
  81.5 2.4 collective-permute-done.8
  83.9 2.8 %collective-permute-start.9 = (f32[64,2,256]{2,1,0:T(2,128)S(1)}, f32[64,2,256]{2,1,0:T(2,128)S(1)}, u32[]{:S(2)}, u32[]{:S(2)}) collective-permute-start(f32[64,2,256]{2,1,0:T(2,128)S(1)} %bitcast.93), channel_id=1, source_target_pairs={{0,1},{1,0},{2,3},{3,2},{4,5},{5,4},{6,7},{7,6},{8,9},{9,8},{10,11... | collective-permute-start | bytes 393224 | tf_op jit(solution)/shard_map/ppermute | solution.py:67
  86.9 3.9 %collective-permute-done.9 = f32[64,2,256]{2,1,0:T(2,128)S(1)} collective-permute-done((f32[64,2,256]{2,1,0:T(2,128)S(1)}, f32[64,2,256]{2,1,0:T(2,128)S(1)}, u32[]{:S(2)}, u32[]{:S(2)}) %collective-permute-start.9) | collective-permute-done | bytes 131104 | tf_op jit(solution)/shard_map/ppermute | solution.py:67
  90.9 3.5 %collective-permute-start.10 = (f32[64,2,256]{2,1,0:T(2,128)S(1)}, f32[64,2,256]{2,1,0:T(2,128)S(1)}, u32[]{:S(2)}, u32[]{:S(2)}) collective-permute-start(f32[64,2,256]{2,1,0:T(2,128)S(1)} %bitcast_add_fusion), channel_id=1, source_target_pairs={{0,2},{1,3},{2,0},{3,1},{4,6},{5,7},{6,4},{7,5},{8,10},{9,11},{10,... | collective-permute-start | bytes 393224 | tf_op jit(solution)/shard_map/ppermute | solution.py:67
  94.5 6.3 %collective-permute-done.10 = f32[64,2,256]{2,1,0:T(2,128)S(1)} collective-permute-done((f32[64,2,256]{2,1,0:T(2,128)S(1)}, f32[64,2,256]{2,1,0:T(2,128)S(1)}, u32[]{:S(2)}, u32[]{:S(2)}) %collective-permute-start.10) | collective-permute-done | bytes 131104 | tf_op jit(solution)/shard_map/ppermute | solution.py:67
  101.4 1.3 convolution_divide_fusion
  102.8 1.3 fusion.18
  104.3 4.5 %fusion.4 = f32[1,64,32]{2,0,1:T(1,128)S(1)} fusion(f32[256,1,1]{0,1,2:T(1,128)S(1)} %bitcast.101, s32[64,32]{1,0:T(8,128)S(1)} %get-tuple-element.28, s32[64,32]{1,0:T(8,128)S(1)} %get-tuple-element.27), kind=kOutput, calls=%fused_computation.16 | convolution fusion | flops 8912896 | bytes 25600 | tf_op jit(solution)/shard_map/dot_general | solution.py:47
  109.0 36.7 %all-to-all-done = f32[1,16,256,128]{3,1,0,2:T(8,128)} async-done(((f32[1,16,256,128]{3,1,0,2:T(8,128)}), f32[1,16,256,128]{3,1,0,2:T(8,128)}, u32[]{:S(2)}, u32[]{:S(2)}) %all-to-all-start) | async-done | bytes 2097184 | tf_op jit(solution)/shard_map/all_to_all | solution.py:156
  145.7 2.2 copy.31
  148.1 2.6 fusion.1
  150.7 2.4 fusion.39
  153.1 3.1 %copy.33 = f32[1,128,32,128]{3,2,0,1:T(8,128)} copy(f32[1,128,32,128]{1,3,2,0:T(8,128)} %bitcast.91) | data formatting | bytes 4194304 | tf_op jit(solution)/shard_map/reshape | solution.py:170
  156.2 72.2 %all-to-all-start.1 = ((f32[1,128,32,128]{3,2,0,1:T(8,128)}), f32[1,128,32,128]{3,2,0,1:T(8,128)}, u32[]{:S(2)}, u32[]{:S(2)}) async-start(f32[1,128,32,128]{3,2,0,1:T(8,128)} %copy.33), calls=%async_computation.1 | async-start | bytes 4194304 | tf_op jit(solution)/shard_map/all_to_all | solution.py:171
  228.8 3.1 %fusion.52 = f32[4096,128]{1,0:T(8,128)S(1)} fusion(f32[4096,64]{0,1:T(8,128)} %collective-permute-done.5, s32[128]{0:T(128)S(1)} %add_reduce_fusion, pred[128]{0:T(512)(128)(4,1)S(1)} %get-tuple-element.33), kind=kOutput, calls=%fused_computation.79 | convolution fusion | flops 402669568 | bytes 3146368 | tf_op jit(solution)/shard_map/dot_general | solution.py:173
  231.9 3.1 %convolution_add_fusion = f32[4096,128]{1,0:T(8,128)S(1)} fusion(f32[4096,128]{1,0:T(8,128)S(1)} %fusion.52, f32[4096,64]{0,1:T(8,128)} %collective-permute-done.4, s32[128]{0:T(128)S(1)} %add_reduce_fusion.1, pred[128]{0:T(512)(128)(4,1)S(1)} %get-tuple-element.36), kind=kOutput, calls=%fused_computation | convolution fusion | flops 403193856 | bytes 5243520 | tf_op jit(solution)/shard_map/dot_general | solution.py:173
  235.1 3.0 %multiply_add_fusion.1 = f32[1,16,256,128]{3,2,1,0:T(8,128)} fusion(f32[1,16,256,128]{3,2,1,0:T(8,128)S(1)} %copy-done, f32[1,16,255,128]{3,2,1,0:T(8,128)S(1)} %get-tuple-element.20, f32[1,16,255,128]{3,2,1,0:T(8,128)S(1)} %get-tuple-element.19, f32[1,16,256,128]{3,2,1,0:T(8,128)S(1)} %bitcast.92, f32[16,128]{1,0:T(8,128)S(1)} %copy-done.6, ...), kind=kLoop, calls=%fused_computation.15 | loop fusion | flops 6291456 | bytes 10480208 | tf_op jit(solution)/shard_map/add | solution.py:190
  238.0 29.8 %all-to-all-done.1 = f32[1,128,32,128]{3,2,0,1:T(8,128)} async-done(((f32[1,128,32,128]{3,2,0,1:T(8,128)}), f32[1,128,32,128]{3,2,0,1:T(8,128)}, u32[]{:S(2)}, u32[]{:S(2)}) %all-to-all-start.1) | async-done | bytes 2097184 | tf_op jit(solution)/shard_map/all_to_all | solution.py:171
  267.9 2.0 copy.34
  270.1 1.6 multiply_add_fusion
  (67 shorter events, 4.1 us)
Async XLA Ops:
  0.0 2.2 copy-start
  2.2 1.6 copy-start.8
  4.2 1.2 copy-start.3
  4.9 1.3 copy-start.1
  7.7 44.6 %collective-permute-start.5 = (f32[4096,64]{0,1:T(8,128)}, f32[4096,64]{0,1:T(8,128)}, u32[]{:S(2)}, u32[]{:S(2)}) collective-permute-start(f32[4096,64]{0,1:T(8,128)} %convolution_add_fusion.1), channel_id=1, source_target_pairs={{8,0},{16,8},{24,16},{32,24},{40,32},{48,40},{56,48},{64,56},{72,6... | collective-permute-start | bytes 3145736 | tf_op jit(solution)/shard_map/ppermute | solution.py:135
  10.2 1.2 copy-start.4
  11.4 1.2 copy-start.2
  12.7 2.8 %copy-start.7 = (s32[1,256]{1,0:T(1,128)S(1)}, s32[1,256]{1,0:T(1,128)}, u32[]{:S(2)}) copy-start(s32[1,256]{1,0:T(1,128)} %param.8) | copy-start | bytes 3076
  12.7 2.8 %copy-start.9 = (f32[6]{0:T(128)S(1)}, f32[6]{0:T(128)}, u32[]{:S(2)}) copy-start(f32[6]{0:T(128)} %param.10) | copy-start | bytes 76
  12.7 2.8 %copy-start.10 = (f32[6]{0:T(128)S(1)}, f32[6]{0:T(128)}, u32[]{:S(2)}) copy-start(f32[6]{0:T(128)} %param.9) | copy-start | bytes 76
  13.3 39.1 %collective-permute-start.4 = (f32[4096,64]{0,1:T(8,128)S(1)}, f32[4096,64]{0,1:T(8,128)}, u32[]{:S(2)}, u32[]{:S(2)}) collective-permute-start(f32[4096,64]{0,1:T(8,128)S(1)} %convolution_add_fusion.3), channel_id=1, source_target_pairs={{0,8},{8,16},{16,24},{24,32},{32,40},{40,48},{48,56},{56,64},{64,7... | collective-permute-start | bytes 3145736 | tf_op jit(solution)/shard_map/ppermute | solution.py:134
  15.6 14.3 %collective-permute-start = (f32[1,2,256]{2,1,0:T(2,128)S(1)}, f32[1,2,256]{2,1,0:T(2,128)S(1)}, u32[]{:S(2)}, u32[]{:S(2)}) collective-permute-start(f32[1,2,256]{2,1,0:T(2,128)S(1)} %pad_maximum_fusion), channel_id=1, source_target_pairs={{0,4},{1,5},{2,6},{3,7},{4,0},{5,1},{6,2},{7,3},{8,12},{9,13},{10,... | collective-permute-start | bytes 6152 | tf_op jit(solution)/shard_map/ppermute | solution.py:67
  29.9 5.5 %collective-permute-start.1 = (f32[1,2,256]{2,1,0:T(2,128)S(1)}, f32[1,2,256]{2,1,0:T(2,128)S(1)}, u32[]{:S(2)}, u32[]{:S(2)}) collective-permute-start(f32[1,2,256]{2,1,0:T(2,128)S(1)} %fusion.109), channel_id=1, source_target_pairs={{0,64},{8,72},{16,80},{24,88},{32,96},{40,104},{48,112},{56,120},{... | collective-permute-start | bytes 6152 | tf_op jit(solution)/shard_map/ppermute | solution.py:75
  35.4 7.5 %collective-permute-start.2 = (f32[2,2,256]{2,1,0:T(2,128)S(1)}, f32[2,2,256]{2,1,0:T(2,128)S(1)}, u32[]{:S(2)}, u32[]{:S(2)}) collective-permute-start(f32[2,2,256]{2,1,0:T(2,128)S(1)} %maximum_select_fusion.5), channel_id=1, source_target_pairs={{0,128},{8,136},{16,144},{24,152},{32,160},{40,168},{48,176},{56,1... | collective-permute-start | bytes 12296 | tf_op jit(solution)/shard_map/ppermute | solution.py:75
  42.9 9.4 %collective-permute-start.3 = (f32[4,2,256]{2,1,0:T(2,128)S(1)}, f32[4,2,256]{2,1,0:T(2,128)S(1)}, u32[]{:S(2)}, u32[]{:S(2)}) collective-permute-start(f32[4,2,256]{2,1,0:T(2,128)S(1)} %maximum_select_fusion.4), channel_id=1, source_target_pairs={{0,256},{8,264},{16,272},{24,280},{32,288},{40,296},{48,304},{56,3... | collective-permute-start | bytes 24584 | tf_op jit(solution)/shard_map/ppermute | solution.py:75
  54.9 90.8 %all-to-all-start = ((f32[1,16,256,128]{3,1,0,2:T(8,128)}), f32[1,16,256,128]{3,1,0,2:T(8,128)}, u32[]{:S(2)}, u32[]{:S(2)}) async-start(f32[1,16,256,128]{3,1,0,2:T(8,128)} %copy.30), calls=%async_computation | async-start | bytes 4194304 | tf_op jit(solution)/shard_map/all_to_all | solution.py:156
  67.2 3.1 %collective-permute-start.6 = (f32[8,2,256]{2,1,0:T(2,128)S(1)}, f32[8,2,256]{2,1,0:T(2,128)S(1)}, u32[]{:S(2)}, u32[]{:S(2)}) collective-permute-start(f32[8,2,256]{2,1,0:T(2,128)S(1)} %maximum_select_fusion.3), channel_id=1, source_target_pairs={{0,8},{8,0},{16,24},{24,16},{32,40},{40,32},{48,56},{56,48},{64,72... | collective-permute-start | bytes 49160 | tf_op jit(solution)/shard_map/ppermute | solution.py:75
  70.3 5.8 %collective-permute-start.7 = (f32[16,2,256]{2,1,0:T(2,128)S(1)}, f32[16,2,256]{2,1,0:T(2,128)S(1)}, u32[]{:S(2)}, u32[]{:S(2)}) collective-permute-start(f32[16,2,256]{2,1,0:T(2,128)S(1)} %maximum_select_fusion.2), channel_id=1, source_target_pairs={{0,16},{8,24},{16,0},{24,8},{32,48},{40,56},{48,32},{56,40},{64,80... | collective-permute-start | bytes 98312 | tf_op jit(solution)/shard_map/ppermute | solution.py:75
  76.2 7.7 %collective-permute-start.8 = (f32[32,2,256]{2,1,0:T(2,128)S(1)}, f32[32,2,256]{2,1,0:T(2,128)S(1)}, u32[]{:S(2)}, u32[]{:S(2)}) collective-permute-start(f32[32,2,256]{2,1,0:T(2,128)S(1)} %maximum_select_fusion.1), channel_id=1, source_target_pairs={{0,32},{8,40},{16,48},{24,56},{32,0},{40,8},{48,16},{56,24},{64,96... | collective-permute-start | bytes 196616 | tf_op jit(solution)/shard_map/ppermute | solution.py:75
  83.9 6.9 %collective-permute-start.9 = (f32[64,2,256]{2,1,0:T(2,128)S(1)}, f32[64,2,256]{2,1,0:T(2,128)S(1)}, u32[]{:S(2)}, u32[]{:S(2)}) collective-permute-start(f32[64,2,256]{2,1,0:T(2,128)S(1)} %bitcast.93), channel_id=1, source_target_pairs={{0,1},{1,0},{2,3},{3,2},{4,5},{5,4},{6,7},{7,6},{8,9},{9,8},{10,11... | collective-permute-start | bytes 393224 | tf_op jit(solution)/shard_map/ppermute | solution.py:67
  90.9 10.0 %collective-permute-start.10 = (f32[64,2,256]{2,1,0:T(2,128)S(1)}, f32[64,2,256]{2,1,0:T(2,128)S(1)}, u32[]{:S(2)}, u32[]{:S(2)}) collective-permute-start(f32[64,2,256]{2,1,0:T(2,128)S(1)} %bitcast_add_fusion), channel_id=1, source_target_pairs={{0,2},{1,3},{2,0},{3,1},{4,6},{5,7},{6,4},{7,5},{8,10},{9,11},{10,... | collective-permute-start | bytes 393224 | tf_op jit(solution)/shard_map/ppermute | solution.py:67
  156.1 72.2 %copy-start.11 = (f32[128]{0:T(128)S(1)}, f32[128]{0:T(128)}, u32[]{:S(2)}) copy-start(f32[128]{0:T(128)} %param.12) | copy-start | bytes 1540
  156.2 111.7 %all-to-all-start.1 = ((f32[1,128,32,128]{3,2,0,1:T(8,128)}), f32[1,128,32,128]{3,2,0,1:T(8,128)}, u32[]{:S(2)}, u32[]{:S(2)}) async-start(f32[1,128,32,128]{3,2,0,1:T(8,128)} %copy.33), calls=%async_computation.1 | async-start | bytes 4194304 | tf_op jit(solution)/shard_map/all_to_all | solution.py:171
  231.9 3.2 %copy-start.6 = (f32[16,128]{1,0:T(8,128)S(1)}, f32[16,128]{1,0:T(8,128)}, u32[]{:S(2)}) copy-start(f32[16,128]{1,0:T(8,128)} %param.11) | copy-start | bytes 24580
  267.9 2.2 copy-start.5

commit v10 on v8

--- a/solution.py
+++ b/solution.py
@@ -108,6 +108,8 @@
     charge = sum_over(jnp.stack([partial_value, partial_charge], axis=1), "ky", z_bits)
     far_bits = [bit for bit in (8, 16, 32) if bit < space_count]
     near_bits = [bit for bit in (1, 2, 4) if bit < space_count]
+    far_rows = gather_rows(charge, "space", far_bits)
+    held, far_rows = lax.optimization_barrier((distribution, far_rows))
     positive_kx = upwind_sign > 0
     half_kx = kx_count // 2
     rank_pos = jnp.cumsum(positive_kx.astype(jnp.int32)) - 1
@@ -115,17 +117,13 @@
     slots = jnp.arange(half_kx, dtype=jnp.int32)
     pick_pos = (positive_kx[:, None] & (rank_pos[:, None] == slots[None, :])).astype(jnp.float32)
     pick_neg = ((~positive_kx)[:, None] & (rank_neg[:, None] == slots[None, :])).astype(jnp.float32)
-    flat = distribution.reshape(-1, kx_count)
+    flat = held.reshape(-1, kx_count)
     send_right = jnp.dot(flat, pick_pos, precision=precise)
     send_left = jnp.dot(flat, pick_neg, precision=precise)
     forward_pairs = [(i, i + 1) for i in range(space_count - 1)]
     backward_pairs = [(i + 1, i) for i in range(space_count - 1)]
     got_left = lax.ppermute(send_right, "space", forward_pairs)
     got_right = lax.ppermute(send_left, "space", backward_pairs)
-    far_rows = gather_rows(charge, "space", far_bits)
-    held, far_rows, got_left, got_right = lax.optimization_barrier(
-        (distribution, far_rows, got_left, got_right)
-    )
     every_row = gather_rows(far_rows, "space", near_bits)
     every_row = in_row_order(every_row, far_bits + near_bits, space_count * row_count)
     every_row = sum_over(every_row, "ky", y_bits)
@@ -157,6 +155,7 @@
         precision=triple,
     )
     mixed = mixed.reshape(row_count, ky_count, local_cols, kx_count)
+    mixed, got_left, got_right = lax.optimization_barrier((mixed, got_left, got_right))
     wigner = lax.all_to_all(mixed, "ky", split_axis=1, concat_axis=2, tiled=True)
 
     upstream_x = jnp.dot(got_left, pick_pos.T, precision=precise) + jnp.dot(

time: 268 us -> 266 us (level)
  the two profiles are of different devices: /device:TPU:123 before, /device:TPU:47 now
where the time goes in v10:
time: 266 us; the launch traced here: 265 us
  waiting for transfers between devices  120 us (45%)
  starting transfers between devices  103 us (39%)
  matrix products  22.5 us (8%)
  local copies, waits for them, and re-layouts  11.1 us (4%)
  other arithmetic  8.5 us (3%)
    all_to_all x1, waiting for transfers between devices, shards(): lax.all_to_all(mixed, 'ky', split_axis=1, concat_axis=2, tiled=True)  53.4 us
    all_to_all x1, waiting for transfers between devices, shards(): spread = lax.all_to_all(held, 'ky', split_axis=2, concat_axis=1, tiled=True)  50.6 us
    all_to_all x1, starting transfers between devices, shards(): lax.all_to_all(mixed, 'ky', split_axis=1, concat_axis=2, tiled=True)  35.1 us
    ppermute x6, starting transfers between devices, gather_rows(): other = lax.ppermute(value, axis, xor_pairs(count, bit))  25.9 us
    ppermute x3, starting transfers between devices, sum_over(): value = value + lax.ppermute(value, axis, xor_pairs(count, bit))  21 us
    all_to_all x1, starting transfers between devices, shards(): spread = lax.all_to_all(held, 'ky', split_axis=2, concat_axis=1, tiled=True)  14.4 us
    ppermute x6, waiting for transfers between devices, gather_rows(): other = lax.ppermute(value, axis, xor_pairs(count, bit))  12.3 us
  transfers between devices with their start and end apart: 13, of which 10 were waited for; matrix products, arithmetic and copies ran while one was open for 11% of the time, Pallas kernels for 0%

profile of v10, /device:TPU:47, one launch (start us, length us, event | category | flops | bytes accessed | tf_op | source)
XLA Modules:
  0.0 265.4 jit_solution(16752818518465788958)
XLA Ops:
  0.0 1.9 reduce_sum.27
  2.1 14.5 %collective-permute-start = (f32[1,2,256]{2,1,0:T(2,128)S(1)}, f32[1,2,256]{2,1,0:T(2,128)S(1)}, u32[]{:S(2)}, u32[]{:S(2)}) collective-permute-start(f32[1,2,256]{2,1,0:T(2,128)S(1)} %pad_maximum_fusion), channel_id=1, source_target_pairs={{0,4},{1,5},{2,6},{3,7},{4,0},{5,1},{6,2},{7,3},{8,12},{9,13},{10,... | collective-permute-start | bytes 6152 | tf_op jit(solution)/shard_map/ppermute | solution.py:67
  16.7 1.0 collective-permute-done
  17.6 2.6 collective-permute-start.1
  20.3 1.7 collective-permute-done.1
  22.0 3.1 %collective-permute-start.2 = (f32[2,2,256]{2,1,0:T(2,128)S(1)}, f32[2,2,256]{2,1,0:T(2,128)S(1)}, u32[]{:S(2)}, u32[]{:S(2)}) collective-permute-start(f32[2,2,256]{2,1,0:T(2,128)S(1)} %maximum_select_fusion.5), channel_id=1, source_target_pairs={{0,128},{8,136},{16,144},{24,152},{32,160},{40,168},{48,176},{56,1... | collective-permute-start | bytes 12296 | tf_op jit(solution)/shard_map/ppermute | solution.py:75
  25.1 2.1 collective-permute-done.2
  27.2 7.0 %collective-permute-start.3 = (f32[4,2,256]{2,1,0:T(2,128)S(1)}, f32[4,2,256]{2,1,0:T(2,128)S(1)}, u32[]{:S(2)}, u32[]{:S(2)}) collective-permute-start(f32[4,2,256]{2,1,0:T(2,128)S(1)} %maximum_select_fusion.4), channel_id=1, source_target_pairs={{0,256},{8,264},{16,272},{24,280},{32,288},{40,296},{48,304},{56,3... | collective-permute-start | bytes 24584 | tf_op jit(solution)/shard_map/ppermute | solution.py:75
  34.2 1.3 collective-permute-done.3
  35.5 2.5 copy.28
  38.1 14.4 %all-to-all-start = ((f32[1,16,256,128]{3,1,0,2:T(8,128)}), f32[1,16,256,128]{3,1,0,2:T(8,128)}, u32[]{:S(2)}, u32[]{:S(2)}) async-start(f32[1,16,256,128]{3,1,0,2:T(8,128)} %copy.28), calls=%async_computation | async-start | bytes 4194304 | tf_op jit(solution)/shard_map/all_to_all | solution.py:143
  52.6 0.2 reduce-window.16
  52.9 0.2 reduce-window.17
  53.3 0.2 fusion.63
  53.5 0.2 fusion.81
  53.8 0.3 fusion.68
  54.1 7.7 %collective-permute-start.4 = (f32[8,2,256]{2,1,0:T(2,128)S(1)}, f32[8,2,256]{2,1,0:T(2,128)S(1)}, u32[]{:S(2)}, u32[]{:S(2)}) collective-permute-start(f32[8,2,256]{2,1,0:T(2,128)S(1)} %maximum_select_fusion.3), channel_id=1, source_target_pairs={{0,8},{8,0},{16,24},{24,16},{32,40},{40,32},{48,56},{56,48},{64,72... | collective-permute-start | bytes 49160 | tf_op jit(solution)/shard_map/ppermute | solution.py:75
  61.8 0.8 collective-permute-done.4
  62.7 2.5 collective-permute-start.5
  65.2 2.5 collective-permute-done.5
  67.7 3.0 %collective-permute-start.6 = (f32[32,2,256]{2,1,0:T(2,128)S(1)}, f32[32,2,256]{2,1,0:T(2,128)S(1)}, u32[]{:S(2)}, u32[]{:S(2)}) collective-permute-start(f32[32,2,256]{2,1,0:T(2,128)S(1)} %maximum_select_fusion.1), channel_id=1, source_target_pairs={{0,32},{8,40},{16,48},{24,56},{32,0},{40,8},{48,16},{56,24},{64,96... | collective-permute-start | bytes 196616 | tf_op jit(solution)/shard_map/ppermute | solution.py:75
  70.8 3.8 %collective-permute-done.6 = f32[32,2,256]{2,1,0:T(2,128)S(1)} collective-permute-done((f32[32,2,256]{2,1,0:T(2,128)S(1)}, f32[32,2,256]{2,1,0:T(2,128)S(1)}, u32[]{:S(2)}, u32[]{:S(2)}) %collective-permute-start.6) | collective-permute-done | bytes 65568 | tf_op jit(solution)/shard_map/ppermute | solution.py:75
  74.8 1.9 collective-permute-start.7
  76.7 2.4 fusion.50
  79.1 4.3 %collective-permute-start.9 = (f32[4096,64]{0,1:T(8,128)}, f32[4096,64]{0,1:T(8,128)}, u32[]{:S(2)}, u32[]{:S(2)}) collective-permute-start(f32[4096,64]{0,1:T(8,128)} %fusion.50), channel_id=1, source_target_pairs={{0,8},{8,16},{16,24},{24,32},{32,40},{40,48},{48,56},{56,64},{64,7... | collective-permute-start | bytes 3145736 | tf_op jit(solution)/shard_map/ppermute | solution.py:125
  83.5 4.5 %collective-permute-start.8 = (f32[64,2,256]{2,1,0:T(2,128)S(1)}, f32[64,2,256]{2,1,0:T(2,128)S(1)}, u32[]{:S(2)}, u32[]{:S(2)}) collective-permute-start(f32[64,2,256]{2,1,0:T(2,128)S(1)} %bitcast_add_fusion), channel_id=1, source_target_pairs={{0,2},{1,3},{2,0},{3,1},{4,6},{5,7},{6,4},{7,5},{8,10},{9,11},{10,... | collective-permute-start | bytes 393224 | tf_op jit(solution)/shard_map/ppermute | solution.py:67
  88.0 2.4 fusion.55
  90.4 2.1 collective-permute-start.10
  92.7 0.4 fusion.42
  93.1 1.3 convolution_divide_fusion
  94.4 1.3 fusion.17
  95.8 0.1 fusion.85
  95.9 4.5 %fusion.4 = f32[1,64,32]{2,0,1:T(1,128)S(1)} fusion(f32[256,1,1]{0,1,2:T(1,128)S(1)} %bitcast.83, s32[64,32]{1,0:T(8,128)S(1)} %get-tuple-element.26, s32[64,32]{1,0:T(8,128)S(1)} %get-tuple-element.25), kind=kOutput, calls=%fused_computation.8 | convolution fusion | flops 8912896 | bytes 25600 | tf_op jit(solution)/shard_map/dot_general | solution.py:47
  100.6 50.6 %all-to-all-done = f32[1,16,256,128]{3,1,0,2:T(8,128)} async-done(((f32[1,16,256,128]{3,1,0,2:T(8,128)}), f32[1,16,256,128]{3,1,0,2:T(8,128)}, u32[]{:S(2)}, u32[]{:S(2)}) %all-to-all-start) | async-done | bytes 2097184 | tf_op jit(solution)/shard_map/all_to_all | solution.py:143
  151.2 2.2 copy.29
  153.5 2.6 fusion.1
  156.1 2.4 fusion.38
  158.5 3.0 %collective-permute-done.10 = f32[4096,64]{0,1:T(8,128)S(1)} collective-permute-done((f32[4096,64]{0,1:T(8,128)}, f32[4096,64]{0,1:T(8,128)S(1)}, u32[]{:S(2)}, u32[]{:S(2)}) %collective-permute-start.10) | collective-permute-done | bytes 1048608 | tf_op jit(solution)/shard_map/ppermute | solution.py:126
  161.5 3.1 %copy.33 = f32[1,128,32,128]{3,2,0,1:T(8,128)} copy(f32[1,128,32,128]{1,3,2,0:T(8,128)} %bitcast.73) | data formatting | bytes 4194304 | tf_op jit(solution)/shard_map/optimization_barrier | solution.py:158
  164.6 35.1 %all-to-all-start.1 = ((f32[1,128,32,128]{3,2,0,1:T(8,128)}), f32[1,128,32,128]{3,2,0,1:T(8,128)}, u32[]{:S(2)}, u32[]{:S(2)}) async-start(f32[1,128,32,128]{3,2,0,1:T(8,128)} %copy.33), calls=%async_computation.1 | async-start | bytes 4194304 | tf_op jit(solution)/shard_map/all_to_all | solution.py:159
  199.7 0.4 fusion.106
  200.2 1.9 fusion.53
  202.1 3.1 %convolution_add_fusion = f32[4096,128]{1,0:T(8,128)S(1)} fusion(f32[4096,128]{1,0:T(8,128)S(1)} %fusion.53, f32[4096,64]{0,1:T(8,128)} %collective-permute-done.9, s32[128]{0:T(128)S(1)} %add_reduce_fusion.1, pred[128]{0:T(512)(128)(4,1)S(1)} %get-tuple-element.30), kind=kOutput, calls=%fused_computation | convolution fusion | flops 403193856 | bytes 5243520 | tf_op jit(solution)/shard_map/dot_general | solution.py:161
  205.2 3.0 %multiply_add_fusion.1 = f32[1,16,256,128]{3,2,1,0:T(8,128)} fusion(f32[1,16,256,128]{3,2,1,0:T(8,128)S(1)} %copy-done, f32[1,16,255,128]{3,2,1,0:T(8,128)S(1)} %get-tuple-element.22, f32[1,16,255,128]{3,2,1,0:T(8,128)S(1)} %get-tuple-element.21, f32[1,16,256,128]{3,2,1,0:T(8,128)S(1)} %bitcast.74, f32[16,128]{1,0:T(8,128)S(1)} %copy-done.2, ...), kind=kLoop, calls=%fused_computation.7 | loop fusion | flops 6291456 | bytes 10480208 | tf_op jit(solution)/shard_map/add | solution.py:178
  208.2 53.4 %all-to-all-done.1 = f32[1,128,32,128]{3,2,0,1:T(8,128)} async-done(((f32[1,128,32,128]{3,2,0,1:T(8,128)}), f32[1,128,32,128]{3,2,0,1:T(8,128)}, u32[]{:S(2)}, u32[]{:S(2)}) %all-to-all-start.1) | async-done | bytes 2097184 | tf_op jit(solution)/shard_map/all_to_all | solution.py:159
  261.6 2.0 copy.34
  263.6 0.2 copy-done.1
  263.8 1.6 multiply_add_fusion
  (54 shorter events, 1.5 us)
Async XLA Ops:
  0.0 35.5 %copy-start = (f32[1,16,256,128]{3,2,1,0:T(8,128)S(1)}, f32[1,16,256,128]{3,2,1,0:T(8,128)}, u32[]{:S(2)}) copy-start(f32[1,16,256,128]{3,2,1,0:T(8,128)} %param.7) | copy-start | bytes 6291460
  0.0 2.0 copy-start.5
  0.0 2.0 copy-start.6
  0.0 2.0 copy-start.3
  2.1 15.5 %collective-permute-start = (f32[1,2,256]{2,1,0:T(2,128)S(1)}, f32[1,2,256]{2,1,0:T(2,128)S(1)}, u32[]{:S(2)}, u32[]{:S(2)}) collective-permute-start(f32[1,2,256]{2,1,0:T(2,128)S(1)} %pad_maximum_fusion), channel_id=1, source_target_pairs={{0,4},{1,5},{2,6},{3,7},{4,0},{5,1},{6,2},{7,3},{8,12},{9,13},{10,... | collective-permute-start | bytes 6152 | tf_op jit(solution)/shard_map/ppermute | solution.py:67
  17.6 4.3 %collective-permute-start.1 = (f32[1,2,256]{2,1,0:T(2,128)S(1)}, f32[1,2,256]{2,1,0:T(2,128)S(1)}, u32[]{:S(2)}, u32[]{:S(2)}) collective-permute-start(f32[1,2,256]{2,1,0:T(2,128)S(1)} %fusion.104), channel_id=1, source_target_pairs={{0,64},{8,72},{16,80},{24,88},{32,96},{40,104},{48,112},{56,120},{... | collective-permute-start | bytes 6152 | tf_op jit(solution)/shard_map/ppermute | solution.py:75
  22.0 5.2 %collective-permute-start.2 = (f32[2,2,256]{2,1,0:T(2,128)S(1)}, f32[2,2,256]{2,1,0:T(2,128)S(1)}, u32[]{:S(2)}, u32[]{:S(2)}) collective-permute-start(f32[2,2,256]{2,1,0:T(2,128)S(1)} %maximum_select_fusion.5), channel_id=1, source_target_pairs={{0,128},{8,136},{16,144},{24,152},{32,160},{40,168},{48,176},{56,1... | collective-permute-start | bytes 12296 | tf_op jit(solution)/shard_map/ppermute | solution.py:75
  27.2 8.3 %collective-permute-start.3 = (f32[4,2,256]{2,1,0:T(2,128)S(1)}, f32[4,2,256]{2,1,0:T(2,128)S(1)}, u32[]{:S(2)}, u32[]{:S(2)}) collective-permute-start(f32[4,2,256]{2,1,0:T(2,128)S(1)} %maximum_select_fusion.4), channel_id=1, source_target_pairs={{0,256},{8,264},{16,272},{24,280},{32,288},{40,296},{48,304},{56,3... | collective-permute-start | bytes 24584 | tf_op jit(solution)/shard_map/ppermute | solution.py:75
  38.1 14.4 %copy-start.4 = (s32[128]{0:T(128)S(1)}, s32[128]{0:T(128)}, u32[]{:S(2)}) copy-start(s32[128]{0:T(128)} %param.13) | copy-start | bytes 1540
  38.1 113.1 %all-to-all-start = ((f32[1,16,256,128]{3,1,0,2:T(8,128)}), f32[1,16,256,128]{3,1,0,2:T(8,128)}, u32[]{:S(2)}, u32[]{:S(2)}) async-start(f32[1,16,256,128]{3,1,0,2:T(8,128)} %copy.28), calls=%async_computation | async-start | bytes 4194304 | tf_op jit(solution)/shard_map/all_to_all | solution.py:143
  54.1 8.6 %collective-permute-start.4 = (f32[8,2,256]{2,1,0:T(2,128)S(1)}, f32[8,2,256]{2,1,0:T(2,128)S(1)}, u32[]{:S(2)}, u32[]{:S(2)}) collective-permute-start(f32[8,2,256]{2,1,0:T(2,128)S(1)} %maximum_select_fusion.3), channel_id=1, source_target_pairs={{0,8},{8,0},{16,24},{24,16},{32,40},{40,32},{48,56},{56,48},{64,72... | collective-permute-start | bytes 49160 | tf_op jit(solution)/shard_map/ppermute | solution.py:75
  62.7 5.1 %collective-permute-start.5 = (f32[16,2,256]{2,1,0:T(2,128)S(1)}, f32[16,2,256]{2,1,0:T(2,128)S(1)}, u32[]{:S(2)}, u32[]{:S(2)}) collective-permute-start(f32[16,2,256]{2,1,0:T(2,128)S(1)} %maximum_select_fusion.2), channel_id=1, source_target_pairs={{0,16},{8,24},{16,0},{24,8},{32,48},{40,56},{48,32},{56,40},{64,80... | collective-permute-start | bytes 98312 | tf_op jit(solution)/shard_map/ppermute | solution.py:75
  67.7 6.9 %collective-permute-start.6 = (f32[32,2,256]{2,1,0:T(2,128)S(1)}, f32[32,2,256]{2,1,0:T(2,128)S(1)}, u32[]{:S(2)}, u32[]{:S(2)}) collective-permute-start(f32[32,2,256]{2,1,0:T(2,128)S(1)} %maximum_select_fusion.1), channel_id=1, source_target_pairs={{0,32},{8,40},{16,48},{24,56},{32,0},{40,8},{48,16},{56,24},{64,96... | collective-permute-start | bytes 196616 | tf_op jit(solution)/shard_map/ppermute | solution.py:75
  74.8 8.6 %collective-permute-start.7 = (f32[64,2,256]{2,1,0:T(2,128)S(1)}, f32[64,2,256]{2,1,0:T(2,128)S(1)}, u32[]{:S(2)}, u32[]{:S(2)}) collective-permute-start(f32[64,2,256]{2,1,0:T(2,128)S(1)} %bitcast.75), channel_id=1, source_target_pairs={{0,1},{1,0},{2,3},{3,2},{4,5},{5,4},{6,7},{7,6},{8,9},{9,8},{10,11... | collective-permute-start | bytes 393224 | tf_op jit(solution)/shard_map/ppermute | solution.py:67
  79.1 79.5 %collective-permute-start.9 = (f32[4096,64]{0,1:T(8,128)}, f32[4096,64]{0,1:T(8,128)}, u32[]{:S(2)}, u32[]{:S(2)}) collective-permute-start(f32[4096,64]{0,1:T(8,128)} %fusion.50), channel_id=1, source_target_pairs={{0,8},{8,16},{16,24},{24,32},{32,40},{40,48},{48,56},{56,64},{64,7... | collective-permute-start | bytes 3145736 | tf_op jit(solution)/shard_map/ppermute | solution.py:125
  83.5 9.0 %collective-permute-start.8 = (f32[64,2,256]{2,1,0:T(2,128)S(1)}, f32[64,2,256]{2,1,0:T(2,128)S(1)}, u32[]{:S(2)}, u32[]{:S(2)}) collective-permute-start(f32[64,2,256]{2,1,0:T(2,128)S(1)} %bitcast_add_fusion), channel_id=1, source_target_pairs={{0,2},{1,3},{2,0},{3,1},{4,6},{5,7},{6,4},{7,5},{8,10},{9,11},{10,... | collective-permute-start | bytes 393224 | tf_op jit(solution)/shard_map/ppermute | solution.py:67
  90.4 71.1 %collective-permute-start.10 = (f32[4096,64]{0,1:T(8,128)}, f32[4096,64]{0,1:T(8,128)S(1)}, u32[]{:S(2)}, u32[]{:S(2)}) collective-permute-start(f32[4096,64]{0,1:T(8,128)} %fusion.55), channel_id=1, source_target_pairs={{8,0},{16,8},{24,16},{32,24},{40,32},{48,40},{56,48},{64,56},{72,6... | collective-permute-start | bytes 3145736 | tf_op jit(solution)/shard_map/ppermute | solution.py:126
  164.6 35.1 %copy-start.7 = (f32[128]{0:T(128)S(1)}, f32[128]{0:T(128)}, u32[]{:S(2)}) copy-start(f32[128]{0:T(128)} %param.12) | copy-start | bytes 1540
  164.6 97.0 %all-to-all-start.1 = ((f32[1,128,32,128]{3,2,0,1:T(8,128)}), f32[1,128,32,128]{3,2,0,1:T(8,128)}, u32[]{:S(2)}, u32[]{:S(2)}) async-start(f32[1,128,32,128]{3,2,0,1:T(8,128)} %copy.33), calls=%async_computation.1 | async-start | bytes 4194304 | tf_op jit(solution)/shard_map/all_to_all | solution.py:159
  202.0 3.1 %copy-start.2 = (f32[16,128]{1,0:T(8,128)S(1)}, f32[16,128]{1,0:T(8,128)}, u32[]{:S(2)}) copy-start(f32[16,128]{1,0:T(8,128)} %param.11) | copy-start | bytes 24580
  261.6 2.2 copy-start.1

commit v11 on v10

--- a/solution.py
+++ b/solution.py
@@ -105,7 +105,7 @@
     z_bits = [ky_size // 2] if ky_size > 1 else []
     y_bits = [bit for bit in (1, 2, 4, 8, 16) if bit < ky_size // 2]
     partial_charge = partial_value - jnp.where(lax.axis_index("ky") == 0, doping, 0.0)
-    charge = sum_over(jnp.stack([partial_value, partial_charge], axis=1), "ky", z_bits)
+    charge = jnp.stack([partial_value, partial_charge], axis=1)
     far_bits = [bit for bit in (8, 16, 32) if bit < space_count]
     near_bits = [bit for bit in (1, 2, 4) if bit < space_count]
     far_rows = gather_rows(charge, "space", far_bits)
@@ -126,7 +126,7 @@
     got_right = lax.ppermute(send_left, "space", backward_pairs)
     every_row = gather_rows(far_rows, "space", near_bits)
     every_row = in_row_order(every_row, far_bits + near_bits, space_count * row_count)
-    every_row = sum_over(every_row, "ky", y_bits)
+    every_row = sum_over(every_row, "ky", y_bits + z_bits)
     density = lax.dynamic_slice_in_dim(every_row[:, 0], row_start, row_count, 0)
     every_row = every_row[:, 1]
 

time: 266 us -> 284 us (1.068)
  the two profiles are of different devices: /device:TPU:47 before, /device:TPU:105 now
where the time goes in v11:
time: 284 us
  waiting for transfers between devices  169 us (60%)
  starting transfers between devices  71.7 us (25%)
  matrix products  22.5 us (8%)
  local copies, waits for them, and re-layouts  11.1 us (4%)
  other arithmetic  8.55 us (3%)
    all_to_all x1, waiting for transfers between devices, shards(): lax.all_to_all(mixed, 'ky', split_axis=1, concat_axis=2, tiled=True)  94.5 us
    ppermute x3, waiting for transfers between devices, sum_over(): value = value + lax.ppermute(value, axis, xor_pairs(count, bit))  63.7 us
    ppermute x6, starting transfers between devices, gather_rows(): other = lax.ppermute(value, axis, xor_pairs(count, bit))  27 us
    ppermute x3, starting transfers between devices, sum_over(): value = value + lax.ppermute(value, axis, xor_pairs(count, bit))  17.4 us
    all_to_all x1, starting transfers between devices, shards(): spread = lax.all_to_all(held, 'ky', split_axis=2, concat_axis=1, tiled=True)  13.5 us
    ppermute x6, waiting for transfers between devices, gather_rows(): other = lax.ppermute(value, axis, xor_pairs(count, bit))  11.2 us
    ppermute x1, starting transfers between devices, shards(): got_left = lax.ppermute(send_right, 'space', forward_pairs)  6.27 us
  transfers between devices with their start and end apart: 13, of which 9 were waited for; matrix products, arithmetic and copies ran while one was open for 11% of the time, Pallas kernels for 0%

profile of v11, /device:TPU:105, one launch (start us, length us, event | category | flops | bytes accessed | tf_op | source)
XLA Modules:
  0.0 283.7 jit_solution(14206542905658782961)
XLA Ops:
  0.0 1.9 reduce_sum.27
  2.1 1.9 collective-permute-start
  4.1 2.4 collective-permute-done
  6.5 1.9 collective-permute-start.1
  8.4 3.3 %collective-permute-done.1 = f32[2,2,256]{2,1,0:T(2,128)S(1)} collective-permute-done((f32[2,2,256]{2,1,0:T(2,128)S(1)}, f32[2,2,256]{2,1,0:T(2,128)S(1)}, u32[]{:S(2)}, u32[]{:S(2)}) %collective-permute-start.1) | collective-permute-done | bytes 4128 | tf_op jit(solution)/shard_map/ppermute | solution.py:75
  11.7 8.8 %collective-permute-start.2 = (f32[4,2,256]{2,1,0:T(2,128)S(1)}, f32[4,2,256]{2,1,0:T(2,128)S(1)}, u32[]{:S(2)}, u32[]{:S(2)}) collective-permute-start(f32[4,2,256]{2,1,0:T(2,128)S(1)} %maximum_select_fusion.4), channel_id=1, source_target_pairs={{0,256},{8,264},{16,272},{24,280},{32,288},{40,296},{48,304},{56,3... | collective-permute-start | bytes 24584 | tf_op jit(solution)/shard_map/ppermute | solution.py:75
  20.5 1.0 collective-permute-done.2
  21.6 2.5 copy.28
  24.1 13.5 %all-to-all-start = ((f32[1,16,256,128]{3,1,0,2:T(8,128)}), f32[1,16,256,128]{3,1,0,2:T(8,128)}, u32[]{:S(2)}, u32[]{:S(2)}) async-start(f32[1,16,256,128]{3,1,0,2:T(8,128)} %copy.28), calls=%async_computation | async-start | bytes 4194304 | tf_op jit(solution)/shard_map/all_to_all | solution.py:143
  37.7 0.2 reduce-window.16
  37.9 0.2 fusion.63
  38.1 0.2 fusion.81
  38.4 0.3 fusion.68
  38.7 6.6 %collective-permute-start.3 = (f32[8,2,256]{2,1,0:T(2,128)S(1)}, f32[8,2,256]{2,1,0:T(2,128)S(1)}, u32[]{:S(2)}, u32[]{:S(2)}) collective-permute-start(f32[8,2,256]{2,1,0:T(2,128)S(1)} %maximum_select_fusion.3), channel_id=1, source_target_pairs={{0,8},{8,0},{16,24},{24,16},{32,40},{40,32},{48,56},{56,48},{64,72... | collective-permute-start | bytes 49160 | tf_op jit(solution)/shard_map/ppermute | solution.py:75
  45.4 0.7 collective-permute-done.3
  46.1 3.1 %collective-permute-start.4 = (f32[16,2,256]{2,1,0:T(2,128)S(1)}, f32[16,2,256]{2,1,0:T(2,128)S(1)}, u32[]{:S(2)}, u32[]{:S(2)}) collective-permute-start(f32[16,2,256]{2,1,0:T(2,128)S(1)} %maximum_select_fusion.2), channel_id=1, source_target_pairs={{0,16},{8,24},{16,0},{24,8},{32,48},{40,56},{48,32},{56,40},{64,80... | collective-permute-start | bytes 98312 | tf_op jit(solution)/shard_map/ppermute | solution.py:75
  49.3 1.9 collective-permute-done.4
  51.2 4.7 %collective-permute-start.5 = (f32[32,2,256]{2,1,0:T(2,128)S(1)}, f32[32,2,256]{2,1,0:T(2,128)S(1)}, u32[]{:S(2)}, u32[]{:S(2)}) collective-permute-start(f32[32,2,256]{2,1,0:T(2,128)S(1)} %maximum_select_fusion.1), channel_id=1, source_target_pairs={{0,32},{8,40},{16,48},{24,56},{32,0},{40,8},{48,16},{56,24},{64,96... | collective-permute-start | bytes 196616 | tf_op jit(solution)/shard_map/ppermute | solution.py:75
  56.0 1.8 collective-permute-done.5
  57.9 1.9 collective-permute-start.6
  59.9 0.2 reduce-window.17
  60.2 3.7 %collective-permute-done.6 = f32[64,2,256]{2,1,0:T(2,128)S(1)} collective-permute-done((f32[64,2,256]{2,1,0:T(2,128)S(1)}, f32[64,2,256]{2,1,0:T(2,128)S(1)}, u32[]{:S(2)}, u32[]{:S(2)}) %collective-permute-start.6) | collective-permute-done | bytes 131104 | tf_op jit(solution)/shard_map/ppermute | solution.py:67
  64.1 3.7 %collective-permute-start.7 = (f32[64,2,256]{2,1,0:T(2,128)S(1)}, f32[64,2,256]{2,1,0:T(2,128)S(1)}, u32[]{:S(2)}, u32[]{:S(2)}) collective-permute-start(f32[64,2,256]{2,1,0:T(2,128)S(1)} %bitcast_add_fusion), channel_id=1, source_target_pairs={{0,2},{1,3},{2,0},{3,1},{4,6},{5,7},{6,4},{7,5},{8,10},{9,11},{10,... | collective-permute-start | bytes 393224 | tf_op jit(solution)/shard_map/ppermute | solution.py:67
  67.8 2.4 fusion.50
  70.1 6.3 %collective-permute-start.9 = (f32[4096,64]{0,1:T(8,128)}, f32[4096,64]{0,1:T(8,128)}, u32[]{:S(2)}, u32[]{:S(2)}) collective-permute-start(f32[4096,64]{0,1:T(8,128)} %fusion.50), channel_id=1, source_target_pairs={{0,8},{8,16},{16,24},{24,32},{32,40},{40,48},{48,56},{56,64},{64,7... | collective-permute-start | bytes 3145736 | tf_op jit(solution)/shard_map/ppermute | solution.py:125
  76.5 11.8 %collective-permute-start.8 = (f32[64,2,256]{2,1,0:T(2,128)S(1)}, f32[64,2,256]{2,1,0:T(2,128)S(1)}, u32[]{:S(2)}, u32[]{:S(2)}) collective-permute-start(f32[64,2,256]{2,1,0:T(2,128)S(1)} %add.202), channel_id=1, source_target_pairs={{0,4},{1,5},{2,6},{3,7},{4,0},{5,1},{6,2},{7,3},{8,12},{9,13},{10,... | collective-permute-start | bytes 393224 | tf_op jit(solution)/shard_map/ppermute | solution.py:67
  88.3 2.4 fusion.55
  90.7 2.1 collective-permute-start.10
  92.8 60.0 %collective-permute-done.8 = f32[64,2,256]{2,1,0:T(2,128)S(1)} collective-permute-done((f32[64,2,256]{2,1,0:T(2,128)S(1)}, f32[64,2,256]{2,1,0:T(2,128)S(1)}, u32[]{:S(2)}, u32[]{:S(2)}) %collective-permute-start.8) | collective-permute-done | bytes 131104 | tf_op jit(solution)/shard_map/ppermute | solution.py:67
  153.0 0.4 fusion.42
  153.4 1.3 convolution_divide_fusion
  154.7 1.3 fusion.17
  156.1 0.1 fusion.85
  156.2 4.5 %fusion.4 = f32[1,64,32]{2,0,1:T(1,128)S(1)} fusion(f32[256,1,1]{0,1,2:T(1,128)S(1)} %bitcast.83, s32[64,32]{1,0:T(8,128)S(1)} %get-tuple-element.26, s32[64,32]{1,0:T(8,128)S(1)} %get-tuple-element.25), kind=kOutput, calls=%fused_computation.8 | convolution fusion | flops 8912896 | bytes 25600 | tf_op jit(solution)/shard_map/dot_general | solution.py:47
  160.9 2.2 copy.29
  163.1 0.1 mul.251
  163.3 2.6 fusion.1
  165.9 2.4 fusion.38
  168.3 3.1 %copy.33 = f32[1,128,32,128]{3,2,0,1:T(8,128)} copy(f32[1,128,32,128]{1,3,2,0:T(8,128)} %bitcast.73) | data formatting | bytes 4194304 | tf_op jit(solution)/shard_map/optimization_barrier | solution.py:158
  171.4 5.4 %all-to-all-start.1 = ((f32[1,128,32,128]{3,2,0,1:T(8,128)}), f32[1,128,32,128]{3,2,0,1:T(8,128)}, u32[]{:S(2)}, u32[]{:S(2)}) async-start(f32[1,128,32,128]{3,2,0,1:T(8,128)} %copy.33), calls=%async_computation.1 | async-start | bytes 4194304 | tf_op jit(solution)/shard_map/all_to_all | solution.py:159
  176.8 0.4 fusion.105
  177.3 1.9 fusion.53
  179.2 3.1 %convolution_add_fusion = f32[4096,128]{1,0:T(8,128)S(1)} fusion(f32[4096,128]{1,0:T(8,128)S(1)} %fusion.53, f32[4096,64]{0,1:T(8,128)} %collective-permute-done.9, s32[128]{0:T(128)S(1)} %add_reduce_fusion.1, pred[128]{0:T(512)(128)(4,1)S(1)} %get-tuple-element.30), kind=kOutput, calls=%fused_computation | convolution fusion | flops 403193856 | bytes 5243520 | tf_op jit(solution)/shard_map/dot_general | solution.py:161
  182.3 3.0 %multiply_add_fusion.1 = f32[1,16,256,128]{3,2,1,0:T(8,128)} fusion(f32[1,16,256,128]{3,2,1,0:T(8,128)S(1)} %copy-done, f32[1,16,255,128]{3,2,1,0:T(8,128)S(1)} %get-tuple-element.22, f32[1,16,255,128]{3,2,1,0:T(8,128)S(1)} %get-tuple-element.21, f32[1,16,256,128]{3,2,1,0:T(8,128)S(1)} %bitcast.74, f32[16,128]{1,0:T(8,128)S(1)} %copy-done.2, ...), kind=kLoop, calls=%fused_computation.7 | loop fusion | flops 6291456 | bytes 10480208 | tf_op jit(solution)/shard_map/add | solution.py:178
  185.3 94.5 %all-to-all-done.1 = f32[1,128,32,128]{3,2,0,1:T(8,128)} async-done(((f32[1,128,32,128]{3,2,0,1:T(8,128)}), f32[1,128,32,128]{3,2,0,1:T(8,128)}, u32[]{:S(2)}, u32[]{:S(2)}) %all-to-all-start.1) | async-done | bytes 2097184 | tf_op jit(solution)/shard_map/all_to_all | solution.py:159
  279.8 2.0 copy.34
  281.8 0.2 copy-done.1
  282.0 1.6 multiply_add_fusion
  (54 shorter events, 1.5 us)
Async XLA Ops:
  0.0 21.6 %copy-start = (f32[1,16,256,128]{3,2,1,0:T(8,128)S(1)}, f32[1,16,256,128]{3,2,1,0:T(8,128)}, u32[]{:S(2)}) copy-start(f32[1,16,256,128]{3,2,1,0:T(8,128)} %param.7) | copy-start | bytes 6291460
  0.0 2.0 copy-start.5
  0.0 2.0 copy-start.6
  0.0 2.0 copy-start.3
  2.1 4.3 %collective-permute-start = (f32[1,2,256]{2,1,0:T(2,128)S(1)}, f32[1,2,256]{2,1,0:T(2,128)S(1)}, u32[]{:S(2)}, u32[]{:S(2)}) collective-permute-start(f32[1,2,256]{2,1,0:T(2,128)S(1)} %pad_maximum_fusion), channel_id=1, source_target_pairs={{0,64},{8,72},{16,80},{24,88},{32,96},{40,104},{48,112},{56,120},{... | collective-permute-start | bytes 6152 | tf_op jit(solution)/shard_map/ppermute | solution.py:75
  6.5 5.3 %collective-permute-start.1 = (f32[2,2,256]{2,1,0:T(2,128)S(1)}, f32[2,2,256]{2,1,0:T(2,128)S(1)}, u32[]{:S(2)}, u32[]{:S(2)}) collective-permute-start(f32[2,2,256]{2,1,0:T(2,128)S(1)} %maximum_select_fusion.5), channel_id=1, source_target_pairs={{0,128},{8,136},{16,144},{24,152},{32,160},{40,168},{48,176},{56,1... | collective-permute-start | bytes 12296 | tf_op jit(solution)/shard_map/ppermute | solution.py:75
  11.7 9.8 %collective-permute-start.2 = (f32[4,2,256]{2,1,0:T(2,128)S(1)}, f32[4,2,256]{2,1,0:T(2,128)S(1)}, u32[]{:S(2)}, u32[]{:S(2)}) collective-permute-start(f32[4,2,256]{2,1,0:T(2,128)S(1)} %maximum_select_fusion.4), channel_id=1, source_target_pairs={{0,256},{8,264},{16,272},{24,280},{32,288},{40,296},{48,304},{56,3... | collective-permute-start | bytes 24584 | tf_op jit(solution)/shard_map/ppermute | solution.py:75
  24.1 13.5 %copy-start.4 = (s32[128]{0:T(128)S(1)}, s32[128]{0:T(128)}, u32[]{:S(2)}) copy-start(s32[128]{0:T(128)} %param.13) | copy-start | bytes 1540
  24.1 136.8 %all-to-all-start = ((f32[1,16,256,128]{3,1,0,2:T(8,128)}), f32[1,16,256,128]{3,1,0,2:T(8,128)}, u32[]{:S(2)}, u32[]{:S(2)}) async-start(f32[1,16,256,128]{3,1,0,2:T(8,128)} %copy.28), calls=%async_computation | async-start | bytes 4194304 | tf_op jit(solution)/shard_map/all_to_all | solution.py:143
  38.7 7.4 %collective-permute-start.3 = (f32[8,2,256]{2,1,0:T(2,128)S(1)}, f32[8,2,256]{2,1,0:T(2,128)S(1)}, u32[]{:S(2)}, u32[]{:S(2)}) collective-permute-start(f32[8,2,256]{2,1,0:T(2,128)S(1)} %maximum_select_fusion.3), channel_id=1, source_target_pairs={{0,8},{8,0},{16,24},{24,16},{32,40},{40,32},{48,56},{56,48},{64,72... | collective-permute-start | bytes 49160 | tf_op jit(solution)/shard_map/ppermute | solution.py:75
  46.1 5.1 %collective-permute-start.4 = (f32[16,2,256]{2,1,0:T(2,128)S(1)}, f32[16,2,256]{2,1,0:T(2,128)S(1)}, u32[]{:S(2)}, u32[]{:S(2)}) collective-permute-start(f32[16,2,256]{2,1,0:T(2,128)S(1)} %maximum_select_fusion.2), channel_id=1, source_target_pairs={{0,16},{8,24},{16,0},{24,8},{32,48},{40,56},{48,32},{56,40},{64,80... | collective-permute-start | bytes 98312 | tf_op jit(solution)/shard_map/ppermute | solution.py:75
  51.2 6.5 %collective-permute-start.5 = (f32[32,2,256]{2,1,0:T(2,128)S(1)}, f32[32,2,256]{2,1,0:T(2,128)S(1)}, u32[]{:S(2)}, u32[]{:S(2)}) collective-permute-start(f32[32,2,256]{2,1,0:T(2,128)S(1)} %maximum_select_fusion.1), channel_id=1, source_target_pairs={{0,32},{8,40},{16,48},{24,56},{32,0},{40,8},{48,16},{56,24},{64,96... | collective-permute-start | bytes 196616 | tf_op jit(solution)/shard_map/ppermute | solution.py:75
  57.9 6.1 %collective-permute-start.6 = (f32[64,2,256]{2,1,0:T(2,128)S(1)}, f32[64,2,256]{2,1,0:T(2,128)S(1)}, u32[]{:S(2)}, u32[]{:S(2)}) collective-permute-start(f32[64,2,256]{2,1,0:T(2,128)S(1)} %bitcast.75), channel_id=1, source_target_pairs={{0,1},{1,0},{2,3},{3,2},{4,5},{5,4},{6,7},{7,6},{8,9},{9,8},{10,11... | collective-permute-start | bytes 393224 | tf_op jit(solution)/shard_map/ppermute | solution.py:67
  64.1 12.4 %collective-permute-start.7 = (f32[64,2,256]{2,1,0:T(2,128)S(1)}, f32[64,2,256]{2,1,0:T(2,128)S(1)}, u32[]{:S(2)}, u32[]{:S(2)}) collective-permute-start(f32[64,2,256]{2,1,0:T(2,128)S(1)} %bitcast_add_fusion), channel_id=1, source_target_pairs={{0,2},{1,3},{2,0},{3,1},{4,6},{5,7},{6,4},{7,5},{8,10},{9,11},{10,... | collective-permute-start | bytes 393224 | tf_op jit(solution)/shard_map/ppermute | solution.py:67
  70.1 98.1 %collective-permute-start.9 = (f32[4096,64]{0,1:T(8,128)}, f32[4096,64]{0,1:T(8,128)}, u32[]{:S(2)}, u32[]{:S(2)}) collective-permute-start(f32[4096,64]{0,1:T(8,128)} %fusion.50), channel_id=1, source_target_pairs={{0,8},{8,16},{16,24},{24,32},{32,40},{40,48},{48,56},{56,64},{64,7... | collective-permute-start | bytes 3145736 | tf_op jit(solution)/shard_map/ppermute | solution.py:125
  76.5 76.3 %collective-permute-start.8 = (f32[64,2,256]{2,1,0:T(2,128)S(1)}, f32[64,2,256]{2,1,0:T(2,128)S(1)}, u32[]{:S(2)}, u32[]{:S(2)}) collective-permute-start(f32[64,2,256]{2,1,0:T(2,128)S(1)} %add.202), channel_id=1, source_target_pairs={{0,4},{1,5},{2,6},{3,7},{4,0},{5,1},{6,2},{7,3},{8,12},{9,13},{10,... | collective-permute-start | bytes 393224 | tf_op jit(solution)/shard_map/ppermute | solution.py:67
  90.7 77.6 %collective-permute-start.10 = (f32[4096,64]{0,1:T(8,128)}, f32[4096,64]{0,1:T(8,128)S(1)}, u32[]{:S(2)}, u32[]{:S(2)}) collective-permute-start(f32[4096,64]{0,1:T(8,128)} %fusion.55), channel_id=1, source_target_pairs={{8,0},{16,8},{24,16},{32,24},{40,32},{48,40},{56,48},{64,56},{72,6... | collective-permute-start | bytes 3145736 | tf_op jit(solution)/shard_map/ppermute | solution.py:126
  171.4 5.4 %copy-start.7 = (f32[128]{0:T(128)S(1)}, f32[128]{0:T(128)}, u32[]{:S(2)}) copy-start(f32[128]{0:T(128)} %param.12) | copy-start | bytes 1540
  171.4 108.4 %all-to-all-start.1 = ((f32[1,128,32,128]{3,2,0,1:T(8,128)}), f32[1,128,32,128]{3,2,0,1:T(8,128)}, u32[]{:S(2)}, u32[]{:S(2)}) async-start(f32[1,128,32,128]{3,2,0,1:T(8,128)} %copy.33), calls=%async_computation.1 | async-start | bytes 4194304 | tf_op jit(solution)/shard_map/all_to_all | solution.py:159
  179.2 3.1 %copy-start.2 = (f32[16,128]{1,0:T(8,128)S(1)}, f32[16,128]{1,0:T(8,128)}, u32[]{:S(2)}) copy-start(f32[16,128]{1,0:T(8,128)} %param.11) | copy-start | bytes 24580
  279.8 2.2 copy-start.1

commit v12 on v10

--- a/solution.py
+++ b/solution.py
@@ -86,6 +86,25 @@
     order = sorted(range(levels), key=lambda axis: -bits[levels - 1 - axis])
     shaped = jnp.transpose(shaped, order + list(range(levels, shaped.ndim)))
     return shaped.reshape((count,) + value.shape[1:])
+
+
+def spread_by_shifts(block):
+    ky_size = lax.axis_size("ky")
+    index = lax.axis_index("ky")
+    rows, ky_local, col_count, kx_count = block.shape
+    width = col_count // ky_size
+    blocks = block.reshape(rows, ky_local, ky_size, width, kx_count)
+    received = []
+    for shift in range(ky_size):
+        piece = lax.dynamic_index_in_dim(blocks, (index + shift) % ky_size, 2, keepdims=False)
+        if shift:
+            pairs = [(i, (i + shift) % ky_size) for i in range(ky_size)]
+            piece = lax.ppermute(piece, "ky", pairs)
+        received.append(piece)
+    stacked = jnp.stack(received, 0)
+    stacked = jnp.take(stacked, (index - jnp.arange(ky_size)) % ky_size, axis=0)
+    stacked = jnp.moveaxis(stacked, 0, 1)
+    return stacked.reshape(rows, ky_size * ky_local, width, kx_count)
 
 
 def shards(distribution, region, region_doping, region_relax, equilibrium, kx_speed, upwind_sign):
@@ -140,7 +159,7 @@
     own_rows = lax.dynamic_slice_in_dim(sine_rows, row_start, row_count, 0)
     potential = POISSON * jnp.dot(own_rows, back_cols, precision=precise)
 
-    spread = lax.all_to_all(held, "ky", split_axis=2, concat_axis=1, tiled=True)
+    spread = spread_by_shifts(held)
     local_cols = spread.shape[2]
     forward, backward = wigner_tables(ky_count)
     weights = own_differences(potential, ky_count, lax.axis_index("ky") * local_cols, local_cols)

time: 266 us -> 350 us (1.32)
  the two profiles are of different devices: /device:TPU:47 before, /device:TPU:54 now
where the time goes in v12:
time: 350 us
  waiting for transfers between devices  196 us (56%)
  starting transfers between devices  98.4 us (28%)
  matrix products  24 us (7%)
  local copies, waits for them, and re-layouts  18.1 us (5%)
  other arithmetic  12.4 us (4%)
    ppermute x7, waiting for transfers between devices, spread_by_shifts(): piece = lax.ppermute(piece, 'ky', pairs)  101 us
    all_to_all x1, waiting for transfers between devices, shards(): lax.all_to_all(mixed, 'ky', split_axis=1, concat_axis=2, tiled=True)  86.9 us
    ppermute x7, starting transfers between devices, spread_by_shifts(): piece = lax.ppermute(piece, 'ky', pairs)  38.1 us
    ppermute x6, starting transfers between devices, gather_rows(): other = lax.ppermute(value, axis, xor_pairs(count, bit))  20.5 us
    ppermute x3, starting transfers between devices, sum_over(): value = value + lax.ppermute(value, axis, xor_pairs(count, bit))  20.1 us
    all_to_all x1, starting transfers between devices, shards(): lax.all_to_all(mixed, 'ky', split_axis=1, concat_axis=2, tiled=True)  15.1 us
    ppermute x6, waiting for transfers between devices, gather_rows(): other = lax.ppermute(value, axis, xor_pairs(count, bit))  7.26 us
  transfers between devices with their start and end apart: 19, of which 8 were waited for; matrix products, arithmetic and copies ran while one was open for 12% of the time, Pallas kernels for 0%

profile of v12, /device:TPU:54, one launch (start us, length us, event | category | flops | bytes accessed | tf_op | source)
XLA Modules:
  0.0 349.6 jit_solution(1023095536658896012)
XLA Ops:
  0.0 1.9 reduce_sum.27
  2.7 14.8 %collective-permute-start = (f32[1,2,256]{2,1,0:T(2,128)S(1)}, f32[1,2,256]{2,1,0:T(2,128)S(1)}, u32[]{:S(2)}, u32[]{:S(2)}) collective-permute-start(f32[1,2,256]{2,1,0:T(2,128)S(1)} %pad_maximum_fusion), channel_id=1, source_target_pairs={{0,4},{1,5},{2,6},{3,7},{4,0},{5,1},{6,2},{7,3},{8,12},{9,13},{10,... | collective-permute-start | bytes 6152 | tf_op jit(solution)/shard_map/ppermute | solution.py:67
  19.8 2.9 collective-permute-start.1
  23.3 2.0 collective-permute-done.1
  25.3 3.4 collective-permute-start.2
  29.3 2.4 collective-permute-done.2
  31.7 6.5 %collective-permute-start.3 = (f32[4,2,256]{2,1,0:T(2,128)S(1)}, f32[4,2,256]{2,1,0:T(2,128)S(1)}, u32[]{:S(2)}, u32[]{:S(2)}) collective-permute-start(f32[4,2,256]{2,1,0:T(2,128)S(1)} %maximum_select_fusion.4), channel_id=1, source_target_pairs={{0,256},{8,264},{16,272},{24,280},{32,288},{40,296},{48,304},{56,3... | collective-permute-start | bytes 24584 | tf_op jit(solution)/shard_map/ppermute | solution.py:75
  38.2 2.9 collective-permute-done.3
  41.1 1.9 collective-permute-start.11
  44.4 2.7 collective-permute-start.12
  47.2 2.4 fusion.51
  49.5 2.1 collective-permute-start.16
  51.7 3.0 collective-permute-start.13
  54.8 2.4 fusion.56
  57.1 2.5 collective-permute-start.17
  59.8 3.2 collective-permute-start.14
  63.2 2.1 collective-permute-start.10
  65.3 3.7 %collective-permute-start.4 = (f32[1,16,32,128]{3,2,1,0:T(8,128)S(1)}, f32[1,16,32,128]{3,2,1,0:T(8,128)S(1)}, u32[]{:S(2)}, u32[]{:S(2)}) collective-permute-start(f32[1,16,32,128]{3,2,1,0:T(8,128)S(1)} %get-tuple-element.29), channel_id=1, source_target_pairs={{0,1},{1,2},{2,3},{3,4},{4,5},{5,6},{6,7},{7,0},{8,9},{9,10},{10,1... | collective-permute-start | bytes 786440 | tf_op jit(solution)/shard_map/ppermute | solution.py:102
  69.1 0.7 bitcast_dynamic-update-slice_fusion.7
  69.8 12.3 %collective-permute-start.5 = (f32[1,16,32,128]{3,2,1,0:T(8,128)S(1)}, f32[1,16,32,128]{3,2,1,0:T(8,128)S(1)}, u32[]{:S(2)}, u32[]{:S(2)}) collective-permute-start(f32[1,16,32,128]{3,2,1,0:T(8,128)S(1)} %get-tuple-element.28), channel_id=1, source_target_pairs={{0,2},{1,3},{2,4},{3,5},{4,6},{5,7},{6,0},{7,1},{8,10},{9,11},{10,... | collective-permute-start | bytes 786440 | tf_op jit(solution)/shard_map/ppermute | solution.py:102
  82.2 13.9 %collective-permute-start.6 = (f32[1,16,32,128]{3,2,1,0:T(8,128)S(1)}, f32[1,16,32,128]{3,2,1,0:T(8,128)S(1)}, u32[]{:S(2)}, u32[]{:S(2)}) collective-permute-start(f32[1,16,32,128]{3,2,1,0:T(8,128)S(1)} %get-tuple-element.27), channel_id=1, source_target_pairs={{0,3},{1,4},{2,5},{3,6},{4,7},{5,0},{6,1},{7,2},{8,11},{9,12},{10,... | collective-permute-start | bytes 786440 | tf_op jit(solution)/shard_map/ppermute | solution.py:102
  96.1 0.7 bitcast_dynamic-update-slice_fusion.6
  96.9 19.6 %collective-permute-done.5 = f32[1,16,32,128]{3,2,1,0:T(8,128)S(1)} collective-permute-done((f32[1,16,32,128]{3,2,1,0:T(8,128)S(1)}, f32[1,16,32,128]{3,2,1,0:T(8,128)S(1)}, u32[]{:S(2)}, u32[]{:S(2)}) %collective-permute-start.5) | collective-permute-done | bytes 262176 | tf_op jit(solution)/shard_map/ppermute | solution.py:102
  116.5 2.2 collective-permute-start.7
  118.7 0.7 bitcast_dynamic-update-slice_fusion.5
  119.4 56.2 %collective-permute-done.6 = f32[1,16,32,128]{3,2,1,0:T(8,128)S(1)} collective-permute-done((f32[1,16,32,128]{3,2,1,0:T(8,128)S(1)}, f32[1,16,32,128]{3,2,1,0:T(8,128)S(1)}, u32[]{:S(2)}, u32[]{:S(2)}) %collective-permute-start.6) | collective-permute-done | bytes 262176 | tf_op jit(solution)/shard_map/ppermute | solution.py:102
  175.6 1.9 collective-permute-start.8
  177.5 0.7 bitcast_dynamic-update-slice_fusion.4
  178.2 1.9 collective-permute-start.9
  180.1 0.7 bitcast_dynamic-update-slice_fusion.3
  180.8 25.5 %collective-permute-done.8 = f32[1,16,32,128]{3,2,1,0:T(8,128)S(1)} collective-permute-done((f32[1,16,32,128]{3,2,1,0:T(8,128)S(1)}, f32[1,16,32,128]{3,2,1,0:T(8,128)S(1)}, u32[]{:S(2)}, u32[]{:S(2)}) %collective-permute-start.8) | collective-permute-done | bytes 262176 | tf_op jit(solution)/shard_map/ppermute | solution.py:102
  206.4 2.1 collective-permute-start.15
  210.7 3.6 %gather_fusion = f32[8,16,32,128]{3,2,1,0:T(8,128)} fusion(f32[8,16,32,128]{3,2,1,0:T(8,128)} %bitcast.19, s32[1024]{0:T(1024)S(1)} %pad_clamp_fusion), kind=kCustom, calls=%fused_computation | custom fusion | bytes 4194336 | tf_op jit(solution)/shard_map/jit(_take)/gather | solution.py:105
  214.8 1.0 add.333
  216.3 2.1 convolution_divide_fusion
  218.4 2.1 fusion.18
  220.7 4.5 %fusion.3 = f32[1,64,32]{2,0,1:T(1,128)S(1)} fusion(f32[256,1,1]{0,1,2:T(1,128)S(1)} %bitcast.119, s32[64,32]{1,0:T(8,128)S(1)} %copy-done.3, s32[64,32]{1,0:T(8,128)S(1)} %get-tuple-element.32), kind=kOutput, calls=%fused_computation.9 | convolution fusion | flops 8912896 | bytes 25600 | tf_op jit(solution)/shard_map/dot_general | solution.py:47
  225.6 1.4 copy-done.1
  226.9 2.7 fusion.1
  229.6 2.4 fusion.39
  232.0 3.1 copy.27
  235.0 15.1 %all-to-all-start = ((f32[1,128,32,128]{3,2,0,1:T(8,128)}), f32[1,128,32,128]{3,2,0,1:T(8,128)}, u32[]{:S(2)}, u32[]{:S(2)}) async-start(f32[1,128,32,128]{3,2,0,1:T(8,128)} %copy.27), calls=%async_computation | async-start | bytes 4194304 | tf_op jit(solution)/shard_map/all_to_all | solution.py:178
  250.9 1.9 fusion.54
  252.8 3.1 convolution_add_fusion
  255.9 3.0 multiply_add_fusion.1
  258.9 86.9 %all-to-all-done = f32[1,128,32,128]{3,2,0,1:T(8,128)} async-done(((f32[1,128,32,128]{3,2,0,1:T(8,128)}), f32[1,128,32,128]{3,2,0,1:T(8,128)}, u32[]{:S(2)}, u32[]{:S(2)}) %all-to-all-start) | async-done | bytes 2097184 | tf_op jit(solution)/shard_map/all_to_all | solution.py:178
  345.8 2.0 copy.28
  348.0 1.6 multiply_add_fusion
  (95 shorter events, 10.5 us)
Async XLA Ops:
  0.0 47.2 %copy-start = (f32[1,16,256,128]{3,2,1,0:T(8,128)S(1)}, f32[1,16,256,128]{3,2,1,0:T(8,128)}, u32[]{:S(2)}) copy-start(f32[1,16,256,128]{3,2,1,0:T(8,128)} %param.7) | copy-start | bytes 6291460
  0.0 2.0 copy-start.13
  0.0 2.0 copy-start.14
  0.0 2.0 copy-start.10
  0.0 18.2 %copy-start.12 = (s32[128]{0:T(128)S(1)}, s32[128]{0:T(128)}, u32[]{:S(2)}) copy-start(s32[128]{0:T(128)} %param.13) | copy-start | bytes 1540
  2.7 17.1 %collective-permute-start = (f32[1,2,256]{2,1,0:T(2,128)S(1)}, f32[1,2,256]{2,1,0:T(2,128)S(1)}, u32[]{:S(2)}, u32[]{:S(2)}) collective-permute-start(f32[1,2,256]{2,1,0:T(2,128)S(1)} %pad_maximum_fusion), channel_id=1, source_target_pairs={{0,4},{1,5},{2,6},{3,7},{4,0},{5,1},{6,2},{7,3},{8,12},{9,13},{10,... | collective-permute-start | bytes 6152 | tf_op jit(solution)/shard_map/ppermute | solution.py:67
  18.3 33.4 %copy-start.5 = (pred[128]{0:T(512)(128)(4,1)}, pred[128]{0:T(512)(128)(4,1)S(1)}, u32[]{:S(2)}) copy-start(pred[128]{0:T(512)(128)(4,1)S(1)} %get-tuple-element.37) | copy-start | bytes 388
  18.3 36.5 %copy-start.7 = (pred[128]{0:T(512)(128)(4,1)}, pred[128]{0:T(512)(128)(4,1)S(1)}, u32[]{:S(2)}) copy-start(pred[128]{0:T(512)(128)(4,1)S(1)} %get-tuple-element.34) | copy-start | bytes 388
  19.8 5.5 %collective-permute-start.1 = (f32[1,2,256]{2,1,0:T(2,128)S(1)}, f32[1,2,256]{2,1,0:T(2,128)S(1)}, u32[]{:S(2)}, u32[]{:S(2)}) collective-permute-start(f32[1,2,256]{2,1,0:T(2,128)S(1)} %fusion.108), channel_id=1, source_target_pairs={{0,64},{8,72},{16,80},{24,88},{32,96},{40,104},{48,112},{56,120},{... | collective-permute-start | bytes 6152 | tf_op jit(solution)/shard_map/ppermute | solution.py:75
  25.3 6.4 %collective-permute-start.2 = (f32[2,2,256]{2,1,0:T(2,128)S(1)}, f32[2,2,256]{2,1,0:T(2,128)S(1)}, u32[]{:S(2)}, u32[]{:S(2)}) collective-permute-start(f32[2,2,256]{2,1,0:T(2,128)S(1)} %maximum_select_fusion.5), channel_id=1, source_target_pairs={{0,128},{8,136},{16,144},{24,152},{32,160},{40,168},{48,176},{56,1... | collective-permute-start | bytes 12296 | tf_op jit(solution)/shard_map/ppermute | solution.py:75
  31.7 9.4 %collective-permute-start.3 = (f32[4,2,256]{2,1,0:T(2,128)S(1)}, f32[4,2,256]{2,1,0:T(2,128)S(1)}, u32[]{:S(2)}, u32[]{:S(2)}) collective-permute-start(f32[4,2,256]{2,1,0:T(2,128)S(1)} %maximum_select_fusion.4), channel_id=1, source_target_pairs={{0,256},{8,264},{16,272},{24,280},{32,288},{40,296},{48,304},{56,3... | collective-permute-start | bytes 24584 | tf_op jit(solution)/shard_map/ppermute | solution.py:75
  41.1 3.2 collective-permute-start.11
  44.4 7.3 %collective-permute-start.12 = (f32[16,2,256]{2,1,0:T(2,128)S(1)}, f32[16,2,256]{2,1,0:T(2,128)S(1)}, u32[]{:S(2)}, u32[]{:S(2)}) collective-permute-start(f32[16,2,256]{2,1,0:T(2,128)S(1)} %maximum_select_fusion.2), channel_id=1, source_target_pairs={{0,16},{8,24},{16,0},{24,8},{32,48},{40,56},{48,32},{56,40},{64,80... | collective-permute-start | bytes 98312 | tf_op jit(solution)/shard_map/ppermute | solution.py:75
  49.5 182.4 %collective-permute-start.16 = (f32[4096,64]{0,1:T(8,128)}, f32[4096,64]{0,1:T(8,128)}, u32[]{:S(2)}, u32[]{:S(2)}) collective-permute-start(f32[4096,64]{0,1:T(8,128)} %fusion.51), channel_id=1, source_target_pairs={{0,8},{8,16},{16,24},{24,32},{32,40},{40,48},{48,56},{56,64},{64,7... | collective-permute-start | bytes 3145736 | tf_op jit(solution)/shard_map/ppermute | solution.py:144
  51.7 8.0 %collective-permute-start.13 = (f32[32,2,256]{2,1,0:T(2,128)S(1)}, f32[32,2,256]{2,1,0:T(2,128)S(1)}, u32[]{:S(2)}, u32[]{:S(2)}) collective-permute-start(f32[32,2,256]{2,1,0:T(2,128)S(1)} %maximum_select_fusion.1), channel_id=1, source_target_pairs={{0,32},{8,40},{16,48},{24,56},{32,0},{40,8},{48,16},{56,24},{64,96... | collective-permute-start | bytes 196616 | tf_op jit(solution)/shard_map/ppermute | solution.py:75
  57.1 174.8 %collective-permute-start.17 = (f32[4096,64]{0,1:T(8,128)}, f32[4096,64]{0,1:T(8,128)S(1)}, u32[]{:S(2)}, u32[]{:S(2)}) collective-permute-start(f32[4096,64]{0,1:T(8,128)} %fusion.56), channel_id=1, source_target_pairs={{8,0},{16,8},{24,16},{32,24},{40,32},{48,40},{56,48},{64,56},{72,6... | collective-permute-start | bytes 3145736 | tf_op jit(solution)/shard_map/ppermute | solution.py:145
  59.8 10.0 %collective-permute-start.14 = (f32[64,2,256]{2,1,0:T(2,128)S(1)}, f32[64,2,256]{2,1,0:T(2,128)S(1)}, u32[]{:S(2)}, u32[]{:S(2)}) collective-permute-start(f32[64,2,256]{2,1,0:T(2,128)S(1)} %bitcast.111), channel_id=1, source_target_pairs={{0,1},{1,0},{2,3},{3,2},{4,5},{5,4},{6,7},{7,6},{8,9},{9,8},{10,11... | collective-permute-start | bytes 393224 | tf_op jit(solution)/shard_map/ppermute | solution.py:67
  63.2 146.7 %collective-permute-start.10 = (f32[1,16,32,128]{3,2,1,0:T(8,128)S(1)}, f32[1,16,32,128]{3,2,1,0:T(8,128)S(1)}, u32[]{:S(2)}, u32[]{:S(2)}) collective-permute-start(f32[1,16,32,128]{3,2,1,0:T(8,128)S(1)} %get-tuple-element.23), channel_id=1, source_target_pairs={{0,7},{1,0},{2,1},{3,2},{4,3},{5,4},{6,5},{7,6},{8,15},{9,8},{10,9... | collective-permute-start | bytes 786440 | tf_op jit(solution)/shard_map/ppermute | solution.py:102
  65.3 16.9 %collective-permute-start.4 = (f32[1,16,32,128]{3,2,1,0:T(8,128)S(1)}, f32[1,16,32,128]{3,2,1,0:T(8,128)S(1)}, u32[]{:S(2)}, u32[]{:S(2)}) collective-permute-start(f32[1,16,32,128]{3,2,1,0:T(8,128)S(1)} %get-tuple-element.29), channel_id=1, source_target_pairs={{0,1},{1,2},{2,3},{3,4},{4,5},{5,6},{6,7},{7,0},{8,9},{9,10},{10,1... | collective-permute-start | bytes 786440 | tf_op jit(solution)/shard_map/ppermute | solution.py:102
  69.8 46.7 %collective-permute-start.5 = (f32[1,16,32,128]{3,2,1,0:T(8,128)S(1)}, f32[1,16,32,128]{3,2,1,0:T(8,128)S(1)}, u32[]{:S(2)}, u32[]{:S(2)}) collective-permute-start(f32[1,16,32,128]{3,2,1,0:T(8,128)S(1)} %get-tuple-element.28), channel_id=1, source_target_pairs={{0,2},{1,3},{2,4},{3,5},{4,6},{5,7},{6,0},{7,1},{8,10},{9,11},{10,... | collective-permute-start | bytes 786440 | tf_op jit(solution)/shard_map/ppermute | solution.py:102
  82.2 93.4 %collective-permute-start.6 = (f32[1,16,32,128]{3,2,1,0:T(8,128)S(1)}, f32[1,16,32,128]{3,2,1,0:T(8,128)S(1)}, u32[]{:S(2)}, u32[]{:S(2)}) collective-permute-start(f32[1,16,32,128]{3,2,1,0:T(8,128)S(1)} %get-tuple-element.27), channel_id=1, source_target_pairs={{0,3},{1,4},{2,5},{3,6},{4,7},{5,0},{6,1},{7,2},{8,11},{9,12},{10,... | collective-permute-start | bytes 786440 | tf_op jit(solution)/shard_map/ppermute | solution.py:102
  116.5 61.7 %collective-permute-start.7 = (f32[1,16,32,128]{3,2,1,0:T(8,128)S(1)}, f32[1,16,32,128]{3,2,1,0:T(8,128)S(1)}, u32[]{:S(2)}, u32[]{:S(2)}) collective-permute-start(f32[1,16,32,128]{3,2,1,0:T(8,128)S(1)} %get-tuple-element.26), channel_id=1, source_target_pairs={{0,4},{1,5},{2,6},{3,7},{4,0},{5,1},{6,2},{7,3},{8,12},{9,13},{10,... | collective-permute-start | bytes 786440 | tf_op jit(solution)/shard_map/ppermute | solution.py:102
  175.6 30.8 %collective-permute-start.8 = (f32[1,16,32,128]{3,2,1,0:T(8,128)S(1)}, f32[1,16,32,128]{3,2,1,0:T(8,128)S(1)}, u32[]{:S(2)}, u32[]{:S(2)}) collective-permute-start(f32[1,16,32,128]{3,2,1,0:T(8,128)S(1)} %get-tuple-element.25), channel_id=1, source_target_pairs={{0,5},{1,6},{2,7},{3,0},{4,1},{5,2},{6,3},{7,4},{8,13},{9,14},{10,... | collective-permute-start | bytes 786440 | tf_op jit(solution)/shard_map/ppermute | solution.py:102
  178.2 31.0 %collective-permute-start.9 = (f32[1,16,32,128]{3,2,1,0:T(8,128)S(1)}, f32[1,16,32,128]{3,2,1,0:T(8,128)S(1)}, u32[]{:S(2)}, u32[]{:S(2)}) collective-permute-start(f32[1,16,32,128]{3,2,1,0:T(8,128)S(1)} %get-tuple-element.24), channel_id=1, source_target_pairs={{0,6},{1,7},{2,0},{3,1},{4,2},{5,3},{6,4},{7,5},{8,14},{9,15},{10,... | collective-permute-start | bytes 786440 | tf_op jit(solution)/shard_map/ppermute | solution.py:102
  206.4 8.5 %collective-permute-start.15 = (f32[64,2,256]{2,1,0:T(2,128)S(1)}, f32[64,2,256]{2,1,0:T(2,128)}, u32[]{:S(2)}, u32[]{:S(2)}) collective-permute-start(f32[64,2,256]{2,1,0:T(2,128)S(1)} %bitcast_add_fusion), channel_id=1, source_target_pairs={{0,2},{1,3},{2,0},{3,1},{4,6},{5,7},{6,4},{7,5},{8,10},{9,11},{10,... | collective-permute-start | bytes 393224 | tf_op jit(solution)/shard_map/ppermute | solution.py:67
  214.3 6.4 %copy-start.3 = (s32[64,32]{1,0:T(8,128)S(1)}, s32[64,32]{1,0:T(8,128)}, u32[]{:S(2)}) copy-start(s32[64,32]{1,0:T(8,128)} %get-tuple-element.33) | copy-start | bytes 24580
  220.7 4.9 %copy-start.11 = (pred[128]{0:T(512)(128)(4,1)S(1)}, pred[128]{0:T(512)(128)(4,1)}, u32[]{:S(2)}) copy-start(pred[128]{0:T(512)(128)(4,1)} %broadcast_in_dim.36) | copy-start | bytes 388
  225.3 1.6 copy-start.1
  235.0 15.1 %copy-start.15 = (f32[128]{0:T(128)S(1)}, f32[128]{0:T(128)}, u32[]{:S(2)}) copy-start(f32[128]{0:T(128)} %param.12) | copy-start | bytes 1540
  235.0 110.7 %all-to-all-start = ((f32[1,128,32,128]{3,2,0,1:T(8,128)}), f32[1,128,32,128]{3,2,0,1:T(8,128)}, u32[]{:S(2)}, u32[]{:S(2)}) async-start(f32[1,128,32,128]{3,2,0,1:T(8,128)} %copy.27), calls=%async_computation | async-start | bytes 4194304 | tf_op jit(solution)/shard_map/all_to_all | solution.py:178
  250.2 0.7 copy-start.8
  250.6 2.1 copy-start.6
  252.7 3.1 copy-start.4
  252.8 3.1 copy-start.9
  345.8 2.2 copy-start.2

commit v13 on v10

--- a/solution.py
+++ b/solution.py
@@ -109,7 +109,6 @@
     far_bits = [bit for bit in (8, 16, 32) if bit < space_count]
     near_bits = [bit for bit in (1, 2, 4) if bit < space_count]
     far_rows = gather_rows(charge, "space", far_bits)
-    held, far_rows = lax.optimization_barrier((distribution, far_rows))
     positive_kx = upwind_sign > 0
     half_kx = kx_count // 2
     rank_pos = jnp.cumsum(positive_kx.astype(jnp.int32)) - 1
@@ -117,9 +116,12 @@
     slots = jnp.arange(half_kx, dtype=jnp.int32)
     pick_pos = (positive_kx[:, None] & (rank_pos[:, None] == slots[None, :])).astype(jnp.float32)
     pick_neg = ((~positive_kx)[:, None] & (rank_neg[:, None] == slots[None, :])).astype(jnp.float32)
-    flat = held.reshape(-1, kx_count)
+    flat = distribution.reshape(-1, kx_count)
     send_right = jnp.dot(flat, pick_pos, precision=precise)
     send_left = jnp.dot(flat, pick_neg, precision=precise)
+    held, far_rows, send_right, send_left = lax.optimization_barrier(
+        (distribution, far_rows, send_right, send_left)
+    )
     forward_pairs = [(i, i + 1) for i in range(space_count - 1)]
     backward_pairs = [(i + 1, i) for i in range(space_count - 1)]
     got_left = lax.ppermute(send_right, "space", forward_pairs)

time: 266 us -> 274 us (1.030)
  the two profiles are of different devices: /device:TPU:47 before, /device:TPU:415 now
where the time goes in v13:
time: 274 us; the launch traced here: 273 us
  waiting for transfers between devices  158 us (58%)
  starting transfers between devices  67.9 us (25%)
  matrix products  24 us (9%)
  other arithmetic  11.6 us (4%)
  local copies, waits for them, and re-layouts  11.2 us (4%)
    ppermute x1, waiting for transfers between devices, shards(): got_right = lax.ppermute(send_left, 'space', backward_pairs)  73.5 us
    all_to_all x1, waiting for transfers between devices, shards(): spread = lax.all_to_all(held, 'ky', split_axis=2, concat_axis=1, tiled=True)  28.6 us
    ppermute x6, starting transfers between devices, gather_rows(): other = lax.ppermute(value, axis, xor_pairs(count, bit))  24.1 us
    all_to_all x1, waiting for transfers between devices, shards(): lax.all_to_all(mixed, 'ky', split_axis=1, concat_axis=2, tiled=True)  17.9 us
    ppermute x1, waiting for transfers between devices, shards(): got_left = lax.ppermute(send_right, 'space', forward_pairs)  16.9 us
    all_to_all x1, starting transfers between devices, shards(): spread = lax.all_to_all(held, 'ky', split_axis=2, concat_axis=1, tiled=True)  13.7 us
    all_to_all x1, starting transfers between devices, shards(): lax.all_to_all(mixed, 'ky', split_axis=1, concat_axis=2, tiled=True)  13.7 us
    ppermute x3, waiting for transfers between devices, sum_over(): value = value + lax.ppermute(value, axis, xor_pairs(count, bit))  12.1 us
  transfers between devices with their start and end apart: 13, of which 11 were waited for; matrix products, arithmetic and copies ran while one was open for 13% of the time, Pallas kernels for 0%

profile of v13, /device:TPU:415, one launch (start us, length us, event | category | flops | bytes accessed | tf_op | source)
XLA Modules:
  0.0 273.3 jit_solution(15454337313970736624)
XLA Ops:
  0.0 1.9 reduce_sum.27
  2.0 0.7 fusion.84
  2.7 3.4 %collective-permute-start = (f32[1,2,256]{2,1,0:T(2,128)S(1)}, f32[1,2,256]{2,1,0:T(2,128)S(1)}, u32[]{:S(2)}, u32[]{:S(2)}) collective-permute-start(f32[1,2,256]{2,1,0:T(2,128)S(1)} %pad_maximum_fusion), channel_id=1, source_target_pairs={{0,4},{1,5},{2,6},{3,7},{4,0},{5,1},{6,2},{7,3},{8,12},{9,13},{10,... | collective-permute-start | bytes 6152 | tf_op jit(solution)/shard_map/ppermute | solution.py:67
  6.5 9.2 %collective-permute-done = f32[1,2,256]{2,1,0:T(2,128)S(1)} collective-permute-done((f32[1,2,256]{2,1,0:T(2,128)S(1)}, f32[1,2,256]{2,1,0:T(2,128)S(1)}, u32[]{:S(2)}, u32[]{:S(2)}) %collective-permute-start) | collective-permute-done | bytes 2080 | tf_op jit(solution)/shard_map/ppermute | solution.py:67
  15.8 2.6 collective-permute-start.1
  18.4 1.4 convolution_bitcast_fusion.1
  20.1 3.1 %collective-permute-start.2 = (f32[2,2,256]{2,1,0:T(2,128)S(1)}, f32[2,2,256]{2,1,0:T(2,128)S(1)}, u32[]{:S(2)}, u32[]{:S(2)}) collective-permute-start(f32[2,2,256]{2,1,0:T(2,128)S(1)} %maximum_select_fusion.5), channel_id=1, source_target_pairs={{0,128},{8,136},{16,144},{24,152},{32,160},{40,168},{48,176},{56,1... | collective-permute-start | bytes 12296 | tf_op jit(solution)/shard_map/ppermute | solution.py:75
  23.3 2.0 collective-permute-done.2
  25.4 5.2 %collective-permute-start.3 = (f32[4,2,256]{2,1,0:T(2,128)S(1)}, f32[4,2,256]{2,1,0:T(2,128)S(1)}, u32[]{:S(2)}, u32[]{:S(2)}) collective-permute-start(f32[4,2,256]{2,1,0:T(2,128)S(1)} %maximum_select_fusion.4), channel_id=1, source_target_pairs={{0,256},{8,264},{16,272},{24,280},{32,288},{40,296},{48,304},{56,3... | collective-permute-start | bytes 24584 | tf_op jit(solution)/shard_map/ppermute | solution.py:75
  30.6 2.4 convolution_bitcast_fusion.2
  32.9 0.8 collective-permute-done.3
  33.7 2.5 copy.30
  36.2 13.7 %all-to-all-start = ((f32[1,16,256,128]{3,1,0,2:T(8,128)}), f32[1,16,256,128]{3,1,0,2:T(8,128)}, u32[]{:S(2)}, u32[]{:S(2)}) async-start(f32[1,16,256,128]{3,1,0,2:T(8,128)} %copy.30), calls=%async_computation | async-start | bytes 4194304 | tf_op jit(solution)/shard_map/all_to_all | solution.py:145
  50.0 0.3 fusion.64
  50.3 7.7 %collective-permute-start.4 = (f32[8,2,256]{2,1,0:T(2,128)S(1)}, f32[8,2,256]{2,1,0:T(2,128)S(1)}, u32[]{:S(2)}, u32[]{:S(2)}) collective-permute-start(f32[8,2,256]{2,1,0:T(2,128)S(1)} %maximum_select_fusion.3), channel_id=1, source_target_pairs={{0,8},{8,0},{16,24},{24,16},{32,40},{40,32},{48,56},{56,48},{64,72... | collective-permute-start | bytes 49160 | tf_op jit(solution)/shard_map/ppermute | solution.py:75
  58.0 0.8 collective-permute-done.4
  58.8 2.5 collective-permute-start.5
  61.3 0.7 broadcast_add_fusion
  62.0 1.9 collective-permute-done.5
  63.9 3.0 %collective-permute-start.6 = (f32[32,2,256]{2,1,0:T(2,128)S(1)}, f32[32,2,256]{2,1,0:T(2,128)S(1)}, u32[]{:S(2)}, u32[]{:S(2)}) collective-permute-start(f32[32,2,256]{2,1,0:T(2,128)S(1)} %maximum_select_fusion.1), channel_id=1, source_target_pairs={{0,32},{8,40},{16,48},{24,56},{32,0},{40,8},{48,16},{56,24},{64,96... | collective-permute-start | bytes 196616 | tf_op jit(solution)/shard_map/ppermute | solution.py:75
  67.2 3.7 %collective-permute-done.6 = f32[32,2,256]{2,1,0:T(2,128)S(1)} collective-permute-done((f32[32,2,256]{2,1,0:T(2,128)S(1)}, f32[32,2,256]{2,1,0:T(2,128)S(1)}, u32[]{:S(2)}, u32[]{:S(2)}) %collective-permute-start.6) | collective-permute-done | bytes 65568 | tf_op jit(solution)/shard_map/ppermute | solution.py:75
  70.9 2.5 collective-permute-start.7
  73.6 0.5 iota_add_fusion
  74.1 2.9 %collective-permute-done.7 = f32[64,2,256]{2,1,0:T(2,128)S(1)} collective-permute-done((f32[64,2,256]{2,1,0:T(2,128)S(1)}, f32[64,2,256]{2,1,0:T(2,128)S(1)}, u32[]{:S(2)}, u32[]{:S(2)}) %collective-permute-start.7) | collective-permute-done | bytes 131104 | tf_op jit(solution)/shard_map/ppermute | solution.py:67
  77.1 3.1 %collective-permute-start.8 = (f32[64,2,256]{2,1,0:T(2,128)S(1)}, f32[64,2,256]{2,1,0:T(2,128)}, u32[]{:S(2)}, u32[]{:S(2)}) collective-permute-start(f32[64,2,256]{2,1,0:T(2,128)S(1)} %bitcast_add_fusion), channel_id=1, source_target_pairs={{0,2},{1,3},{2,0},{3,1},{4,6},{5,7},{6,4},{7,5},{8,10},{9,11},{10,... | collective-permute-start | bytes 393224 | tf_op jit(solution)/shard_map/ppermute | solution.py:67
  80.2 0.5 multiply_multiply_fusion.1
  80.8 5.3 %collective-permute-start.9 = (f32[4096,64]{0,1:T(8,128)}, f32[4096,64]{0,1:T(8,128)}, u32[]{:S(2)}, u32[]{:S(2)}) collective-permute-start(f32[4096,64]{0,1:T(8,128)} %convolution_bitcast_fusion.2), channel_id=1, source_target_pairs={{0,8},{8,16},{16,24},{24,32},{32,40},{40,48},{48,56},{56,64},{64,7... | collective-permute-start | bytes 3145736 | tf_op jit(solution)/shard_map/ppermute | solution.py:127
  86.1 2.1 collective-permute-start.10
  88.2 1.0 add.203
  89.3 0.4 fusion.42
  89.7 2.0 convolution_divide_fusion
  91.7 2.0 fusion.17
  93.9 4.5 %fusion.4 = f32[1,64,32]{2,0,1:T(1,128)S(1)} fusion(f32[256,1,1]{0,1,2:T(1,128)S(1)} %bitcast.87, s32[64,32]{1,0:T(8,128)S(1)} %copy-done.2, s32[64,32]{1,0:T(8,128)S(1)} %get-tuple-element.29), kind=kOutput, calls=%fused_computation.10 | convolution fusion | flops 8912896 | bytes 25600 | tf_op jit(solution)/shard_map/dot_general | solution.py:47
  98.6 28.6 %all-to-all-done = f32[1,16,256,128]{3,1,0,2:T(8,128)} async-done(((f32[1,16,256,128]{3,1,0,2:T(8,128)}), f32[1,16,256,128]{3,1,0,2:T(8,128)}, u32[]{:S(2)}, u32[]{:S(2)}) %all-to-all-start) | async-done | bytes 2097184 | tf_op jit(solution)/shard_map/all_to_all | solution.py:145
  127.2 2.2 copy.31
  129.6 2.6 fusion.1
  132.2 2.4 fusion.38
  134.6 16.9 %collective-permute-done.9 = f32[4096,64]{0,1:T(8,128)} collective-permute-done((f32[4096,64]{0,1:T(8,128)}, f32[4096,64]{0,1:T(8,128)}, u32[]{:S(2)}, u32[]{:S(2)}) %collective-permute-start.9) | collective-permute-done | bytes 1048608 | tf_op jit(solution)/shard_map/ppermute | solution.py:127
  151.5 73.5 %collective-permute-done.10 = f32[4096,64]{0,1:T(8,128)} collective-permute-done((f32[4096,64]{0,1:T(8,128)S(1)}, f32[4096,64]{0,1:T(8,128)}, u32[]{:S(2)}, u32[]{:S(2)}) %collective-permute-start.10) | collective-permute-done | bytes 1048608 | tf_op jit(solution)/shard_map/ppermute | solution.py:128
  224.9 3.1 %copy.33 = f32[1,128,32,128]{3,2,0,1:T(8,128)} copy(f32[1,128,32,128]{1,3,2,0:T(8,128)} %bitcast.77) | data formatting | bytes 4194304 | tf_op jit(solution)/shard_map/optimization_barrier | solution.py:160
  228.0 13.7 %all-to-all-start.1 = ((f32[1,128,32,128]{3,2,0,1:T(8,128)}), f32[1,128,32,128]{3,2,0,1:T(8,128)}, u32[]{:S(2)}, u32[]{:S(2)}) async-start(f32[1,128,32,128]{3,2,0,1:T(8,128)} %copy.33), calls=%async_computation.1 | async-start | bytes 4194304 | tf_op jit(solution)/shard_map/all_to_all | solution.py:161
  241.8 0.4 fusion.106
  242.3 3.1 %fusion.52 = f32[4096,128]{1,0:T(8,128)S(1)} fusion(f32[4096,64]{0,1:T(8,128)} %collective-permute-done.10, s32[128]{0:T(128)S(1)} %add_reduce_fusion, pred[128]{0:T(512)(128)(4,1)S(1)} %copy-done.5), kind=kOutput, calls=%fused_computation.70 | convolution fusion | flops 402669568 | bytes 3146368 | tf_op jit(solution)/shard_map/dot_general | solution.py:163
  245.5 3.1 %convolution_add_fusion = f32[4096,128]{1,0:T(8,128)S(1)} fusion(f32[4096,128]{1,0:T(8,128)S(1)} %fusion.52, f32[4096,64]{0,1:T(8,128)} %collective-permute-done.9, s32[128]{0:T(128)S(1)} %add_reduce_fusion.1, pred[128]{0:T(512)(128)(4,1)S(1)} %get-tuple-element.38), kind=kOutput, calls=%fused_computation | convolution fusion | flops 403193856 | bytes 5243520 | tf_op jit(solution)/shard_map/dot_general | solution.py:163
  248.6 3.0 %multiply_add_fusion.1 = f32[1,16,256,128]{3,2,1,0:T(8,128)} fusion(f32[1,16,256,128]{3,2,1,0:T(8,128)S(1)} %copy-done, f32[1,16,255,128]{3,2,1,0:T(8,128)S(1)} %get-tuple-element.26, f32[1,16,255,128]{3,2,1,0:T(8,128)S(1)} %get-tuple-element.25, f32[1,16,256,128]{3,2,1,0:T(8,128)S(1)} %bitcast.78, f32[16,128]{1,0:T(8,128)S(1)} %copy-done.3, ...), kind=kLoop, calls=%fused_computation.9 | loop fusion | flops 6291456 | bytes 10480208 | tf_op jit(solution)/shard_map/add | solution.py:180
  251.6 17.9 %all-to-all-done.1 = f32[1,128,32,128]{3,2,0,1:T(8,128)} async-done(((f32[1,128,32,128]{3,2,0,1:T(8,128)}), f32[1,128,32,128]{3,2,0,1:T(8,128)}, u32[]{:S(2)}, u32[]{:S(2)}) %all-to-all-start.1) | async-done | bytes 2097184 | tf_op jit(solution)/shard_map/all_to_all | solution.py:161
  269.5 2.0 copy.34
  271.7 1.6 multiply_add_fusion
  (62 shorter events, 2.6 us)
Async XLA Ops:
  0.0 18.4 %copy-start = (f32[1,16,256,128]{3,2,1,0:T(8,128)S(1)}, f32[1,16,256,128]{3,2,1,0:T(8,128)}, u32[]{:S(2)}) copy-start(f32[1,16,256,128]{3,2,1,0:T(8,128)} %param.7) | copy-start | bytes 6291460
  0.0 2.0 copy-start.9
  0.0 2.0 copy-start.10
  0.0 2.0 copy-start.7
  0.0 6.0 %copy-start.8 = (s32[128]{0:T(128)S(1)}, s32[128]{0:T(128)}, u32[]{:S(2)}) copy-start(s32[128]{0:T(128)} %param.13) | copy-start | bytes 1540
  2.7 13.0 %collective-permute-start = (f32[1,2,256]{2,1,0:T(2,128)S(1)}, f32[1,2,256]{2,1,0:T(2,128)S(1)}, u32[]{:S(2)}, u32[]{:S(2)}) collective-permute-start(f32[1,2,256]{2,1,0:T(2,128)S(1)} %pad_maximum_fusion), channel_id=1, source_target_pairs={{0,4},{1,5},{2,6},{3,7},{4,0},{5,1},{6,2},{7,3},{8,12},{9,13},{10,... | collective-permute-start | bytes 6152 | tf_op jit(solution)/shard_map/ppermute | solution.py:67
  6.1 14.0 %copy-start.4 = (pred[128]{0:T(512)(128)(4,1)}, pred[128]{0:T(512)(128)(4,1)S(1)}, u32[]{:S(2)}) copy-start(pred[128]{0:T(512)(128)(4,1)S(1)} %get-tuple-element.35) | copy-start | bytes 388
  15.8 4.3 %collective-permute-start.1 = (f32[1,2,256]{2,1,0:T(2,128)S(1)}, f32[1,2,256]{2,1,0:T(2,128)S(1)}, u32[]{:S(2)}, u32[]{:S(2)}) collective-permute-start(f32[1,2,256]{2,1,0:T(2,128)S(1)} %fusion.104), channel_id=1, source_target_pairs={{0,64},{8,72},{16,80},{24,88},{32,96},{40,104},{48,112},{56,120},{... | collective-permute-start | bytes 6152 | tf_op jit(solution)/shard_map/ppermute | solution.py:75
  20.1 5.3 %collective-permute-start.2 = (f32[2,2,256]{2,1,0:T(2,128)S(1)}, f32[2,2,256]{2,1,0:T(2,128)S(1)}, u32[]{:S(2)}, u32[]{:S(2)}) collective-permute-start(f32[2,2,256]{2,1,0:T(2,128)S(1)} %maximum_select_fusion.5), channel_id=1, source_target_pairs={{0,128},{8,136},{16,144},{24,152},{32,160},{40,168},{48,176},{56,1... | collective-permute-start | bytes 12296 | tf_op jit(solution)/shard_map/ppermute | solution.py:75
  25.4 8.3 %collective-permute-start.3 = (f32[4,2,256]{2,1,0:T(2,128)S(1)}, f32[4,2,256]{2,1,0:T(2,128)S(1)}, u32[]{:S(2)}, u32[]{:S(2)}) collective-permute-start(f32[4,2,256]{2,1,0:T(2,128)S(1)} %maximum_select_fusion.4), channel_id=1, source_target_pairs={{0,256},{8,264},{16,272},{24,280},{32,288},{40,296},{48,304},{56,3... | collective-permute-start | bytes 24584 | tf_op jit(solution)/shard_map/ppermute | solution.py:75
  36.2 91.0 %all-to-all-start = ((f32[1,16,256,128]{3,1,0,2:T(8,128)}), f32[1,16,256,128]{3,1,0,2:T(8,128)}, u32[]{:S(2)}, u32[]{:S(2)}) async-start(f32[1,16,256,128]{3,1,0,2:T(8,128)} %copy.30), calls=%async_computation | async-start | bytes 4194304 | tf_op jit(solution)/shard_map/all_to_all | solution.py:145
  50.3 8.5 %collective-permute-start.4 = (f32[8,2,256]{2,1,0:T(2,128)S(1)}, f32[8,2,256]{2,1,0:T(2,128)S(1)}, u32[]{:S(2)}, u32[]{:S(2)}) collective-permute-start(f32[8,2,256]{2,1,0:T(2,128)S(1)} %maximum_select_fusion.3), channel_id=1, source_target_pairs={{0,8},{8,0},{16,24},{24,16},{32,40},{40,32},{48,56},{56,48},{64,72... | collective-permute-start | bytes 49160 | tf_op jit(solution)/shard_map/ppermute | solution.py:75
  58.8 5.1 %collective-permute-start.5 = (f32[16,2,256]{2,1,0:T(2,128)S(1)}, f32[16,2,256]{2,1,0:T(2,128)S(1)}, u32[]{:S(2)}, u32[]{:S(2)}) collective-permute-start(f32[16,2,256]{2,1,0:T(2,128)S(1)} %maximum_select_fusion.2), channel_id=1, source_target_pairs={{0,16},{8,24},{16,0},{24,8},{32,48},{40,56},{48,32},{56,40},{64,80... | collective-permute-start | bytes 98312 | tf_op jit(solution)/shard_map/ppermute | solution.py:75
  63.9 6.9 %collective-permute-start.6 = (f32[32,2,256]{2,1,0:T(2,128)S(1)}, f32[32,2,256]{2,1,0:T(2,128)S(1)}, u32[]{:S(2)}, u32[]{:S(2)}) collective-permute-start(f32[32,2,256]{2,1,0:T(2,128)S(1)} %maximum_select_fusion.1), channel_id=1, source_target_pairs={{0,32},{8,40},{16,48},{24,56},{32,0},{40,8},{48,16},{56,24},{64,96... | collective-permute-start | bytes 196616 | tf_op jit(solution)/shard_map/ppermute | solution.py:75
  70.9 6.1 %collective-permute-start.7 = (f32[64,2,256]{2,1,0:T(2,128)S(1)}, f32[64,2,256]{2,1,0:T(2,128)S(1)}, u32[]{:S(2)}, u32[]{:S(2)}) collective-permute-start(f32[64,2,256]{2,1,0:T(2,128)S(1)} %bitcast.79), channel_id=1, source_target_pairs={{0,1},{1,0},{2,3},{3,2},{4,5},{5,4},{6,7},{7,6},{8,9},{9,8},{10,11... | collective-permute-start | bytes 393224 | tf_op jit(solution)/shard_map/ppermute | solution.py:67
  77.1 11.1 %collective-permute-start.8 = (f32[64,2,256]{2,1,0:T(2,128)S(1)}, f32[64,2,256]{2,1,0:T(2,128)}, u32[]{:S(2)}, u32[]{:S(2)}) collective-permute-start(f32[64,2,256]{2,1,0:T(2,128)S(1)} %bitcast_add_fusion), channel_id=1, source_target_pairs={{0,2},{1,3},{2,0},{3,1},{4,6},{5,7},{6,4},{7,5},{8,10},{9,11},{10,... | collective-permute-start | bytes 393224 | tf_op jit(solution)/shard_map/ppermute | solution.py:67
  80.7 13.2 %copy-start.2 = (s32[64,32]{1,0:T(8,128)S(1)}, s32[64,32]{1,0:T(8,128)}, u32[]{:S(2)}) copy-start(s32[64,32]{1,0:T(8,128)} %get-tuple-element.30) | copy-start | bytes 24580
  80.8 70.7 %collective-permute-start.9 = (f32[4096,64]{0,1:T(8,128)}, f32[4096,64]{0,1:T(8,128)}, u32[]{:S(2)}, u32[]{:S(2)}) collective-permute-start(f32[4096,64]{0,1:T(8,128)} %convolution_bitcast_fusion.2), channel_id=1, source_target_pairs={{0,8},{8,16},{16,24},{24,32},{32,40},{40,48},{48,56},{56,64},{64,7... | collective-permute-start | bytes 3145736 | tf_op jit(solution)/shard_map/ppermute | solution.py:127
  86.1 138.8 %collective-permute-start.10 = (f32[4096,64]{0,1:T(8,128)S(1)}, f32[4096,64]{0,1:T(8,128)}, u32[]{:S(2)}, u32[]{:S(2)}) collective-permute-start(f32[4096,64]{0,1:T(8,128)S(1)} %convolution_bitcast_fusion.1), channel_id=1, source_target_pairs={{8,0},{16,8},{24,16},{32,24},{40,32},{48,40},{56,48},{64,56},{72,6... | collective-permute-start | bytes 3145736 | tf_op jit(solution)/shard_map/ppermute | solution.py:128
  228.0 13.7 %copy-start.11 = (f32[128]{0:T(128)S(1)}, f32[128]{0:T(128)}, u32[]{:S(2)}) copy-start(f32[128]{0:T(128)} %param.12) | copy-start | bytes 1540
  228.0 41.5 %all-to-all-start.1 = ((f32[1,128,32,128]{3,2,0,1:T(8,128)}), f32[1,128,32,128]{3,2,0,1:T(8,128)}, u32[]{:S(2)}, u32[]{:S(2)}) async-start(f32[1,128,32,128]{3,2,0,1:T(8,128)} %copy.33), calls=%async_computation.1 | async-start | bytes 4194304 | tf_op jit(solution)/shard_map/all_to_all | solution.py:161
  241.7 0.6 copy-start.5
  245.4 3.1 %copy-start.3 = (f32[16,128]{1,0:T(8,128)S(1)}, f32[16,128]{1,0:T(8,128)}, u32[]{:S(2)}) copy-start(f32[16,128]{1,0:T(8,128)} %param.11) | copy-start | bytes 24580
  245.5 3.1 %copy-start.6 = (f32[256]{0:T(256)S(1)}, f32[256]{0:T(256)}, u32[]{:S(2)}) copy-start(f32[256]{0:T(256)} %get-tuple-element.23) | copy-start | bytes 3076
  269.5 2.2 copy-start.1

commit v14 on v10

--- a/solution.py
+++ b/solution.py
@@ -124,6 +124,7 @@
     backward_pairs = [(i + 1, i) for i in range(space_count - 1)]
     got_left = lax.ppermute(send_right, "space", forward_pairs)
     got_right = lax.ppermute(send_left, "space", backward_pairs)
+    far_rows, got_left, got_right = lax.optimization_barrier((far_rows, got_left, got_right))
     every_row = gather_rows(far_rows, "space", near_bits)
     every_row = in_row_order(every_row, far_bits + near_bits, space_count * row_count)
     every_row = sum_over(every_row, "ky", y_bits)

time: 266 us -> 328 us (1.23)
  the two profiles are of different devices: /device:TPU:47 before, /device:TPU:117 now
where the time goes in v14:
time: 328 us; the launch traced here: 327 us
  starting transfers between devices  152 us (46%)
  waiting for transfers between devices  128 us (39%)
  matrix products  23.9 us (7%)
  other arithmetic  11.7 us (4%)
  local copies, waits for them, and re-layouts  11.3 us (3%)
    all_to_all x1, waiting for transfers between devices, shards(): lax.all_to_all(mixed, 'ky', split_axis=1, concat_axis=2, tiled=True)  97.2 us
    ppermute x6, starting transfers between devices, gather_rows(): other = lax.ppermute(value, axis, xor_pairs(count, bit))  95.9 us
    ppermute x3, starting transfers between devices, sum_over(): value = value + lax.ppermute(value, axis, xor_pairs(count, bit))  17.3 us
    all_to_all x1, starting transfers between devices, shards(): lax.all_to_all(mixed, 'ky', split_axis=1, concat_axis=2, tiled=True)  14.7 us
    all_to_all x1, starting transfers between devices, shards(): spread = lax.all_to_all(held, 'ky', split_axis=2, concat_axis=1, tiled=True)  13.4 us
    ppermute x6, waiting for transfers between devices, gather_rows(): other = lax.ppermute(value, axis, xor_pairs(count, bit))  8.6 us
    ppermute x1, starting transfers between devices, shards(): got_left = lax.ppermute(send_right, 'space', forward_pairs)  8.53 us
    ppermute x3, waiting for transfers between devices, sum_over(): value = value + lax.ppermute(value, axis, xor_pairs(count, bit))  7.96 us
  transfers between devices with their start and end apart: 13, of which 12 were waited for; matrix products, arithmetic and copies ran while one was open for 8% of the time, Pallas kernels for 0%

profile of v14, /device:TPU:117, one launch (start us, length us, event | category | flops | bytes accessed | tf_op | source)
XLA Modules:
  0.0 327.3 jit_solution(3789530613518205671)
XLA Ops:
  0.0 1.9 reduce_sum.27
  2.0 0.6 fusion.84
  2.6 12.7 %collective-permute-start = (f32[1,2,256]{2,1,0:T(2,128)S(1)}, f32[1,2,256]{2,1,0:T(2,128)S(1)}, u32[]{:S(2)}, u32[]{:S(2)}) collective-permute-start(f32[1,2,256]{2,1,0:T(2,128)S(1)} %pad_maximum_fusion), channel_id=1, source_target_pairs={{0,4},{1,5},{2,6},{3,7},{4,0},{5,1},{6,2},{7,3},{8,12},{9,13},{10,... | collective-permute-start | bytes 6152 | tf_op jit(solution)/shard_map/ppermute | solution.py:67
  15.4 1.0 collective-permute-done
  16.4 2.6 collective-permute-start.1
  19.0 1.7 collective-permute-done.1
  20.7 3.1 collective-permute-start.2
  23.8 2.2 collective-permute-done.2
  25.9 8.1 %collective-permute-start.3 = (f32[4,2,256]{2,1,0:T(2,128)S(1)}, f32[4,2,256]{2,1,0:T(2,128)S(1)}, u32[]{:S(2)}, u32[]{:S(2)}) collective-permute-start(f32[4,2,256]{2,1,0:T(2,128)S(1)} %maximum_select_fusion.4), channel_id=1, source_target_pairs={{0,256},{8,264},{16,272},{24,280},{32,288},{40,296},{48,304},{56,3... | collective-permute-start | bytes 24584 | tf_op jit(solution)/shard_map/ppermute | solution.py:75
  34.1 1.0 collective-permute-done.3
  35.1 2.5 copy.28
  37.7 13.4 %all-to-all-start = ((f32[1,16,256,128]{3,1,0,2:T(8,128)}), f32[1,16,256,128]{3,1,0,2:T(8,128)}, u32[]{:S(2)}, u32[]{:S(2)}) async-start(f32[1,16,256,128]{3,1,0,2:T(8,128)} %copy.28), calls=%async_computation | async-start | bytes 4194304 | tf_op jit(solution)/shard_map/all_to_all | solution.py:144
  51.9 2.4 fusion.51
  54.2 8.5 %collective-permute-start.4 = (f32[4096,64]{0,1:T(8,128)}, f32[4096,64]{0,1:T(8,128)S(1)}, u32[]{:S(2)}, u32[]{:S(2)}) collective-permute-start(f32[4096,64]{0,1:T(8,128)} %fusion.51), channel_id=1, source_target_pairs={{0,8},{8,16},{16,24},{24,32},{32,40},{40,48},{48,56},{56,64},{64,7... | collective-permute-start | bytes 3145736 | tf_op jit(solution)/shard_map/ppermute | solution.py:125
  62.8 2.4 fusion.55
  65.2 1.9 collective-permute-start.5
  67.4 7.4 %collective-permute-done.4 = f32[4096,64]{0,1:T(8,128)S(1)} collective-permute-done((f32[4096,64]{0,1:T(8,128)}, f32[4096,64]{0,1:T(8,128)S(1)}, u32[]{:S(2)}, u32[]{:S(2)}) %collective-permute-start.4) | collective-permute-done | bytes 1048608 | tf_op jit(solution)/shard_map/ppermute | solution.py:125
  74.8 7.1 %collective-permute-done.5 = f32[4096,64]{0,1:T(8,128)} collective-permute-done((f32[4096,64]{0,1:T(8,128)}, f32[4096,64]{0,1:T(8,128)}, u32[]{:S(2)}, u32[]{:S(2)}) %collective-permute-start.5) | collective-permute-done | bytes 1048608 | tf_op jit(solution)/shard_map/ppermute | solution.py:126
  81.9 1.9 collective-permute-start.6
  83.8 1.1 collective-permute-done.6
  85.0 75.6 %collective-permute-start.7 = (f32[16,2,256]{2,1,0:T(2,128)S(1)}, f32[16,2,256]{2,1,0:T(2,128)S(1)}, u32[]{:S(2)}, u32[]{:S(2)}) collective-permute-start(f32[16,2,256]{2,1,0:T(2,128)S(1)} %maximum_select_fusion.2), channel_id=1, source_target_pairs={{0,16},{8,24},{16,0},{24,8},{32,48},{40,56},{48,32},{56,40},{64,80... | collective-permute-start | bytes 98312 | tf_op jit(solution)/shard_map/ppermute | solution.py:75
  160.6 0.7 broadcast_add_fusion
  161.3 0.9 collective-permute-done.7
  162.2 4.6 %collective-permute-start.8 = (f32[32,2,256]{2,1,0:T(2,128)S(1)}, f32[32,2,256]{2,1,0:T(2,128)S(1)}, u32[]{:S(2)}, u32[]{:S(2)}) collective-permute-start(f32[32,2,256]{2,1,0:T(2,128)S(1)} %maximum_select_fusion.1), channel_id=1, source_target_pairs={{0,32},{8,40},{16,48},{24,56},{32,0},{40,8},{48,16},{56,24},{64,96... | collective-permute-start | bytes 196616 | tf_op jit(solution)/shard_map/ppermute | solution.py:75
  167.0 1.7 collective-permute-done.8
  168.8 2.4 collective-permute-start.9
  171.5 0.6 iota_add_fusion
  172.0 2.5 collective-permute-done.9
  174.6 2.1 collective-permute-start.10
  176.8 0.6 multiply_multiply_fusion.1
  177.4 4.5 %collective-permute-done.10 = f32[64,2,256]{2,1,0:T(2,128)} collective-permute-done((f32[64,2,256]{2,1,0:T(2,128)S(1)}, f32[64,2,256]{2,1,0:T(2,128)}, u32[]{:S(2)}, u32[]{:S(2)}) %collective-permute-start.10) | collective-permute-done | bytes 131104 | tf_op jit(solution)/shard_map/ppermute | solution.py:67
  181.9 1.0 add.203
  183.0 0.4 fusion.42
  183.4 2.1 convolution_divide_fusion
  185.5 2.1 fusion.17
  187.7 4.5 %fusion.4 = f32[1,64,32]{2,0,1:T(1,128)S(1)} fusion(f32[256,1,1]{0,1,2:T(1,128)S(1)} %bitcast.83, s32[64,32]{1,0:T(8,128)S(1)} %copy-done.2, s32[64,32]{1,0:T(8,128)S(1)} %get-tuple-element.31), kind=kOutput, calls=%fused_computation.8 | convolution fusion | flops 8912896 | bytes 25600 | tf_op jit(solution)/shard_map/dot_general | solution.py:47
  192.4 2.2 copy.29
  194.8 2.6 fusion.1
  197.4 2.4 fusion.38
  199.8 3.1 copy.33
  202.9 14.7 %all-to-all-start.1 = ((f32[1,128,32,128]{3,2,0,1:T(8,128)}), f32[1,128,32,128]{3,2,0,1:T(8,128)}, u32[]{:S(2)}, u32[]{:S(2)}) async-start(f32[1,128,32,128]{3,2,0,1:T(8,128)} %copy.33), calls=%async_computation.1 | async-start | bytes 4194304 | tf_op jit(solution)/shard_map/all_to_all | solution.py:160
  217.6 0.4 fusion.106
  218.2 1.9 fusion.49
  220.1 3.1 convolution_add_fusion
  223.3 3.0 multiply_add_fusion.1
  226.2 97.2 %all-to-all-done.1 = f32[1,128,32,128]{3,2,0,1:T(8,128)} async-done(((f32[1,128,32,128]{3,2,0,1:T(8,128)}), f32[1,128,32,128]{3,2,0,1:T(8,128)}, u32[]{:S(2)}, u32[]{:S(2)}) %all-to-all-start.1) | async-done | bytes 2097184 | tf_op jit(solution)/shard_map/all_to_all | solution.py:160
  323.4 2.0 copy.34
  325.6 1.6 multiply_add_fusion
  (62 shorter events, 2.9 us)
Async XLA Ops:
  0.0 35.1 %copy-start = (f32[1,16,256,128]{3,2,1,0:T(8,128)S(1)}, f32[1,16,256,128]{3,2,1,0:T(8,128)}, u32[]{:S(2)}) copy-start(f32[1,16,256,128]{3,2,1,0:T(8,128)} %param.7) | copy-start | bytes 6291460
  0.0 2.0 copy-start.9
  0.0 2.0 copy-start.10
  0.0 2.0 copy-start.7
  2.6 13.7 %collective-permute-start = (f32[1,2,256]{2,1,0:T(2,128)S(1)}, f32[1,2,256]{2,1,0:T(2,128)S(1)}, u32[]{:S(2)}, u32[]{:S(2)}) collective-permute-start(f32[1,2,256]{2,1,0:T(2,128)S(1)} %pad_maximum_fusion), channel_id=1, source_target_pairs={{0,4},{1,5},{2,6},{3,7},{4,0},{5,1},{6,2},{7,3},{8,12},{9,13},{10,... | collective-permute-start | bytes 6152 | tf_op jit(solution)/shard_map/ppermute | solution.py:67
  16.4 4.3 %collective-permute-start.1 = (f32[1,2,256]{2,1,0:T(2,128)S(1)}, f32[1,2,256]{2,1,0:T(2,128)S(1)}, u32[]{:S(2)}, u32[]{:S(2)}) collective-permute-start(f32[1,2,256]{2,1,0:T(2,128)S(1)} %fusion.104), channel_id=1, source_target_pairs={{0,64},{8,72},{16,80},{24,88},{32,96},{40,104},{48,112},{56,120},{... | collective-permute-start | bytes 6152 | tf_op jit(solution)/shard_map/ppermute | solution.py:75
  20.7 5.2 %collective-permute-start.2 = (f32[2,2,256]{2,1,0:T(2,128)S(1)}, f32[2,2,256]{2,1,0:T(2,128)S(1)}, u32[]{:S(2)}, u32[]{:S(2)}) collective-permute-start(f32[2,2,256]{2,1,0:T(2,128)S(1)} %maximum_select_fusion.5), channel_id=1, source_target_pairs={{0,128},{8,136},{16,144},{24,152},{32,160},{40,168},{48,176},{56,1... | collective-permute-start | bytes 12296 | tf_op jit(solution)/shard_map/ppermute | solution.py:75
  25.9 9.2 %collective-permute-start.3 = (f32[4,2,256]{2,1,0:T(2,128)S(1)}, f32[4,2,256]{2,1,0:T(2,128)S(1)}, u32[]{:S(2)}, u32[]{:S(2)}) collective-permute-start(f32[4,2,256]{2,1,0:T(2,128)S(1)} %maximum_select_fusion.4), channel_id=1, source_target_pairs={{0,256},{8,264},{16,272},{24,280},{32,288},{40,296},{48,304},{56,3... | collective-permute-start | bytes 24584 | tf_op jit(solution)/shard_map/ppermute | solution.py:75
  37.7 13.4 %copy-start.8 = (s32[128]{0:T(128)S(1)}, s32[128]{0:T(128)}, u32[]{:S(2)}) copy-start(s32[128]{0:T(128)} %param.13) | copy-start | bytes 1540
  37.7 154.8 %all-to-all-start = ((f32[1,16,256,128]{3,1,0,2:T(8,128)}), f32[1,16,256,128]{3,1,0,2:T(8,128)}, u32[]{:S(2)}, u32[]{:S(2)}) async-start(f32[1,16,256,128]{3,1,0,2:T(8,128)} %copy.28), calls=%async_computation | async-start | bytes 4194304 | tf_op jit(solution)/shard_map/all_to_all | solution.py:144
  51.1 14.1 %copy-start.4 = (pred[128]{0:T(512)(128)(4,1)}, pred[128]{0:T(512)(128)(4,1)S(1)}, u32[]{:S(2)}) copy-start(pred[128]{0:T(512)(128)(4,1)S(1)} %get-tuple-element.40) | copy-start | bytes 388
  54.2 20.6 %collective-permute-start.4 = (f32[4096,64]{0,1:T(8,128)}, f32[4096,64]{0,1:T(8,128)S(1)}, u32[]{:S(2)}, u32[]{:S(2)}) collective-permute-start(f32[4096,64]{0,1:T(8,128)} %fusion.51), channel_id=1, source_target_pairs={{0,8},{8,16},{16,24},{24,32},{32,40},{40,48},{48,56},{56,64},{64,7... | collective-permute-start | bytes 3145736 | tf_op jit(solution)/shard_map/ppermute | solution.py:125
  65.2 16.7 %collective-permute-start.5 = (f32[4096,64]{0,1:T(8,128)}, f32[4096,64]{0,1:T(8,128)}, u32[]{:S(2)}, u32[]{:S(2)}) collective-permute-start(f32[4096,64]{0,1:T(8,128)} %fusion.55), channel_id=1, source_target_pairs={{8,0},{16,8},{24,16},{32,24},{40,32},{48,40},{56,48},{64,56},{72,6... | collective-permute-start | bytes 3145736 | tf_op jit(solution)/shard_map/ppermute | solution.py:126
  81.9 3.1 collective-permute-start.6
  85.0 77.2 %collective-permute-start.7 = (f32[16,2,256]{2,1,0:T(2,128)S(1)}, f32[16,2,256]{2,1,0:T(2,128)S(1)}, u32[]{:S(2)}, u32[]{:S(2)}) collective-permute-start(f32[16,2,256]{2,1,0:T(2,128)S(1)} %maximum_select_fusion.2), channel_id=1, source_target_pairs={{0,16},{8,24},{16,0},{24,8},{32,48},{40,56},{48,32},{56,40},{64,80... | collective-permute-start | bytes 98312 | tf_op jit(solution)/shard_map/ppermute | solution.py:75
  162.2 6.5 %collective-permute-start.8 = (f32[32,2,256]{2,1,0:T(2,128)S(1)}, f32[32,2,256]{2,1,0:T(2,128)S(1)}, u32[]{:S(2)}, u32[]{:S(2)}) collective-permute-start(f32[32,2,256]{2,1,0:T(2,128)S(1)} %maximum_select_fusion.1), channel_id=1, source_target_pairs={{0,32},{8,40},{16,48},{24,56},{32,0},{40,8},{48,16},{56,24},{64,96... | collective-permute-start | bytes 196616 | tf_op jit(solution)/shard_map/ppermute | solution.py:75
  168.8 5.7 %collective-permute-start.9 = (f32[64,2,256]{2,1,0:T(2,128)S(1)}, f32[64,2,256]{2,1,0:T(2,128)S(1)}, u32[]{:S(2)}, u32[]{:S(2)}) collective-permute-start(f32[64,2,256]{2,1,0:T(2,128)S(1)} %bitcast.75), channel_id=1, source_target_pairs={{0,1},{1,0},{2,3},{3,2},{4,5},{5,4},{6,7},{7,6},{8,9},{9,8},{10,11... | collective-permute-start | bytes 393224 | tf_op jit(solution)/shard_map/ppermute | solution.py:67
  174.6 7.3 %collective-permute-start.10 = (f32[64,2,256]{2,1,0:T(2,128)S(1)}, f32[64,2,256]{2,1,0:T(2,128)}, u32[]{:S(2)}, u32[]{:S(2)}) collective-permute-start(f32[64,2,256]{2,1,0:T(2,128)S(1)} %bitcast_add_fusion), channel_id=1, source_target_pairs={{0,2},{1,3},{2,0},{3,1},{4,6},{5,7},{6,4},{7,5},{8,10},{9,11},{10,... | collective-permute-start | bytes 393224 | tf_op jit(solution)/shard_map/ppermute | solution.py:67
  177.4 10.3 %copy-start.2 = (s32[64,32]{1,0:T(8,128)S(1)}, s32[64,32]{1,0:T(8,128)}, u32[]{:S(2)}) copy-start(s32[64,32]{1,0:T(8,128)} %get-tuple-element.32) | copy-start | bytes 24580
  202.9 14.7 %copy-start.11 = (f32[128]{0:T(128)S(1)}, f32[128]{0:T(128)}, u32[]{:S(2)}) copy-start(f32[128]{0:T(128)} %param.12) | copy-start | bytes 1540
  202.9 120.5 %all-to-all-start.1 = ((f32[1,128,32,128]{3,2,0,1:T(8,128)}), f32[1,128,32,128]{3,2,0,1:T(8,128)}, u32[]{:S(2)}, u32[]{:S(2)}) async-start(f32[1,128,32,128]{3,2,0,1:T(8,128)} %copy.33), calls=%async_computation.1 | async-start | bytes 4194304 | tf_op jit(solution)/shard_map/all_to_all | solution.py:160
  217.6 0.6 copy-start.5
  220.1 3.1 copy-start.3
  220.1 3.1 copy-start.6
  323.4 2.2 copy-start.1
